TPU v7x, 512 devices: a whole 4x8x8 slice. The times are simulated.
512 devices in a mesh: rep: 8 (over y_lo, core), seq: 2 (over y_hi), tp: 32 (over x, z).
Axes of the slice: x: 4, y: 8 (y_hi: 2, y_lo: 4; y = y_hi * 4 + y_lo), z: 8, core: 2. Of those that a mesh axis runs over, the one named last changes fastest.
Arguments:
- hidden: bfloat16 [3072, 8192], P('rep', ('seq', 'tp')), may hold values from -100 to 100
- gain: float32 [8192], replicated, may hold values from 0.1 to 1.9
- w_query: bfloat16 [8192, 8192], P('seq', 'tp'), may hold values from -1 to 1
- w_keyval: bfloat16 [2, 4096, 2048], P(None, 'tp'), may hold values from -1 to 1
- lengths: int32 [8, 2], replicated, may hold values from 128 to 192, as said below
- routes: int32 [8, 2], replicated, may hold values from 0 to 7, as said below
Outputs:
- attended: bfloat16 [3072, 8192], P(('rep', 'seq'), 'tp')
Inputs may be any that keep to these rules, and one draw needn't show every extreme that they name: `routes`: for each j, the responses j of the 8 rollout groups go to 8 different replicas, so each replica receives exactly 2 responses. `lengths`: the responses that one rollout group sends to one replica hold at most 192 tokens together, and in every draw some group sends exactly 192 tokens to one replica.
All inputs are finite; a program needn't handle non-finite values.
Results may differ from a plain program's by a relative error of at most 0.0076.
Values may be sent and summed in bfloat16 or wider, within the bound.
No kernel may reach another device: no remote copies, remote signals or barrier semaphores. Data moves between devices by JAX's collectives and lax.ppermute only.
A program may use at most 64 MiB of HBM per device.

v0:
```python
import math

import jax
import jax.numpy as jnp
from jax import lax
from jax.sharding import PartitionSpec as P

D = 8192
QH = 64
KVH = 8
HD = 128
RESP = 2
LMAX = 192
BUFFER = 384


ROPE_BASE = 500000.0
NORM_EPS = 1e-05
MASK_FILL = -1e30


def response_tables(lengths, routes):
    flat_len = lengths.reshape(-1)
    flat_route = routes.reshape(-1)
    response_ids = jnp.arange(flat_len.shape[0], dtype=jnp.int32)
    group_of = response_ids // RESP
    same_route = flat_route[:, None] == flat_route[None, :]
    same_group = group_of[:, None] == group_of[None, :]
    earlier = response_ids[None, :] < response_ids[:, None]
    dest_off = jnp.sum(jnp.where(same_route & earlier, flat_len[None, :], 0), axis=1)
    pair_off = jnp.sum(jnp.where(same_route & same_group & earlier, flat_len[None, :], 0), axis=1)
    src_start = jnp.sum(jnp.where(same_group & earlier, flat_len[None, :], 0), axis=1)
    return (flat_len, flat_route, group_of, dest_off, pair_off, src_start)


def locate(positions, replica, tables):
    flat_len, flat_route, group_of, dest_off, pair_off, src_start = tables
    response_ids = jnp.arange(flat_len.shape[0], dtype=jnp.int32)
    position_col = positions[:, None]
    inside = (
        (flat_route[None, :] == replica)
        & (dest_off[None, :] <= position_col)
        & (position_col < dest_off[None, :] + flat_len[None, :])
    )
    inside_int = inside.astype(jnp.int32)
    segment = jnp.sum(inside_int * (response_ids[None, :] + 1), axis=1) - 1
    seg_start = jnp.sum(inside_int * dest_off[None, :], axis=1)
    source_group = jnp.sum(inside_int * group_of[None, :], axis=1)
    pair_first = jnp.sum(inside_int * (dest_off - pair_off)[None, :], axis=1)
    source = jnp.sum(inside_int * src_start[None, :], axis=1)
    within = jnp.where(segment >= 0, positions - seg_start, 0)
    return (segment, within, source_group, pair_first, source)


def rotary(values_in, within):
    head_dim = values_in.shape[-1]
    half_dim = head_dim // 2
    freq_index = jnp.arange(half_dim, dtype=jnp.float32)
    inverse = jnp.power(ROPE_BASE, -2.0 * freq_index / head_dim)
    angles = within.astype(jnp.float32)[:, None] * inverse[None, :]
    cosine = jnp.cos(angles)[:, None, :]
    sine_part = jnp.sin(angles)[:, None, :]
    lower_half = values_in[..., :half_dim]
    upper_half = values_in[..., half_dim:]
    return jnp.concatenate(
        [
            lower_half * cosine - upper_half * sine_part,
            upper_half * cosine + lower_half * sine_part,
        ],
        axis=-1,
    )


def fill_rows(table, indices, present):
    taken = jnp.take(table, indices.reshape(-1), axis=0)
    return jnp.where(present.reshape(-1)[:, None], taken, jnp.zeros((), table.dtype))


def local(hidden, gain, w_query, w_keyval, lengths, routes):
    rep_count = lax.axis_size("rep")
    seq_count = lax.axis_size("seq")
    replica = lax.axis_index("rep")
    seq_index = lax.axis_index("seq")
    column = lax.axis_index("tp")
    feature_cols = hidden.shape[1]
    local_rows = BUFFER // seq_count
    capacity = (RESP + rep_count - 1) // rep_count * LMAX
    head_count = w_query.shape[1] // HD
    tables = response_tables(lengths, routes)
    flat_len, flat_route, group_of, dest_off, pair_off, src_start = tables
    my_len = lax.dynamic_slice_in_dim(flat_len, replica * RESP, RESP)
    my_route = lax.dynamic_slice_in_dim(flat_route, replica * RESP, RESP)
    my_pair = lax.dynamic_slice_in_dim(pair_off, replica * RESP, RESP)
    my_start = lax.dynamic_slice_in_dim(src_start, replica * RESP, RESP)
    slot_ids = jnp.arange(capacity, dtype=jnp.int32)
    targets = jnp.arange(rep_count, dtype=jnp.int32)
    block_off = jnp.broadcast_to(slot_ids[None, :], (rep_count, capacity))
    offsets = block_off[:, :, None]
    inside = (
        (my_route[None, None, :] == targets[:, None, None])
        & (my_pair[None, None, :] <= offsets)
        & (offsets < (my_pair + my_len)[None, None, :])
    )
    inside_int = inside.astype(jnp.int32)
    src_rows = jnp.sum(
        inside_int * (my_start[None, None, :] + offsets - my_pair[None, None, :]), axis=2
    )
    src_rows, present = (src_rows, jnp.any(inside, axis=2))
    outgoing = fill_rows(hidden, src_rows, present)
    incoming = lax.all_to_all(outgoing, "rep", split_axis=0, concat_axis=0, tiled=True)
    all_pos = jnp.arange(BUFFER, dtype=jnp.int32)
    segment, within, source_group, pair_first, source = locate(all_pos, replica, tables)
    gathered_idx = jnp.where(segment >= 0, source_group * capacity + all_pos - pair_first, 0)
    assembled = fill_rows(incoming, gathered_idx, segment >= 0)
    local_x = lax.all_to_all(
        assembled.reshape(BUFFER, 1, feature_cols), "seq", split_axis=0, concat_axis=1, tiled=True
    )
    query_pos = seq_index * local_rows + jnp.arange(local_rows, dtype=jnp.int32)
    query_info = locate(query_pos, replica, tables)
    query_seg = query_info[0]
    query_within = query_info[1]
    query_valid = query_seg >= 0
    gain_halves = gain.reshape(seq_count, D // seq_count)
    gain_local = lax.dynamic_slice_in_dim(gain_halves, column * feature_cols, feature_cols, 1)
    kv_head = column * head_count // (QH // KVH)
    query_weights = lax.all_gather(
        w_query.reshape(1, w_query.shape[0], w_query.shape[1]), "seq", axis=0, tiled=True
    )
    feature_piece = lax.all_gather(local_x, "tp", axis=2, tiled=True)
    scaled_piece = (feature_piece.astype(jnp.float32) * gain_halves[None]).astype(jnp.bfloat16)
    query_acc = jnp.einsum(
        "rsn,snf->rf", scaled_piece, query_weights, preferred_element_type=jnp.float32
    )
    squares = jnp.sum(jnp.square(feature_piece.astype(jnp.float32)), axis=(1, 2))
    inverse_rms = lax.rsqrt(squares / D + NORM_EPS)
    queries = rotary(
        inverse_rms[:, None, None] * query_acc.reshape(local_rows, head_count, HD), query_within
    ).astype(jnp.bfloat16)
    scaled_local = (local_x.astype(jnp.float32) * gain_local[None]).astype(jnp.bfloat16)
    kv_partial = jnp.einsum(
        "rsw,swc->rc", scaled_local, w_keyval, preferred_element_type=jnp.float32
    )
    kv_total = lax.psum(kv_partial, "tp")
    head_block = lax.dynamic_slice_in_dim(kv_total, kv_head * 2 * HD, 2 * HD, 1)
    keys = rotary(inverse_rms[:, None, None] * head_block[:, None, :HD], query_within)[:, 0].astype(
        jnp.bfloat16
    )
    values = (inverse_rms[:, None] * head_block[:, HD:]).astype(jnp.bfloat16)
    score_scale = 1.0 / math.sqrt(HD)
    running = jnp.full((local_rows, head_count), MASK_FILL, jnp.float32)
    key_part = lax.all_gather(keys, "seq", axis=0, tiled=True)
    value_part = lax.all_gather(values, "seq", axis=0, tiled=True)
    key_count = key_part.shape[0]
    key_pos = jnp.arange(key_count, dtype=jnp.int32)
    key_seg = locate(key_pos, replica, tables)[0]
    allowed = (key_seg[None, :] == query_seg[:, None]) & query_valid[:, None] & (
        key_pos[None, :] <= query_pos[:, None]
    ) | (key_pos[None, :] == query_pos[:, None])
    scores = (
        jnp.einsum("rhd,kd->rhk", queries, key_part, preferred_element_type=jnp.float32)
        * score_scale
    )
    scores = jnp.where(allowed[:, None, :], scores, MASK_FILL)
    new_max = jnp.maximum(running, jnp.max(scores, axis=2))
    prob_terms = jnp.where(allowed[:, None, :], jnp.exp(scores - new_max[:, :, None]), 0.0)
    totals = jnp.sum(prob_terms, axis=2)
    accum = jnp.einsum(
        "rhk,kd->rhd",
        prob_terms.astype(jnp.bfloat16),
        value_part,
        preferred_element_type=jnp.float32,
    )
    attended = (
        (accum / totals[:, :, None]).reshape(local_rows, head_count * HD).astype(jnp.bfloat16)
    )
    return jnp.where(query_valid[:, None], attended, jnp.zeros((), jnp.bfloat16))


def solution(mesh):
    in_specs = (P("rep", ("seq", "tp")), P(), P("seq", "tp"), P(None, "tp", None), P(), P())
    out_specs = P(("rep", "seq"), "tp")
    return jax.shard_map(local, mesh=mesh, in_specs=in_specs, out_specs=out_specs, check_vma=False)
```

profile of v0, /device:TPU:56, one launch (start us, length us, event | category | flops | bytes accessed | tf_op | source)
XLA Modules:
  0.0 440.0 jit_solution(4229495986316716021)
XLA Ops:
  6.5 0.8 copy.25
  7.5 0.8 copy.24
  9.1 3.5 gather_fusion
  12.7 1.3 select_select_fusion
  14.0 6.3 %all-to-all-start = ((bf16[8,192,128]{2,1,0:T(8,128)(2,1)}), bf16[8,192,128]{2,1,0:T(8,128)(2,1)S(1)}, u32[]{:S(2)}, u32[]{:S(2)}) async-start(bf16[8,192,128]{2,1,0:T(8,128)(2,1)} %select_select_fusion), calls=%async_computation | async-start | bytes 786432 | tf_op jit(solution)/shard_map/all_to_all | solution.py:110
  20.5 9.8 %all-to-all-done = bf16[8,192,128]{2,1,0:T(8,128)(2,1)S(1)} async-done(((bf16[8,192,128]{2,1,0:T(8,128)(2,1)}), bf16[8,192,128]{2,1,0:T(8,128)(2,1)S(1)}, u32[]{:S(2)}, u32[]{:S(2)}) %all-to-all-start) | async-done | bytes 393248 | tf_op jit(solution)/shard_map/all_to_all | solution.py:110
  30.3 1.4 gather_fusion.1
  31.9 0.5 broadcast.494
  32.4 0.7 reduce.4
  33.1 10.1 %all_to_all.27 = bf16[2,2,12288]{2,1,0:T(2,128)(2,1)S(1)} all-to-all(bf16[2,2,12288]{2,1,0:T(2,128)(2,1)S(1)} %reshape.481), channel_id=1, replica_groups=mesh['rep'=8,'seq'=2,'tp'=32] {'seq'}, dimensions={0} | all-to-all | bytes 196608 | tf_op jit(solution)/shard_map/all_to_all | solution.py:115
  43.3 0.7 copy.29
  44.1 0.7 all-gather.8.cloned.1.call-update
  45.2 2.5 convolution_bitcast_fusion
  47.7 0.4 multiply_cosine_fusion.1
  48.2 84.7 %all-gather.6.cloned.1.call-done = bf16[192,2,1,4096]{3,0,1,2:T(8,128)(2,1)} async-done(((bf16[192,2,1,128]{3,0,1,2:T(8,128)(2,1)}), bf16[192,2,1,4096]{3,0,1,2:T(8,128)(2,1)}) %all-gather.6.cloned.1.call-update) | async-done | bytes 3145744 | tf_op jit(solution)/shard_map/all_gather | solution.py:129
  132.9 2.6 fusion
  135.5 101.0 %all-gather.8.cloned.1.call-done = bf16[8192,256]{1,0:T(8,128)(2,1)} async-done(((bf16[4096,256]{1,0:T(8,128)(2,1)}), bf16[8192,256]{1,0:T(8,128)(2,1)}) %all-gather.8.cloned.1.call-update) | async-done | bytes 4194320 | tf_op jit(solution)/shard_map/all_gather | solution.py:126
  236.5 4.1 fusion.7
  240.7 171.8 %all-reduce.2.cloned.1.call-done = f32[192,2048]{1,0:T(8,128)} async-done(((f32[192,2048]{1,0:T(8,128)}), f32[192,2048]{1,0:T(8,128)}) %all-reduce.2.cloned.1.call-update) | async-done | bytes 1572880 | tf_op jit(solution)/shard_map/psum | solution.py:143
  412.5 1.0 fusion.30
  413.5 0.5 fusion.26
  414.0 8.8 %all-gather.2 = bf16[384,1,128]{2,0,1:T(8,128)(2,1)S(1)} all-gather(bf16[192,1,128]{2,0,1:T(8,128)(2,1)S(1)} %pad_maximum_fusion), channel_id=4, replica_groups=mesh['rep'=8,'seq'=2,'tp'=32] {'seq'}, dimensions={0}, use_global_device_ids=true | all-gather | bytes 147456 | tf_op jit(solution)/shard_map/all_gather | solution.py:151
  423.4 8.7 %all_gather.15 = bf16[384,128]{1,0:T(8,128)(2,1)S(1)} all-gather(bf16[192,128]{1,0:T(8,128)(2,1)S(1)} %get-tuple-element.19), channel_id=1, replica_groups=mesh['rep'=8,'seq'=2,'tp'=32] {'seq'}, dimensions={0}, use_global_device_ids=true | all-gather | bytes 147456 | tf_op jit(solution)/shard_map/all_gather | solution.py:152
  432.7 0.7 bitcast_select_fusion
  (49 shorter events, 3.2 us)
Async XLA Ops:
  6.5 38.7 %copy-start = (bf16[2,128,2048]{2,1,0:T(8,128)(2,1)S(1)}, bf16[2,128,2048]{2,1,0:T(8,128)(2,1)}, u32[]{:S(2)}) copy-start(bf16[2,128,2048]{2,1,0:T(8,128)(2,1)} %param.9) | copy-start | bytes 3145732
  12.7 32.1 %copy-start.1 = (f32[8192]{0:T(1024)S(1)}, f32[8192]{0:T(1024)}, u32[]{:S(2)}) copy-start(f32[8192]{0:T(1024)} %param.7) | copy-start | bytes 98308
  14.0 16.3 %all-to-all-start = ((bf16[8,192,128]{2,1,0:T(8,128)(2,1)}), bf16[8,192,128]{2,1,0:T(8,128)(2,1)S(1)}, u32[]{:S(2)}, u32[]{:S(2)}) async-start(bf16[8,192,128]{2,1,0:T(8,128)(2,1)} %select_select_fusion), calls=%async_computation | async-start | bytes 786432 | tf_op jit(solution)/shard_map/all_to_all | solution.py:110
  20.3 112.6 %all-gather.6.cloned.1.call-start = ((), (), s32[]{:S(2)}) async-start(), calls=%async_computation.3 | async-start | bytes 3244032 | tf_op jit(solution)/shard_map/all_gather | solution.py:129
  44.0 192.4 %all-gather.8.cloned.1.call-start = ((), (), s32[]{:S(2)}) async-start(), calls=%async_computation.4 | async-start | bytes 6291456 | tf_op jit(solution)/shard_map/all_gather | solution.py:126
  44.8 367.7 %all-reduce.2.cloned.1.call-start = ((), (), s32[]{:S(2)}) async-start(), calls=%async_computation.2 | async-start | bytes 3145728 | tf_op jit(solution)/shard_map/psum | solution.py:143
Sparse Core Ops, SparseCore 0:
  44.1 88.6 all-gather.5
  135.0 101.4 all-gather.7
  239.9 172.5 all-reduce.1
where the time goes:
time: 441 us; the launch traced here: 440 us
  waiting for transfers between devices  368 us (83%)
  blocking collectives  27.6 us (6%)
  between operations  13.4 us (3%)
  other arithmetic  9.02 us (2%)
  local copies, waits for them, and re-layouts  8.3 us (2%)
  matrix products  7.34 us (2%)
  starting transfers between devices  6.39 us (1%)
    psum x1, waiting for transfers between devices, local(): kv_total = lax.psum(kv_partial, 'tp')  172 us
    all_gather x1, waiting for transfers between devices, local(): lax.all_gather(w_query.reshape(1, w_query.shape[0], w_query.shape[1]), 's...  101 us
    all_gather x1, waiting for transfers between devices, local(): feature_piece = lax.all_gather(local_x, 'tp', axis=2, tiled=True)  84.7 us
    all_to_all x1, blocking collectives, local(): lax.all_to_all(assembled.reshape(BUFFER, 1, feature_cols), 'seq', split_a...  10.1 us
    all_to_all x1, waiting for transfers between devices, local(): lax.all_to_all(outgoing, 'rep', split_axis=0, concat_axis=0, tiled=True)  9.76 us
  transfers between devices with their start and end apart: 4, of which 4 were waited for; matrix products, arithmetic and copies ran while one was open for 2% of the time, Pallas kernels for 0%

commit v1 on v0

--- a/solution.py
+++ b/solution.py
@@ -79,13 +79,18 @@
 def local(hidden, gain, w_query, w_keyval, lengths, routes):
     rep_count = lax.axis_size("rep")
     seq_count = lax.axis_size("seq")
+    group_size = lax.axis_size("tu")
+    tp_count = lax.axis_size("tg") * group_size
     replica = lax.axis_index("rep")
     seq_index = lax.axis_index("seq")
-    column = lax.axis_index("tp")
+    sub = lax.axis_index("tu")
     feature_cols = hidden.shape[1]
     local_rows = BUFFER // seq_count
     capacity = (RESP + rep_count - 1) // rep_count * LMAX
     head_count = w_query.shape[1] // HD
+    kv_cols = 2 * HD // group_size
+    quarter = HD // 4
+
     tables = response_tables(lengths, routes)
     flat_len, flat_route, group_of, dest_off, pair_off, src_start = tables
     my_len = lax.dynamic_slice_in_dim(flat_len, replica * RESP, RESP)
@@ -94,8 +99,7 @@
     my_start = lax.dynamic_slice_in_dim(src_start, replica * RESP, RESP)
     slot_ids = jnp.arange(capacity, dtype=jnp.int32)
     targets = jnp.arange(rep_count, dtype=jnp.int32)
-    block_off = jnp.broadcast_to(slot_ids[None, :], (rep_count, capacity))
-    offsets = block_off[:, :, None]
+    offsets = jnp.broadcast_to(slot_ids[None, :], (rep_count, capacity))[:, :, None]
     inside = (
         (my_route[None, None, :] == targets[:, None, None])
         & (my_pair[None, None, :] <= offsets)
@@ -105,55 +109,71 @@
     src_rows = jnp.sum(
         inside_int * (my_start[None, None, :] + offsets - my_pair[None, None, :]), axis=2
     )
-    src_rows, present = (src_rows, jnp.any(inside, axis=2))
+    present = jnp.any(inside, axis=2)
     outgoing = fill_rows(hidden, src_rows, present)
     incoming = lax.all_to_all(outgoing, "rep", split_axis=0, concat_axis=0, tiled=True)
     all_pos = jnp.arange(BUFFER, dtype=jnp.int32)
     segment, within, source_group, pair_first, source = locate(all_pos, replica, tables)
-    gathered_idx = jnp.where(segment >= 0, source_group * capacity + all_pos - pair_first, 0)
-    assembled = fill_rows(incoming, gathered_idx, segment >= 0)
-    local_x = lax.all_to_all(
-        assembled.reshape(BUFFER, 1, feature_cols), "seq", split_axis=0, concat_axis=1, tiled=True
-    )
+    valid = segment >= 0
+    gathered_idx = jnp.where(valid, source_group * capacity + all_pos - pair_first, 0)
+    assembled = fill_rows(incoming, gathered_idx, valid)
+
+    w_half = lax.dynamic_index_in_dim(w_keyval, seq_index, 0, keepdims=False)
+    w_half = w_half.reshape(feature_cols, KVH, 2, 2, 2, quarter)
+    w_half = w_half.transpose(1, 2, 4, 0, 3, 5).reshape(tp_count, feature_cols, kv_cols)
+    w_kv = lax.all_to_all(w_half, ("tg", "tu"), split_axis=0, concat_axis=0, tiled=True)
+
+    gathered = lax.all_gather(assembled, ("tg", "tu"), axis=0, tiled=False)
+    gain_half = lax.dynamic_index_in_dim(
+        gain.reshape(seq_count, tp_count, feature_cols), seq_index, 0, keepdims=False
+    )
+    gathered_f = gathered.astype(jnp.float32)
+    scaled = (gathered_f * gain_half[:, None, :]).astype(jnp.bfloat16)
+    squares = jnp.sum(gathered_f * gathered_f, axis=(0, 2))
+    w_q = w_query.reshape(tp_count, feature_cols, w_query.shape[1])
+    query_part = jnp.einsum("tri,tic->rc", scaled, w_q, preferred_element_type=jnp.float32)
+    kv_part = jnp.einsum("tri,tic->rc", scaled, w_kv, preferred_element_type=jnp.float32)
+
+    query_halves = query_part.reshape(seq_count, local_rows, query_part.shape[1])
+    partner = seq_count - 1 - seq_index
+    to_partner = lax.dynamic_index_in_dim(query_halves, partner, 0, keepdims=False)
+    got_query, got_kv, got_squares = lax.ppermute(
+        (to_partner, kv_part, squares), "seq", perm=[(0, 1), (1, 0)]
+    )
+    query_raw = lax.dynamic_index_in_dim(query_halves, seq_index, 0, keepdims=False) + got_query
+    kv_raw = kv_part + got_kv
+    inverse_rms = lax.rsqrt((squares + got_squares) / D + NORM_EPS)
+
     query_pos = seq_index * local_rows + jnp.arange(local_rows, dtype=jnp.int32)
-    query_info = locate(query_pos, replica, tables)
-    query_seg = query_info[0]
-    query_within = query_info[1]
+    query_seg = lax.dynamic_slice_in_dim(segment, seq_index * local_rows, local_rows)
+    query_within = lax.dynamic_slice_in_dim(within, seq_index * local_rows, local_rows)
+    query_rms = lax.dynamic_slice_in_dim(inverse_rms, seq_index * local_rows, local_rows)
     query_valid = query_seg >= 0
-    gain_halves = gain.reshape(seq_count, D // seq_count)
-    gain_local = lax.dynamic_slice_in_dim(gain_halves, column * feature_cols, feature_cols, 1)
-    kv_head = column * head_count // (QH // KVH)
-    query_weights = lax.all_gather(
-        w_query.reshape(1, w_query.shape[0], w_query.shape[1]), "seq", axis=0, tiled=True
-    )
-    feature_piece = lax.all_gather(local_x, "tp", axis=2, tiled=True)
-    scaled_piece = (feature_piece.astype(jnp.float32) * gain_halves[None]).astype(jnp.bfloat16)
-    query_acc = jnp.einsum(
-        "rsn,snf->rf", scaled_piece, query_weights, preferred_element_type=jnp.float32
-    )
-    squares = jnp.sum(jnp.square(feature_piece.astype(jnp.float32)), axis=(1, 2))
-    inverse_rms = lax.rsqrt(squares / D + NORM_EPS)
     queries = rotary(
-        inverse_rms[:, None, None] * query_acc.reshape(local_rows, head_count, HD), query_within
+        query_rms[:, None, None] * query_raw.reshape(local_rows, head_count, HD), query_within
     ).astype(jnp.bfloat16)
-    scaled_local = (local_x.astype(jnp.float32) * gain_local[None]).astype(jnp.bfloat16)
-    kv_partial = jnp.einsum(
-        "rsw,swc->rc", scaled_local, w_keyval, preferred_element_type=jnp.float32
-    )
-    kv_total = lax.psum(kv_partial, "tp")
-    head_block = lax.dynamic_slice_in_dim(kv_total, kv_head * 2 * HD, 2 * HD, 1)
-    keys = rotary(inverse_rms[:, None, None] * head_block[:, None, :HD], query_within)[:, 0].astype(
-        jnp.bfloat16
-    )
-    values = (inverse_rms[:, None] * head_block[:, HD:]).astype(jnp.bfloat16)
+
+    kv_scaled = (inverse_rms[:, None] * kv_raw).reshape(BUFFER, 2, quarter)
+    freq_index = (sub % 2 * quarter + jnp.arange(quarter, dtype=jnp.int32)).astype(jnp.float32)
+    inverse = jnp.power(ROPE_BASE, -2.0 * freq_index / HD)
+    angles = within.astype(jnp.float32)[:, None] * inverse[None, :]
+    cosine = jnp.cos(angles)
+    sine_part = jnp.sin(angles)
+    lower_half = kv_scaled[:, 0]
+    upper_half = kv_scaled[:, 1]
+    roped = jnp.stack(
+        [lower_half * cosine - upper_half * sine_part, upper_half * cosine + lower_half * sine_part],
+        axis=1,
+    )
+    piece = jnp.where(sub < 2, roped, kv_scaled).astype(jnp.bfloat16)
+    pieces = lax.all_gather(piece, "tu", axis=0, tiled=False)
+    pieces = pieces.reshape(2, 2, BUFFER, 2, quarter).transpose(0, 2, 3, 1, 4)
+    key_part = pieces[0].reshape(BUFFER, HD)
+    value_part = pieces[1].reshape(BUFFER, HD)
+
     score_scale = 1.0 / math.sqrt(HD)
-    running = jnp.full((local_rows, head_count), MASK_FILL, jnp.float32)
-    key_part = lax.all_gather(keys, "seq", axis=0, tiled=True)
-    value_part = lax.all_gather(values, "seq", axis=0, tiled=True)
-    key_count = key_part.shape[0]
-    key_pos = jnp.arange(key_count, dtype=jnp.int32)
-    key_seg = locate(key_pos, replica, tables)[0]
-    allowed = (key_seg[None, :] == query_seg[:, None]) & query_valid[:, None] & (
+    key_pos = all_pos
+    allowed = (segment[None, :] == query_seg[:, None]) & query_valid[:, None] & (
         key_pos[None, :] <= query_pos[:, None]
     ) | (key_pos[None, :] == query_pos[:, None])
     scores = (
@@ -161,7 +181,7 @@
         * score_scale
     )
     scores = jnp.where(allowed[:, None, :], scores, MASK_FILL)
-    new_max = jnp.maximum(running, jnp.max(scores, axis=2))
+    new_max = jnp.max(scores, axis=2)
     prob_terms = jnp.where(allowed[:, None, :], jnp.exp(scores - new_max[:, :, None]), 0.0)
     totals = jnp.sum(prob_terms, axis=2)
     accum = jnp.einsum(
@@ -177,6 +197,21 @@
 
 
 def solution(mesh):
-    in_specs = (P("rep", ("seq", "tp")), P(), P("seq", "tp"), P(None, "tp", None), P(), P())
-    out_specs = P(("rep", "seq"), "tp")
-    return jax.shard_map(local, mesh=mesh, in_specs=in_specs, out_specs=out_specs, check_vma=False)
+    heads_per_kv = QH // KVH
+    tp_count = mesh.shape["tp"]
+    group_size = heads_per_kv * tp_count // QH
+    devices = mesh.devices.reshape(
+        mesh.shape["rep"], mesh.shape["seq"], tp_count // group_size, group_size
+    )
+    grid = jax.sharding.Mesh(devices, ("rep", "seq", "tg", "tu"))
+    tp = ("tg", "tu")
+    in_specs = (
+        P("rep", ("seq",) + tp),
+        P(),
+        P("seq", tp),
+        P(None, tp, None),
+        P(),
+        P(),
+    )
+    out_specs = P(("rep", "seq"), tp)
+    return jax.shard_map(local, mesh=grid, in_specs=in_specs, out_specs=out_specs, check_vma=False)

time: 441 us -> 176 us (0.40)
  waiting for transfers between devices: 368 us -> 90.6 us
  starting transfers between devices: 6.39 us -> 34.4 us
  blocking collectives: 27.6 us -> 13.6 us
    psum x1 -> x0, waiting for transfers between devices: 172 us -> none  [local(): kv_total = lax.psum(kv_partial, 'tp')]
    all_gather x2 -> x1, waiting for transfers between devices: 186 us -> 73.7 us  [local(): gathered = lax.all_gather(assembled, ('tg', 'tu'), axis=0, tiled=False)]
    ppermute x0 -> x3, starting transfers between devices: none -> 14.8 us  [local(): lax.ppermute((to_partner, kv_part, squares), 'seq', perm=[(0, 1), (1, 0)])]
    all_to_all x0 -> x1, starting transfers between devices: none -> 13.2 us  [local(): lax.all_to_all(w_half, ('tg', 'tu'), split_axis=0, concat_axis=0, tiled=T...]
    all_to_all x1 -> x0, blocking collectives: 10.1 us -> none  [local(): lax.all_to_all(assembled.reshape(BUFFER, 1, feature_cols), 'seq', split_a...]
    ppermute x0 -> x3, waiting for transfers between devices: none -> 7.12 us  [local(): lax.ppermute((to_partner, kv_part, squares), 'seq', perm=[(0, 1), (1, 0)])]
    all_gather x2 -> x1, blocking collectives: 17.5 us -> 13.6 us  [local(): pieces = lax.all_gather(piece, 'tu', axis=0, tiled=False)]
  transfers between devices with their start and end apart: 4 -> 6, of which waited for: 4 -> 3; matrix products, arithmetic and copies ran while one was open for 2% -> 6% of each run, Pallas kernels for 0% -> 0%
where the time goes in v1:
time: 176 us
  waiting for transfers between devices  90.6 us (51%)
  starting transfers between devices  34.4 us (20%)
  between operations  13.7 us (8%)
  blocking collectives  13.6 us (8%)
  local copies, waits for them, and re-layouts  9.4 us (5%)
  other arithmetic  9.2 us (5%)
  matrix products  4.75 us (3%)
    all_gather x1, waiting for transfers between devices, local(): gathered = lax.all_gather(assembled, ('tg', 'tu'), axis=0, tiled=False)  73.7 us
    ppermute x3, starting transfers between devices, local(): lax.ppermute((to_partner, kv_part, squares), 'seq', perm=[(0, 1), (1, 0)])  14.8 us
    all_gather x1, blocking collectives, local(): pieces = lax.all_gather(piece, 'tu', axis=0, tiled=False)  13.6 us
    all_to_all x1, starting transfers between devices, local(): lax.all_to_all(w_half, ('tg', 'tu'), split_axis=0, concat_axis=0, tiled=T...  13.2 us
    all_to_all x1, waiting for transfers between devices, local(): lax.all_to_all(outgoing, 'rep', split_axis=0, concat_axis=0, tiled=True)  9.75 us
    ppermute x3, waiting for transfers between devices, local(): lax.ppermute((to_partner, kv_part, squares), 'seq', perm=[(0, 1), (1, 0)])  7.12 us
    all_to_all x1, starting transfers between devices, local(): lax.all_to_all(outgoing, 'rep', split_axis=0, concat_axis=0, tiled=True)  6.44 us
    gather x2, local copies, waits for them, and re-layouts, fill_rows(): taken = jnp.take(table, indices.reshape(-1), axis=0)  4.98 us
  transfers between devices with their start and end apart: 6, of which 3 were waited for; matrix products, arithmetic and copies ran while one was open for 6% of the time, Pallas kernels for 0%

profile of v1, /device:TPU:56, one launch (start us, length us, event | category | flops | bytes accessed | tf_op | source)
XLA Modules:
  0.0 175.7 jit_solution(4423869843370620643)
XLA Ops:
  6.5 0.9 copy.41
  7.5 0.8 copy.40
  9.2 3.5 %gather_fusion = bf16[1536,128]{1,0:T(8,128)(2,1)S(1)} fusion(bf16[384,128]{1,0:T(8,128)(2,1)} %param.6, s32[2048]{0:T(1024)S(1)} %pad_clamp_fusion), kind=kCustom, calls=%fused_computation | custom fusion | bytes 792576 | tf_op jit(solution)/shard_map/jit(_take)/gather | solution.py:75
  12.7 1.3 select_select_fusion
  14.0 6.4 %all-to-all-start = ((bf16[8,192,128]{2,1,0:T(8,128)(2,1)}), bf16[8,192,128]{2,1,0:T(8,128)(2,1)S(1)}, u32[]{:S(2)}, u32[]{:S(2)}) async-start(bf16[8,192,128]{2,1,0:T(8,128)(2,1)} %select_select_fusion), calls=%async_computation | async-start | bytes 786432 | tf_op jit(solution)/shard_map/all_to_all | solution.py:114
  20.7 9.7 %all-to-all-done = bf16[8,192,128]{2,1,0:T(8,128)(2,1)S(1)} async-done(((bf16[8,192,128]{2,1,0:T(8,128)(2,1)}), bf16[8,192,128]{2,1,0:T(8,128)(2,1)S(1)}, u32[]{:S(2)}, u32[]{:S(2)}) %all-to-all-start) | async-done | bytes 393248 | tf_op jit(solution)/shard_map/all_to_all | solution.py:114
  30.4 1.4 gather_fusion.1
  31.9 0.8 fusion.17
  32.7 1.1 constant_dynamic-slice_fusion
  34.1 0.9 copy.44
  35.0 13.2 %all-to-all-start.1 = ((bf16[32,128,64]{1,2,0:T(8,128)(2,1)}), bf16[32,128,64]{1,2,0:T(8,128)(2,1)S(1)}, u32[]{:S(2)}, u32[]{:S(2)}) async-start(bf16[32,128,64]{1,2,0:T(8,128)(2,1)} %bitcast.15), calls=%async_computation.1 | async-start | bytes 1048576 | tf_op jit(solution)/shard_map/all_to_all | solution.py:124
  48.5 0.4 multiply_cosine_fusion
  49.0 73.7 %all-gather.2.cloned.1.call-done = bf16[32,384,128]{2,1,0:T(8,128)(2,1)} async-done(((bf16[1,384,128]{2,1,0:T(8,128)(2,1)}), bf16[32,384,128]{2,1,0:T(8,128)(2,1)}) %all-gather.2.cloned.1.call-update) | async-done | bytes 3145744 | tf_op jit(solution)/shard_map/all_gather | solution.py:126
  122.7 3.4 %fusion.1 = (f32[384]{0:T(512)S(1)}, bf16[32,384,128]{2,1,0:T(8,128)(2,1)S(1)}) fusion(bf16[32,384,128]{2,1,0:T(8,128)(2,1)} %all-gather.2.cloned.1.call-done, f32[32,128]{1,0:T(8,128)S(1)} %dynamic-slice_bitcast_fusion.1), kind=kLoop, calls=%fused_computation.5 | loop fusion | flops 7863936 | bytes 6309376 | tf_op jit(solution)/shard_map/reduce_sum | solution.py:132
  126.1 5.1 %collective-permute-start = (f32[384]{0:T(512)S(1)}, f32[384]{0:T(512)S(1)}, u32[]{:S(2)}, u32[]{:S(2)}) collective-permute-start(f32[384]{0:T(512)S(1)} %get-tuple-element.19), channel_id=1, source_target_pairs={{0,32},{32,0},{1,33},{33,1},{2,34},{34,2},{3,35},{35,3},{4,36},{36... | collective-permute-start | bytes 4616 | tf_op jit(solution)/shard_map/ppermute | solution.py:140
  131.2 1.0 convolution_bitcast_fusion
  132.2 4.7 %collective-permute-start.1 = (f32[192,256]{1,0:T(8,128)S(1)}, f32[192,256]{1,0:T(8,128)}, u32[]{:S(2)}, u32[]{:S(2)}) collective-permute-start(f32[192,256]{1,0:T(8,128)S(1)} %dynamic-slice_bitcast_fusion), channel_id=1, source_target_pairs={{0,32},{32,0},{1,33},{33,1},{2,34},{34,2},{3,35},{35,3},{4,36},{36... | collective-permute-start | bytes 589832 | tf_op jit(solution)/shard_map/ppermute | solution.py:140
  136.9 2.9 %convolution_bitcast_fusion.1 = f32[384,64]{0,1:T(8,128)S(1)} fusion(bf16[32,384,128]{2,1,0:T(8,128)(2,1)} %copy-done.1, bf16[32,128,64]{1,2,0:T(8,128)(2,1)S(1)} %all-to-all-done.1), kind=kOutput, calls=%fused_computation.15 | convolution fusion | flops 201326592 | bytes 3768320 | tf_op jit(solution)/shard_map/tri,tic->rc/dot_general | solution.py:135
  139.9 5.1 %collective-permute-start.2 = (f32[384,64]{0,1:T(8,128)S(1)}, f32[384,64]{0,1:T(8,128)S(1)}, u32[]{:S(2)}, u32[]{:S(2)}) collective-permute-start(f32[384,64]{0,1:T(8,128)S(1)} %convolution_bitcast_fusion.1), channel_id=1, source_target_pairs={{0,32},{32,0},{1,33},{33,1},{2,34},{34,2},{3,35},{35,3},{4,36},{36... | collective-permute-start | bytes 294920 | tf_op jit(solution)/shard_map/ppermute | solution.py:140
  145.0 7.1 %collective-permute-done.2 = f32[384,64]{0,1:T(8,128)S(1)} collective-permute-done((f32[384,64]{0,1:T(8,128)S(1)}, f32[384,64]{0,1:T(8,128)S(1)}, u32[]{:S(2)}, u32[]{:S(2)}) %collective-permute-start.2) | collective-permute-done | bytes 98336 | tf_op jit(solution)/shard_map/ppermute | solution.py:140
  152.5 13.6 %all_gather.9 = bf16[4,384,2,32]{1,3,2,0:T(8,128)(2,1)S(1)} all-gather(bf16[1,384,2,32]{1,3,2,0:T(8,128)(2,1)S(1)} %fusion.16), channel_id=1, replica_groups=mesh['rep'=8,'seq'=2,'tg'=8,'tu'=4] {'tu'}, dimensions={0}, use_global_device_ids=true | all-gather | bytes 245760 | tf_op jit(solution)/shard_map/all_gather | solution.py:169
  166.1 1.0 bitcast_multiply_fusion
  167.3 0.6 fusion.47
  168.1 0.7 bitcast_select_fusion
  (52 shorter events, 2.7 us)
Async XLA Ops:
  6.5 124.6 %copy-start = (bf16[4096,256]{1,0:T(8,128)(2,1)S(1)}, bf16[4096,256]{1,0:T(8,128)(2,1)}, u32[]{:S(2)}) copy-start(bf16[4096,256]{1,0:T(8,128)(2,1)} %param.8) | copy-start | bytes 6291460
  14.0 34.9 %copy-start.2 = (f32[8192]{0:T(1024)S(1)}, f32[8192]{0:T(1024)}, u32[]{:S(2)}) copy-start(f32[8192]{0:T(1024)} %param.7) | copy-start | bytes 98308
  14.0 16.4 %all-to-all-start = ((bf16[8,192,128]{2,1,0:T(8,128)(2,1)}), bf16[8,192,128]{2,1,0:T(8,128)(2,1)S(1)}, u32[]{:S(2)}, u32[]{:S(2)}) async-start(bf16[8,192,128]{2,1,0:T(8,128)(2,1)} %select_select_fusion), calls=%async_computation | async-start | bytes 786432 | tf_op jit(solution)/shard_map/all_to_all | solution.py:114
  20.5 102.2 %all-gather.2.cloned.1.call-start = ((), (), s32[]{:S(2)}) async-start(), calls=%async_computation.2 | async-start | bytes 3244032 | tf_op jit(solution)/shard_map/all_gather | solution.py:126
  35.0 101.9 %all-to-all-start.1 = ((bf16[32,128,64]{1,2,0:T(8,128)(2,1)}), bf16[32,128,64]{1,2,0:T(8,128)(2,1)S(1)}, u32[]{:S(2)}, u32[]{:S(2)}) async-start(bf16[32,128,64]{1,2,0:T(8,128)(2,1)} %bitcast.15), calls=%async_computation.1 | async-start | bytes 1048576 | tf_op jit(solution)/shard_map/all_to_all | solution.py:124
  126.1 6.1 %copy-start.1 = (bf16[32,384,128]{2,1,0:T(8,128)(2,1)}, bf16[32,384,128]{2,1,0:T(8,128)(2,1)S(1)}, u32[]{:S(2)}) copy-start(bf16[32,384,128]{2,1,0:T(8,128)(2,1)S(1)} %get-tuple-element.20) | copy-start | bytes 9437188
  126.1 18.9 %collective-permute-start = (f32[384]{0:T(512)S(1)}, f32[384]{0:T(512)S(1)}, u32[]{:S(2)}, u32[]{:S(2)}) collective-permute-start(f32[384]{0:T(512)S(1)} %get-tuple-element.19), channel_id=1, source_target_pairs={{0,32},{32,0},{1,33},{33,1},{2,34},{34,2},{3,35},{35,3},{4,36},{36... | collective-permute-start | bytes 4616 | tf_op jit(solution)/shard_map/ppermute | solution.py:140
  132.2 33.9 %collective-permute-start.1 = (f32[192,256]{1,0:T(8,128)S(1)}, f32[192,256]{1,0:T(8,128)}, u32[]{:S(2)}, u32[]{:S(2)}) collective-permute-start(f32[192,256]{1,0:T(8,128)S(1)} %dynamic-slice_bitcast_fusion), channel_id=1, source_target_pairs={{0,32},{32,0},{1,33},{33,1},{2,34},{34,2},{3,35},{35,3},{4,36},{36... | collective-permute-start | bytes 589832 | tf_op jit(solution)/shard_map/ppermute | solution.py:140
  139.9 12.3 %collective-permute-start.2 = (f32[384,64]{0,1:T(8,128)S(1)}, f32[384,64]{0,1:T(8,128)S(1)}, u32[]{:S(2)}, u32[]{:S(2)}) collective-permute-start(f32[384,64]{0,1:T(8,128)S(1)} %convolution_bitcast_fusion.1), channel_id=1, source_target_pairs={{0,32},{32,0},{1,33},{33,1},{2,34},{34,2},{3,35},{35,3},{4,36},{36... | collective-permute-start | bytes 294920 | tf_op jit(solution)/shard_map/ppermute | solution.py:140
Sparse Core Ops, SparseCore 0:
  32.8 89.8 all-gather.1

commit v2 on v1

--- a/solution.py
+++ b/solution.py
@@ -79,67 +79,69 @@
 def local(hidden, gain, w_query, w_keyval, lengths, routes):
     rep_count = lax.axis_size("rep")
     seq_count = lax.axis_size("seq")
-    group_size = lax.axis_size("tu")
-    tp_count = lax.axis_size("tg") * group_size
+    x_count = lax.axis_size("x")
+    group_size = lax.axis_size("zl")
+    z_count = lax.axis_size("zh") * group_size
+    tp_count = x_count * z_count
     replica = lax.axis_index("rep")
     seq_index = lax.axis_index("seq")
-    sub = lax.axis_index("tu")
+    sub = lax.axis_index("zl")
     feature_cols = hidden.shape[1]
     local_rows = BUFFER // seq_count
-    capacity = (RESP + rep_count - 1) // rep_count * LMAX
     head_count = w_query.shape[1] // HD
     kv_cols = 2 * HD // group_size
     quarter = HD // 4
 
     tables = response_tables(lengths, routes)
     flat_len, flat_route, group_of, dest_off, pair_off, src_start = tables
-    my_len = lax.dynamic_slice_in_dim(flat_len, replica * RESP, RESP)
     my_route = lax.dynamic_slice_in_dim(flat_route, replica * RESP, RESP)
-    my_pair = lax.dynamic_slice_in_dim(pair_off, replica * RESP, RESP)
     my_start = lax.dynamic_slice_in_dim(src_start, replica * RESP, RESP)
-    slot_ids = jnp.arange(capacity, dtype=jnp.int32)
+    first_block = lax.dynamic_slice_in_dim(hidden, my_start[0], LMAX, 0)
+    second_block = lax.dynamic_slice_in_dim(hidden, my_start[1], LMAX, 0)
     targets = jnp.arange(rep_count, dtype=jnp.int32)
-    offsets = jnp.broadcast_to(slot_ids[None, :], (rep_count, capacity))[:, :, None]
-    inside = (
-        (my_route[None, None, :] == targets[:, None, None])
-        & (my_pair[None, None, :] <= offsets)
-        & (offsets < (my_pair + my_len)[None, None, :])
-    )
-    inside_int = inside.astype(jnp.int32)
-    src_rows = jnp.sum(
-        inside_int * (my_start[None, None, :] + offsets - my_pair[None, None, :]), axis=2
-    )
-    present = jnp.any(inside, axis=2)
-    outgoing = fill_rows(hidden, src_rows, present)
+    outgoing = jnp.where(
+        (targets == my_route[0])[:, None, None], first_block[None], second_block[None]
+    ).reshape(rep_count * LMAX, feature_cols)
     incoming = lax.all_to_all(outgoing, "rep", split_axis=0, concat_axis=0, tiled=True)
     all_pos = jnp.arange(BUFFER, dtype=jnp.int32)
     segment, within, source_group, pair_first, source = locate(all_pos, replica, tables)
     valid = segment >= 0
-    gathered_idx = jnp.where(valid, source_group * capacity + all_pos - pair_first, 0)
+    gathered_idx = jnp.where(valid, source_group * LMAX + all_pos - pair_first, 0)
     assembled = fill_rows(incoming, gathered_idx, valid)
 
     w_half = lax.dynamic_index_in_dim(w_keyval, seq_index, 0, keepdims=False)
     w_half = w_half.reshape(feature_cols, KVH, 2, 2, 2, quarter)
     w_half = w_half.transpose(1, 2, 4, 0, 3, 5).reshape(tp_count, feature_cols, kv_cols)
-    w_kv = lax.all_to_all(w_half, ("tg", "tu"), split_axis=0, concat_axis=0, tiled=True)
-
-    gathered = lax.all_gather(assembled, ("tg", "tu"), axis=0, tiled=False)
+    w_kv = lax.all_to_all(w_half, ("x", "zh", "zl"), split_axis=0, concat_axis=0, tiled=True)
+    w_kv = w_kv.reshape(x_count, z_count, feature_cols, kv_cols)
+
+    gathered = lax.all_gather(assembled, "x", axis=0, tiled=False)
+    gathered = lax.all_gather(gathered, ("zh", "zl"), axis=0, tiled=False)
     gain_half = lax.dynamic_index_in_dim(
-        gain.reshape(seq_count, tp_count, feature_cols), seq_index, 0, keepdims=False
+        gain.reshape(seq_count, x_count, z_count, feature_cols), seq_index, 0, keepdims=False
     )
     gathered_f = gathered.astype(jnp.float32)
-    scaled = (gathered_f * gain_half[:, None, :]).astype(jnp.bfloat16)
-    squares = jnp.sum(gathered_f * gathered_f, axis=(0, 2))
-    w_q = w_query.reshape(tp_count, feature_cols, w_query.shape[1])
-    query_part = jnp.einsum("tri,tic->rc", scaled, w_q, preferred_element_type=jnp.float32)
-    kv_part = jnp.einsum("tri,tic->rc", scaled, w_kv, preferred_element_type=jnp.float32)
+    scaled = (gathered_f * gain_half.transpose(1, 0, 2)[:, :, None, :]).astype(jnp.bfloat16)
+    squares = jnp.sum(gathered_f * gathered_f, axis=(0, 1, 3))
+    w_q = w_query.reshape(x_count, z_count, feature_cols, w_query.shape[1])
+    query_part = jnp.einsum("zxri,xzic->rc", scaled, w_q, preferred_element_type=jnp.float32)
+    kv_part = jnp.einsum("zxri,xzic->rc", scaled, w_kv, preferred_element_type=jnp.float32)
 
     query_halves = query_part.reshape(seq_count, local_rows, query_part.shape[1])
     partner = seq_count - 1 - seq_index
     to_partner = lax.dynamic_index_in_dim(query_halves, partner, 0, keepdims=False)
-    got_query, got_kv, got_squares = lax.ppermute(
-        (to_partner, kv_part, squares), "seq", perm=[(0, 1), (1, 0)]
-    )
+    kv_rows = kv_part.reshape(seq_count, local_rows, kv_cols).transpose(1, 0, 2)
+    square_rows = squares.reshape(seq_count, local_rows).transpose(1, 0)
+    payload = jnp.concatenate(
+        [to_partner, kv_rows.reshape(local_rows, -1), square_rows], axis=1
+    )
+    got = lax.ppermute(payload, "seq", perm=[(0, 1), (1, 0)])
+    query_cols = query_part.shape[1]
+    kv_width = seq_count * kv_cols
+    got_query = got[:, :query_cols]
+    got_kv = got[:, query_cols : query_cols + kv_width].reshape(local_rows, seq_count, kv_cols)
+    got_kv = got_kv.transpose(1, 0, 2).reshape(BUFFER, kv_cols)
+    got_squares = got[:, query_cols + kv_width :].transpose(1, 0).reshape(BUFFER)
     query_raw = lax.dynamic_index_in_dim(query_halves, seq_index, 0, keepdims=False) + got_query
     kv_raw = kv_part + got_kv
     inverse_rms = lax.rsqrt((squares + got_squares) / D + NORM_EPS)
@@ -166,7 +168,12 @@
         axis=1,
     )
     piece = jnp.where(sub < 2, roped, kv_scaled).astype(jnp.bfloat16)
-    pieces = lax.all_gather(piece, "tu", axis=0, tiled=False)
+    shifted = [piece] + [
+        lax.ppermute(piece, "zl", perm=[(i, (i + k) % group_size) for i in range(group_size)])
+        for k in range(1, group_size)
+    ]
+    owners = (sub - jnp.arange(group_size, dtype=jnp.int32)) % group_size
+    pieces = jnp.take(jnp.stack(shifted), owners, axis=0)
     pieces = pieces.reshape(2, 2, BUFFER, 2, quarter).transpose(0, 2, 3, 1, 4)
     key_part = pieces[0].reshape(BUFFER, HD)
     value_part = pieces[1].reshape(BUFFER, HD)
@@ -200,11 +207,13 @@
     heads_per_kv = QH // KVH
     tp_count = mesh.shape["tp"]
     group_size = heads_per_kv * tp_count // QH
+    x_count = 4
+    z_count = tp_count // x_count
     devices = mesh.devices.reshape(
-        mesh.shape["rep"], mesh.shape["seq"], tp_count // group_size, group_size
-    )
-    grid = jax.sharding.Mesh(devices, ("rep", "seq", "tg", "tu"))
-    tp = ("tg", "tu")
+        mesh.shape["rep"], mesh.shape["seq"], x_count, z_count // group_size, group_size
+    )
+    grid = jax.sharding.Mesh(devices, ("rep", "seq", "x", "zh", "zl"))
+    tp = ("x", "zh", "zl")
     in_specs = (
         P("rep", ("seq",) + tp),
         P(),

time: 176 us -> 170 us (0.966); the launches traced: 176 us -> 168 us
  waiting for transfers between devices: 90.6 us -> 75 us
  other arithmetic: 9.2 us -> 14 us
  between operations: 13.7 us -> 17.8 us
  starting transfers between devices: 34.4 us -> 31.6 us
  matrix products: 4.75 us -> 6.64 us
    all_gather x1, waiting for transfers between devices: 73.7 us -> 40.3 us  [local(): gathered = lax.all_gather(gathered, ('zh', 'zl'), axis=0, tiled=False)]
    ppermute x3 -> x4, waiting for transfers between devices: 7.12 us -> 24.9 us  [the longest x1 19.9 us: local(): got = lax.ppermute(payload, 'seq', perm=[(0, 1), (1, 0)])]
    convert_element_type x0 -> x1, other arithmetic: none -> 4.61 us  [local(): (gathered_f * gain_half.transpose(1, 0, 2)[:, :, None, :]).astype(jnp.bfl...]
    gather x2 -> x1, local copies, waits for them, and re-layouts: 4.98 us -> 1.44 us  [fill_rows(): taken = jnp.take(table, indices.reshape(-1), axis=0)]
    ppermute x3 -> x4, starting transfers between devices: 14.8 us -> 12.4 us  [the longest x3 8.87 us: local(): lax.ppermute(piece, 'zl', perm=[(i, (i + k) % group_size) for i in range(...]
    select_n x2 -> x1, other arithmetic: 2.12 us -> 0.17 us  [fill_rows(): jnp.where(present.reshape(-1)[:, None], taken, jnp.zeros((), table.dtype))]
    dot_general x2, matrix products: 3.93 us -> 5.81 us  [the longest x1 2.95 us: local(): jnp.einsum('zxri,xzic->rc', scaled, w_kv, preferred_element_type=jnp.floa...]
    reduce_sum x3 -> x2, other arithmetic: 3.67 us -> 2.81 us  [the longest x1 2.58 us: local(): squares = jnp.sum(gathered_f * gathered_f, axis=(0, 1, 3))]
  transfers between devices with their start and end apart: 6 -> 7, of which waited for: 3 -> 5; matrix products, arithmetic and copies ran while one was open for 6% -> 8% of each run, Pallas kernels for 0% -> 0%
where the time goes in v2:
time: 170 us; the launch traced here: 168 us
  waiting for transfers between devices  75 us (44%)
  starting transfers between devices  31.6 us (19%)
  between operations  17.8 us (10%)
  other arithmetic  14 us (8%)
  blocking collectives  13.6 us (8%)
  local copies, waits for them, and re-layouts  9.08 us (5%)
  matrix products  6.64 us (4%)
    all_gather x1, waiting for transfers between devices, local(): gathered = lax.all_gather(gathered, ('zh', 'zl'), axis=0, tiled=False)  40.3 us
    ppermute x1, waiting for transfers between devices, local(): got = lax.ppermute(payload, 'seq', perm=[(0, 1), (1, 0)])  19.9 us
    all_gather x1, blocking collectives, local(): gathered = lax.all_gather(assembled, 'x', axis=0, tiled=False)  13.6 us
    all_to_all x1, starting transfers between devices, local(): lax.all_to_all(w_half, ('x', 'zh', 'zl'), split_axis=0, concat_axis=0, ti...  12.9 us
    all_to_all x1, waiting for transfers between devices, local(): lax.all_to_all(outgoing, 'rep', split_axis=0, concat_axis=0, tiled=True)  9.73 us
    ppermute x3, starting transfers between devices, local(): lax.ppermute(piece, 'zl', perm=[(i, (i + k) % group_size) for i in range(...  8.87 us
    all_to_all x1, starting transfers between devices, local(): lax.all_to_all(outgoing, 'rep', split_axis=0, concat_axis=0, tiled=True)  6.3 us
    ppermute x3, waiting for transfers between devices, local(): lax.ppermute(piece, 'zl', perm=[(i, (i + k) % group_size) for i in range(...  5.03 us
  transfers between devices with their start and end apart: 7, of which 5 were waited for; matrix products, arithmetic and copies ran while one was open for 8% of the time, Pallas kernels for 0%

profile of v2, /device:TPU:56, one launch (start us, length us, event | category | flops | bytes accessed | tf_op | source)
XLA Modules:
  0.0 167.8 jit_solution(10798916137678537865)
XLA Ops:
  6.5 0.9 copy.61
  13.5 0.9 constant_dynamic-slice_fusion.2
  14.4 0.8 broadcast_select_fusion
  15.2 6.3 %all-to-all-start = ((bf16[8,192,128]{2,1,0:T(8,128)(2,1)}), bf16[8,192,128]{2,1,0:T(8,128)(2,1)S(1)}, u32[]{:S(2)}, u32[]{:S(2)}) async-start(bf16[8,192,128]{2,1,0:T(8,128)(2,1)} %broadcast_select_fusion), calls=%async_computation | async-start | bytes 786432 | tf_op jit(solution)/shard_map/all_to_all | solution.py:105
  21.8 9.7 %all-to-all-done = bf16[8,192,128]{2,1,0:T(8,128)(2,1)S(1)} async-done(((bf16[8,192,128]{2,1,0:T(8,128)(2,1)}), bf16[8,192,128]{2,1,0:T(8,128)(2,1)S(1)}, u32[]{:S(2)}, u32[]{:S(2)}) %all-to-all-start) | async-done | bytes 393248 | tf_op jit(solution)/shard_map/all_to_all | solution.py:105
  31.5 1.4 gather_fusion
  33.1 13.6 %all_gather.10 = bf16[4,384,128]{2,1,0:T(8,128)(2,1)} all-gather(bf16[1,384,128]{2,1,0:T(8,128)(2,1)S(1)} %fusion.17), channel_id=1, replica_groups=mesh['rep'=8,'seq'=2,'x'=4,'zh'=2,'zl'=4] {'x'}, dimensions={0}, use_global_device_ids=true | all-gather | bytes 491520 | tf_op jit(solution)/shard_map/all_gather | solution.py:118
  46.8 1.1 constant_dynamic-slice_fusion
  48.1 0.9 copy.64
  49.0 12.9 %all-to-all-start.1 = ((bf16[32,128,64]{1,2,0:T(8,128)(2,1)}), bf16[32,128,64]{1,2,0:T(8,128)(2,1)S(1)}, u32[]{:S(2)}, u32[]{:S(2)}) async-start(bf16[32,128,64]{1,2,0:T(8,128)(2,1)} %bitcast.20), calls=%async_computation.1 | async-start | bytes 1048576 | tf_op jit(solution)/shard_map/all_to_all | solution.py:115
  63.5 40.3 %all-gather.3.cloned.1.call-done = bf16[32,384,128]{2,1,0:T(8,128)(2,1)} async-done(((bf16[4,384,128]{2,1,0:T(8,128)(2,1)}), bf16[32,384,128]{2,1,0:T(8,128)(2,1)}) %all-gather.3.cloned.1.call-update) | async-done | bytes 3145744 | tf_op jit(solution)/shard_map/all_gather | solution.py:119
  103.8 2.6 %multiply_reduce_fusion = f32[384]{0:T(512)S(1)} fusion(bf16[8,4,384,128]{3,2,1,0:T(8,128)(2,1)} %bitcast.93), kind=kLoop, calls=%fused_computation.5 | loop fusion | flops 4718208 | bytes 3147264 | tf_op jit(solution)/shard_map/reduce_sum | solution.py:125
  106.6 4.6 %fusion.1 = bf16[8,4,384,128]{3,2,0,1:T(8,128)(2,1)} fusion(f32[8,4,128]{2,0,1:T(8,128)S(1)} %dynamic-slice_bitcast_fusion.1, bf16[32,384,128]{2,1,0:T(8,128)(2,1)} %all-gather.3.cloned.1.call-done), kind=kLoop, calls=%fused_computation.4 | loop fusion | flops 4718592 | bytes 6307840 | tf_op jit(solution)/shard_map/convert_element_type | solution.py:124
  111.3 3.0 %convolution_bitcast_fusion.1 = f32[384,64]{0,1:T(8,128)S(1)} fusion(bf16[8,4,384,128]{3,2,0,1:T(8,128)(2,1)} %fusion.1, bf16[4,8,128,64]{2,3,1,0:T(8,128)(2,1)S(1)} %bitcast.96), kind=kOutput, calls=%fused_computation.14 | convolution fusion | flops 201326592 | bytes 3768320 | tf_op jit(solution)/shard_map/zxri,xzic->rc/dot_general | solution.py:128
  114.5 2.9 %convolution_bitcast_fusion = f32[2,192,256]{2,1,0:T(8,128)S(1)} fusion(bf16[2,192,128,4,8]{2,1,0,4,3:T(8,128)(2,1)} %bitcast.92, bf16[4,8,128,256,1]{3,2,4,1,0:T(8,128)(2,1)S(1)} %bitcast.91), kind=kOutput, calls=%fused_computation.11 | convolution fusion | flops 805306368 | bytes 5636096 | tf_op jit(solution)/shard_map/zxri,xzic->rc/dot_general | solution.py:127
  117.4 3.5 %collective-permute-start = (f32[192,386]{1,0:T(8,128)S(1)}, f32[192,386]{1,0:T(8,128)S(1)}, u32[]{:S(2)}, u32[]{:S(2)}) collective-permute-start(f32[192,386]{1,0:T(8,128)S(1)} %pad_maximum_fusion), channel_id=1, source_target_pairs={{0,32},{32,0},{1,33},{33,1},{2,34},{34,2},{3,35},{35,3},{4,36},{36... | collective-permute-start | bytes 889352 | tf_op jit(solution)/shard_map/ppermute | solution.py:138
  122.0 19.9 %collective-permute-done = f32[192,386]{1,0:T(8,128)S(1)} collective-permute-done((f32[192,386]{1,0:T(8,128)S(1)}, f32[192,386]{1,0:T(8,128)S(1)}, u32[]{:S(2)}, u32[]{:S(2)}) %collective-permute-start) | collective-permute-done | bytes 296480 | tf_op jit(solution)/shard_map/ppermute | solution.py:138
  142.6 0.9 fusion.24
  143.6 4.5 %collective-permute-start.3 = (bf16[384,2,32]{0,2,1:T(8,128)(2,1)S(1)}, bf16[384,2,32]{0,2,1:T(8,128)(2,1)S(1)}, u32[]{:S(2)}, u32[]{:S(2)}) collective-permute-start(bf16[384,2,32]{0,2,1:T(8,128)(2,1)S(1)} %fusion.16), channel_id=1, source_target_pairs={{0,3},{1,0},{2,1},{3,2},{4,7},{5,4},{6,5},{7,6},{8,11},{9,8},{10,9... | collective-permute-start | bytes 147464 | tf_op jit(solution)/shard_map/ppermute | solution.py:172
  148.0 1.9 %collective-permute-start.2 = (bf16[384,2,32]{0,2,1:T(8,128)(2,1)S(1)}, bf16[384,2,32]{0,2,1:T(8,128)(2,1)S(1)}, u32[]{:S(2)}, u32[]{:S(2)}) collective-permute-start(bf16[384,2,32]{0,2,1:T(8,128)(2,1)S(1)} %fusion.16), channel_id=1, source_target_pairs={{0,2},{1,3},{2,0},{3,1},{4,6},{5,7},{6,4},{7,5},{8,10},{9,11},{10,... | collective-permute-start | bytes 147464 | tf_op jit(solution)/shard_map/ppermute | solution.py:172
  150.0 2.5 %collective-permute-start.1 = (bf16[384,2,32]{0,2,1:T(8,128)(2,1)S(1)}, bf16[384,2,32]{0,2,1:T(8,128)(2,1)S(1)}, u32[]{:S(2)}, u32[]{:S(2)}) collective-permute-start(bf16[384,2,32]{0,2,1:T(8,128)(2,1)S(1)} %fusion.16), channel_id=1, source_target_pairs={{0,1},{1,2},{2,3},{3,0},{4,5},{5,6},{6,7},{7,4},{8,9},{9,10},{10,1... | collective-permute-start | bytes 147464 | tf_op jit(solution)/shard_map/ppermute | solution.py:172
  152.7 2.2 %collective-permute-done.2 = bf16[384,2,32]{0,2,1:T(8,128)(2,1)S(1)} collective-permute-done((bf16[384,2,32]{0,2,1:T(8,128)(2,1)S(1)}, bf16[384,2,32]{0,2,1:T(8,128)(2,1)S(1)}, u32[]{:S(2)}, u32[]{:S(2)}) %collective-permute-start.2) | collective-permute-done | bytes 49184 | tf_op jit(solution)/shard_map/ppermute | solution.py:172
  154.9 2.8 %collective-permute-done.1 = bf16[384,2,32]{0,2,1:T(8,128)(2,1)S(1)} collective-permute-done((bf16[384,2,32]{0,2,1:T(8,128)(2,1)S(1)}, bf16[384,2,32]{0,2,1:T(8,128)(2,1)S(1)}, u32[]{:S(2)}, u32[]{:S(2)}) %collective-permute-start.1) | collective-permute-done | bytes 49184 | tf_op jit(solution)/shard_map/ppermute | solution.py:172
  158.5 0.8 select_bitcast_fusion
  (71 shorter events, 9.0 us)
Async XLA Ops:
  6.5 107.9 %copy-start = (bf16[4096,256]{1,0:T(8,128)(2,1)S(1)}, bf16[4096,256]{1,0:T(8,128)(2,1)}, u32[]{:S(2)}) copy-start(bf16[4096,256]{1,0:T(8,128)(2,1)} %param.8) | copy-start | bytes 6291460
  15.2 16.3 %all-to-all-start = ((bf16[8,192,128]{2,1,0:T(8,128)(2,1)}), bf16[8,192,128]{2,1,0:T(8,128)(2,1)S(1)}, u32[]{:S(2)}, u32[]{:S(2)}) async-start(bf16[8,192,128]{2,1,0:T(8,128)(2,1)} %broadcast_select_fusion), calls=%async_computation | async-start | bytes 786432 | tf_op jit(solution)/shard_map/all_to_all | solution.py:105
  21.5 82.3 %all-gather.3.cloned.1.call-start = ((), (), s32[]{:S(2)}) async-start(), calls=%async_computation.2 | async-start | bytes 3538944 | tf_op jit(solution)/shard_map/all_gather | solution.py:119
  21.7 41.6 %copy-start.1 = (f32[8192]{0:T(1024)S(1)}, f32[8192]{0:T(1024)}, u32[]{:S(2)}) copy-start(f32[8192]{0:T(1024)} %param.7) | copy-start | bytes 98308
  49.0 62.3 %all-to-all-start.1 = ((bf16[32,128,64]{1,2,0:T(8,128)(2,1)}), bf16[32,128,64]{1,2,0:T(8,128)(2,1)S(1)}, u32[]{:S(2)}, u32[]{:S(2)}) async-start(bf16[32,128,64]{1,2,0:T(8,128)(2,1)} %bitcast.20), calls=%async_computation.1 | async-start | bytes 1048576 | tf_op jit(solution)/shard_map/all_to_all | solution.py:115
  62.7 48.5 %copy-start.2 = (pred[192]{0:T(512)(128)(4,1)}, pred[192]{0:T(512)(128)(4,1)S(1)}, u32[]{:S(2)}) copy-start(pred[192]{0:T(512)(128)(4,1)S(1)} %get-tuple-element.12) | copy-start | bytes 580
  117.4 24.5 %collective-permute-start = (f32[192,386]{1,0:T(8,128)S(1)}, f32[192,386]{1,0:T(8,128)S(1)}, u32[]{:S(2)}, u32[]{:S(2)}) collective-permute-start(f32[192,386]{1,0:T(8,128)S(1)} %pad_maximum_fusion), channel_id=1, source_target_pairs={{0,32},{32,0},{1,33},{33,1},{2,34},{34,2},{3,35},{35,3},{4,36},{36... | collective-permute-start | bytes 889352 | tf_op jit(solution)/shard_map/ppermute | solution.py:138
  143.6 9.2 %collective-permute-start.3 = (bf16[384,2,32]{0,2,1:T(8,128)(2,1)S(1)}, bf16[384,2,32]{0,2,1:T(8,128)(2,1)S(1)}, u32[]{:S(2)}, u32[]{:S(2)}) collective-permute-start(bf16[384,2,32]{0,2,1:T(8,128)(2,1)S(1)} %fusion.16), channel_id=1, source_target_pairs={{0,3},{1,0},{2,1},{3,2},{4,7},{5,4},{6,5},{7,6},{8,11},{9,8},{10,9... | collective-permute-start | bytes 147464 | tf_op jit(solution)/shard_map/ppermute | solution.py:172
  148.0 6.9 %collective-permute-start.2 = (bf16[384,2,32]{0,2,1:T(8,128)(2,1)S(1)}, bf16[384,2,32]{0,2,1:T(8,128)(2,1)S(1)}, u32[]{:S(2)}, u32[]{:S(2)}) collective-permute-start(bf16[384,2,32]{0,2,1:T(8,128)(2,1)S(1)} %fusion.16), channel_id=1, source_target_pairs={{0,2},{1,3},{2,0},{3,1},{4,6},{5,7},{6,4},{7,5},{8,10},{9,11},{10,... | collective-permute-start | bytes 147464 | tf_op jit(solution)/shard_map/ppermute | solution.py:172
  150.0 7.8 %collective-permute-start.1 = (bf16[384,2,32]{0,2,1:T(8,128)(2,1)S(1)}, bf16[384,2,32]{0,2,1:T(8,128)(2,1)S(1)}, u32[]{:S(2)}, u32[]{:S(2)}) collective-permute-start(bf16[384,2,32]{0,2,1:T(8,128)(2,1)S(1)} %fusion.16), channel_id=1, source_target_pairs={{0,1},{1,2},{2,3},{3,0},{4,5},{5,6},{6,7},{7,4},{8,9},{9,10},{10,1... | collective-permute-start | bytes 147464 | tf_op jit(solution)/shard_map/ppermute | solution.py:172
  152.7 7.5 %copy-start.3 = (pred[192]{0:T(512)(128)(4,1)S(1)}, pred[192]{0:T(512)(128)(4,1)}, u32[]{:S(2)}) copy-start(pred[192]{0:T(512)(128)(4,1)} %copy-done.2) | copy-start | bytes 580
Sparse Core Ops, SparseCore 0:
  46.9 56.9 all-gather.2

commit v3 on v2

--- a/solution.py
+++ b/solution.py
@@ -11,6 +11,7 @@
 HD = 128
 RESP = 2
 LMAX = 192
+LMIN = 128
 BUFFER = 384
 
 
@@ -76,6 +77,15 @@
     return jnp.where(present.reshape(-1)[:, None], taken, jnp.zeros((), table.dtype))
 
 
+def chunk_partials(rows, gain_grid, w_q, w_kv):
+    rows_f = rows.astype(jnp.float32)
+    scaled = (rows_f * gain_grid[:, :, None, :]).astype(jnp.bfloat16)
+    squares = jnp.sum(rows_f * rows_f, axis=(0, 1, 3))
+    query_part = jnp.einsum("zxri,xzic->rc", scaled, w_q, preferred_element_type=jnp.float32)
+    kv_part = jnp.einsum("zxri,xzic->rc", scaled, w_kv, preferred_element_type=jnp.float32)
+    return query_part, kv_part, squares
+
+
 def local(hidden, gain, w_query, w_keyval, lengths, routes):
     rep_count = lax.axis_size("rep")
     seq_count = lax.axis_size("seq")
@@ -85,10 +95,14 @@
     tp_count = x_count * z_count
     replica = lax.axis_index("rep")
     seq_index = lax.axis_index("seq")
+    partner = seq_count - 1 - seq_index
     sub = lax.axis_index("zl")
     feature_cols = hidden.shape[1]
     local_rows = BUFFER // seq_count
+    window = BUFFER - LMIN
+    rest = BUFFER - window
     head_count = w_query.shape[1] // HD
+    query_cols = w_query.shape[1]
     kv_cols = 2 * HD // group_size
     quarter = HD // 4
 
@@ -114,51 +128,77 @@
     w_half = w_half.transpose(1, 2, 4, 0, 3, 5).reshape(tp_count, feature_cols, kv_cols)
     w_kv = lax.all_to_all(w_half, ("x", "zh", "zl"), split_axis=0, concat_axis=0, tiled=True)
     w_kv = w_kv.reshape(x_count, z_count, feature_cols, kv_cols)
-
-    gathered = lax.all_gather(assembled, "x", axis=0, tiled=False)
-    gathered = lax.all_gather(gathered, ("zh", "zl"), axis=0, tiled=False)
-    gain_half = lax.dynamic_index_in_dim(
+    w_q = w_query.reshape(x_count, z_count, feature_cols, query_cols)
+    gain_grid = lax.dynamic_index_in_dim(
         gain.reshape(seq_count, x_count, z_count, feature_cols), seq_index, 0, keepdims=False
-    )
-    gathered_f = gathered.astype(jnp.float32)
-    scaled = (gathered_f * gain_half.transpose(1, 0, 2)[:, :, None, :]).astype(jnp.bfloat16)
-    squares = jnp.sum(gathered_f * gathered_f, axis=(0, 1, 3))
-    w_q = w_query.reshape(x_count, z_count, feature_cols, w_query.shape[1])
-    query_part = jnp.einsum("zxri,xzic->rc", scaled, w_q, preferred_element_type=jnp.float32)
-    kv_part = jnp.einsum("zxri,xzic->rc", scaled, w_kv, preferred_element_type=jnp.float32)
-
-    query_halves = query_part.reshape(seq_count, local_rows, query_part.shape[1])
-    partner = seq_count - 1 - seq_index
-    to_partner = lax.dynamic_index_in_dim(query_halves, partner, 0, keepdims=False)
-    kv_rows = kv_part.reshape(seq_count, local_rows, kv_cols).transpose(1, 0, 2)
-    square_rows = squares.reshape(seq_count, local_rows).transpose(1, 0)
+    ).transpose(1, 0, 2)
+
+    by_x = lax.all_gather(assembled, "x", axis=1, tiled=False)
+    first_at = partner * rest
+    second_at = seq_index * window
+    first_rows = lax.dynamic_slice_in_dim(by_x, first_at, window, 0)
+    second_rows = lax.dynamic_slice_in_dim(by_x, second_at, rest, 0)
+    first_all = lax.all_gather(first_rows.transpose(1, 0, 2), ("zh", "zl"), axis=0, tiled=False)
+    first_q, first_kv, first_sq = chunk_partials(first_all, gain_grid, w_q, w_kv)
+    shift = partner * (local_rows - rest)
     payload = jnp.concatenate(
-        [to_partner, kv_rows.reshape(local_rows, -1), square_rows], axis=1
-    )
+        [
+            lax.dynamic_slice_in_dim(first_q, shift, local_rows, 0).reshape(-1),
+            first_kv.reshape(-1),
+            first_sq,
+        ]
+    )
+    second_rows = second_rows.transpose(1, 0, 2)
+    payload, second_rows = lax.optimization_barrier((payload, second_rows))
     got = lax.ppermute(payload, "seq", perm=[(0, 1), (1, 0)])
-    query_cols = query_part.shape[1]
-    kv_width = seq_count * kv_cols
-    got_query = got[:, :query_cols]
-    got_kv = got[:, query_cols : query_cols + kv_width].reshape(local_rows, seq_count, kv_cols)
-    got_kv = got_kv.transpose(1, 0, 2).reshape(BUFFER, kv_cols)
-    got_squares = got[:, query_cols + kv_width :].transpose(1, 0).reshape(BUFFER)
-    query_raw = lax.dynamic_index_in_dim(query_halves, seq_index, 0, keepdims=False) + got_query
-    kv_raw = kv_part + got_kv
-    inverse_rms = lax.rsqrt((squares + got_squares) / D + NORM_EPS)
-
-    query_pos = seq_index * local_rows + jnp.arange(local_rows, dtype=jnp.int32)
-    query_seg = lax.dynamic_slice_in_dim(segment, seq_index * local_rows, local_rows)
-    query_within = lax.dynamic_slice_in_dim(within, seq_index * local_rows, local_rows)
-    query_rms = lax.dynamic_slice_in_dim(inverse_rms, seq_index * local_rows, local_rows)
+    second_all = lax.all_gather(second_rows, ("zh", "zl"), axis=0, tiled=False)
+    got, second_all = lax.optimization_barrier((got, second_all))
+    second_q, second_kv, second_sq = chunk_partials(second_all, gain_grid, w_q, w_kv)
+
+    low_first = seq_index > 0
+    own_q = jnp.where(
+        low_first,
+        jnp.concatenate([first_q, second_q], axis=0),
+        jnp.concatenate([second_q, first_q], axis=0),
+    )
+    own_kv = jnp.where(
+        low_first,
+        jnp.concatenate([first_kv, second_kv], axis=0),
+        jnp.concatenate([second_kv, first_kv], axis=0),
+    )
+    own_sq = jnp.where(
+        low_first,
+        jnp.concatenate([first_sq, second_sq], axis=0),
+        jnp.concatenate([second_sq, first_sq], axis=0),
+    )
+    q_size = local_rows * query_cols
+    kv_size = window * kv_cols
+    got_query = got[:q_size].reshape(local_rows, query_cols)
+    got_kv = got[q_size : q_size + kv_size].reshape(window, kv_cols)
+    got_sq = got[q_size + kv_size :]
+
+    win_at = seq_index * rest
+    query_at = seq_index * local_rows
+    query_raw = lax.dynamic_slice_in_dim(own_q, query_at, local_rows, 0) + got_query
+    kv_raw = lax.dynamic_slice_in_dim(own_kv, win_at, window, 0) + got_kv
+    win_rms = lax.rsqrt((lax.dynamic_slice_in_dim(own_sq, win_at, window) + got_sq) / D + NORM_EPS)
+    query_rms = lax.dynamic_slice_in_dim(win_rms, query_at - win_at, local_rows)
+
+    query_pos = query_at + jnp.arange(local_rows, dtype=jnp.int32)
+    query_seg = lax.dynamic_slice_in_dim(segment, query_at, local_rows)
+    query_within = lax.dynamic_slice_in_dim(within, query_at, local_rows)
     query_valid = query_seg >= 0
     queries = rotary(
         query_rms[:, None, None] * query_raw.reshape(local_rows, head_count, HD), query_within
     ).astype(jnp.bfloat16)
 
-    kv_scaled = (inverse_rms[:, None] * kv_raw).reshape(BUFFER, 2, quarter)
+    key_pos = win_at + jnp.arange(window, dtype=jnp.int32)
+    key_seg = lax.dynamic_slice_in_dim(segment, win_at, window)
+    key_within = lax.dynamic_slice_in_dim(within, win_at, window)
+    kv_scaled = (win_rms[:, None] * kv_raw).reshape(window, 2, quarter)
     freq_index = (sub % 2 * quarter + jnp.arange(quarter, dtype=jnp.int32)).astype(jnp.float32)
     inverse = jnp.power(ROPE_BASE, -2.0 * freq_index / HD)
-    angles = within.astype(jnp.float32)[:, None] * inverse[None, :]
+    angles = key_within.astype(jnp.float32)[:, None] * inverse[None, :]
     cosine = jnp.cos(angles)
     sine_part = jnp.sin(angles)
     lower_half = kv_scaled[:, 0]
@@ -174,13 +214,12 @@
     ]
     owners = (sub - jnp.arange(group_size, dtype=jnp.int32)) % group_size
     pieces = jnp.take(jnp.stack(shifted), owners, axis=0)
-    pieces = pieces.reshape(2, 2, BUFFER, 2, quarter).transpose(0, 2, 3, 1, 4)
-    key_part = pieces[0].reshape(BUFFER, HD)
-    value_part = pieces[1].reshape(BUFFER, HD)
+    pieces = pieces.reshape(2, 2, window, 2, quarter).transpose(0, 2, 3, 1, 4)
+    key_part = pieces[0].reshape(window, HD)
+    value_part = pieces[1].reshape(window, HD)
 
     score_scale = 1.0 / math.sqrt(HD)
-    key_pos = all_pos
-    allowed = (segment[None, :] == query_seg[:, None]) & query_valid[:, None] & (
+    allowed = (key_seg[None, :] == query_seg[:, None]) & query_valid[:, None] & (
         key_pos[None, :] <= query_pos[:, None]
     ) | (key_pos[None, :] == query_pos[:, None])
     scores = (

time: 170 us -> 182 us (1.071)
  local copies, waits for them, and re-layouts: 9.08 us -> 15.4 us
  matrix products: 6.64 us -> 9.2 us
  other arithmetic: 14 us -> 16.3 us
    all_gather x1 -> x2, waiting for transfers between devices: 40.3 us -> 56.4 us  [the longest x1 35.9 us: local(): lax.all_gather(first_rows.transpose(1, 0, 2), ('zh', 'zl'), axis=0, tiled...]
    ppermute x1, waiting for transfers between devices: 19.9 us -> 10.4 us  [local(): got = lax.ppermute(payload, 'seq', perm=[(0, 1), (1, 0)])]
    ppermute x3, waiting for transfers between devices: 5.03 us -> 0.01 us  [local(): lax.ppermute(piece, 'zl', perm=[(i, (i + k) % group_size) for i in range(...]
    convert_element_type x2 -> x1, other arithmetic: 4.61 us -> 0.67 us  [local(): angles = key_within.astype(jnp.float32)[:, None] * inverse[None, :]]
    dot_general x2 -> x4, matrix products: 5.81 us -> 8.48 us  [the longest x2 5.08 us: chunk_partials(): jnp.einsum('zxri,xzic->rc', scaled, w_kv, preferred_element_type=jnp.floa...]
    slice x5 -> x7, local copies, waits for them, and re-layouts: 0.15 us -> 2.63 us  [the longest x2 2.6 us: local(): got_query = got[:q_size].reshape(local_rows, query_cols)]
  transfers between devices with their start and end apart: 7 -> 8, of which waited for: 5 -> 4; matrix products, arithmetic and copies ran while one was open for 8% -> 9% of each run, Pallas kernels for 0% -> 0%
where the time goes in v3:
time: 182 us; the launch traced here: 180 us
  waiting for transfers between devices  76 us (42%)
  starting transfers between devices  32.2 us (18%)
  between operations  17.5 us (10%)
  other arithmetic  16.3 us (9%)
  local copies, waits for them, and re-layouts  15.4 us (8%)
  blocking collectives  12.9 us (7%)
  matrix products  9.2 us (5%)
    all_gather x1, waiting for transfers between devices, local(): lax.all_gather(first_rows.transpose(1, 0, 2), ('zh', 'zl'), axis=0, tiled...  35.9 us
    all_gather x1, waiting for transfers between devices, local(): second_all = lax.all_gather(second_rows, ('zh', 'zl'), axis=0, tiled=False)  20.6 us
    all_to_all x1, starting transfers between devices, local(): lax.all_to_all(w_half, ('x', 'zh', 'zl'), split_axis=0, concat_axis=0, ti...  12.9 us
    all_gather x1, blocking collectives, local(): by_x = lax.all_gather(assembled, 'x', axis=1, tiled=False)  12.9 us
    ppermute x1, waiting for transfers between devices, local(): got = lax.ppermute(payload, 'seq', perm=[(0, 1), (1, 0)])  10.4 us
    all_to_all x1, waiting for transfers between devices, local(): lax.all_to_all(outgoing, 'rep', split_axis=0, concat_axis=0, tiled=True)  9.16 us
    ppermute x3, starting transfers between devices, local(): lax.ppermute(piece, 'zl', perm=[(i, (i + k) % group_size) for i in range(...  8.83 us
    all_to_all x1, starting transfers between devices, local(): lax.all_to_all(outgoing, 'rep', split_axis=0, concat_axis=0, tiled=True)  6.31 us
  transfers between devices with their start and end apart: 8, of which 4 were waited for; matrix products, arithmetic and copies ran while one was open for 9% of the time, Pallas kernels for 0%

profile of v3, /device:TPU:56, one launch (start us, length us, event | category | flops | bytes accessed | tf_op | source)
XLA Modules:
  0.0 179.5 jit_solution(5180426073790916484)
XLA Ops:
  14.8 6.3 %all-to-all-start = ((bf16[8,192,128]{2,1,0:T(8,128)(2,1)}), bf16[8,192,128]{2,1,0:T(8,128)(2,1)S(1)}, u32[]{:S(2)}, u32[]{:S(2)}) async-start(bf16[8,192,128]{2,1,0:T(8,128)(2,1)} %broadcast_select_fusion), calls=%async_computation | async-start | bytes 786432 | tf_op jit(solution)/shard_map/all_to_all | solution.py:119
  21.9 9.2 %all-to-all-done = bf16[8,192,128]{2,1,0:T(8,128)(2,1)S(1)} async-done(((bf16[8,192,128]{2,1,0:T(8,128)(2,1)}), bf16[8,192,128]{2,1,0:T(8,128)(2,1)S(1)}, u32[]{:S(2)}, u32[]{:S(2)}) %all-to-all-start) | async-done | bytes 393248 | tf_op jit(solution)/shard_map/all_to_all | solution.py:119
  31.0 1.4 gather_fusion
  32.6 12.9 %all_gather.16 = bf16[384,4,128]{2,0,1:T(8,128)(2,1)S(1)} all-gather(bf16[384,1,128]{2,0,1:T(8,128)(2,1)S(1)} %fusion.23), channel_id=1, replica_groups=mesh['rep'=8,'seq'=2,'x'=4,'zh'=2,'zl'=4] {'x'}, dimensions={1}, use_global_device_ids=true | all-gather | bytes 491520 | tf_op jit(solution)/shard_map/all_gather | solution.py:136
  46.3 1.1 constant_dynamic-slice_fusion
  48.5 12.9 %all-to-all-start.1 = ((bf16[32,128,64]{1,2,0:T(8,128)(2,1)}), bf16[32,128,64]{1,2,0:T(8,128)(2,1)S(1)}, u32[]{:S(2)}, u32[]{:S(2)}) async-start(bf16[32,128,64]{1,2,0:T(8,128)(2,1)} %bitcast.16), calls=%async_computation.1 | async-start | bytes 1048576 | tf_op jit(solution)/shard_map/all_to_all | solution.py:129
  62.2 35.9 %all-gather.5.cloned.1.call-done = bf16[32,256,128]{2,1,0:T(8,128)(2,1)} async-done(((bf16[4,256,128]{2,1,0:T(8,128)(2,1)}), bf16[32,256,128]{2,1,0:T(8,128)(2,1)}) %all-gather.5.cloned.1.call-update) | async-done | bytes 2097168 | tf_op jit(solution)/shard_map/all_gather | solution.py:141
  98.0 2.1 %multiply_reduce_fusion = f32[256]{0:T(256)S(1)} fusion(bf16[8,4,256,128]{3,2,1,0:T(8,128)(2,1)} %bitcast.89), kind=kLoop, calls=%fused_computation.5 | loop fusion | flops 3145472 | bytes 2098176 | tf_op jit(solution)/shard_map/reduce_sum | solution.py:83
  100.2 2.5 %convolution_bitcast_fusion.2 = f32[256,64]{0,1:T(8,128)S(1)} fusion(bf16[4,8,128,64]{2,3,1,0:T(8,128)(2,1)S(1)} %bitcast.98, f32[8,4,128]{2,0,1:T(8,128)S(1)} %dynamic-slice_bitcast_fusion.3, bf16[32,256,128]{2,1,0:T(8,128)(2,1)} %all-gather.5.cloned.1.call-done), kind=kOutput, calls=%fused_computation.20 | convolution fusion | flops 137363456 | bytes 2703360 | tf_op jit(solution)/shard_map/zxri,xzic->rc/dot_general | solution.py:85
  102.9 2.3 %convolution_bitcast_fusion = f32[256,256]{1,0:T(8,128)S(1)} fusion(bf16[4,8,128,256]{3,2,1,0:T(8,128)(2,1)S(1)} %bitcast.85, f32[8,4,128]{2,0,1:T(8,128)S(1)} %dynamic-slice_bitcast_fusion.3, bf16[32,256,128]{2,1,0:T(8,128)(2,1)} %all-gather.5.cloned.1.call-done), kind=kOutput, calls=%fused_computation.15 | convolution fusion | flops 540016640 | bytes 4472832 | tf_op jit(solution)/shard_map/zxri,xzic->rc/dot_general | solution.py:84
  108.4 4.1 %collective-permute-start = (f32[65792]{0:T(1024)S(1)}, f32[65792]{0:T(1024)S(1)}, u32[]{:S(2)}, u32[]{:S(2)}) collective-permute-start(f32[65792]{0:T(1024)S(1)} %pad_maximum_fusion), channel_id=1, source_target_pairs={{0,32},{32,0},{1,33},{33,1},{2,34},{34,2},{3,35},{35,3},{4,36},{36... | collective-permute-start | bytes 789512 | tf_op jit(solution)/shard_map/ppermute | solution.py:153
  113.0 1.1 multiply_cosine_fusion
  114.1 10.4 %collective-permute-done = f32[65792]{0:T(1024)S(1)} collective-permute-done((f32[65792]{0:T(1024)S(1)}, f32[65792]{0:T(1024)S(1)}, u32[]{:S(2)}, u32[]{:S(2)}) %collective-permute-start) | collective-permute-done | bytes 263200 | tf_op jit(solution)/shard_map/ppermute | solution.py:153
  125.2 20.6 %all-gather.7.cloned.1.call-done = bf16[32,128,128]{2,1,0:T(8,128)(2,1)} async-done(((bf16[4,128,128]{2,1,0:T(8,128)(2,1)}), bf16[32,128,128]{2,1,0:T(8,128)(2,1)}) %all-gather.7.cloned.1.call-update) | async-done | bytes 1048592 | tf_op jit(solution)/shard_map/all_gather | solution.py:154
  145.8 2.5 %convolution_bitcast_fusion.3 = f32[128,64]{0,1:T(8,128)} fusion(bf16[4,8,128,64]{2,3,1,0:T(8,128)(2,1)} %bitcast.99, f32[8,4,128]{2,0,1:T(8,128)S(1)} %dynamic-slice_bitcast_fusion.3, bf16[8,4,128,128]{3,2,1,0:T(8,128)(2,1)} %bitcast.94), kind=kOutput, calls=%fused_computation.21 | convolution fusion | flops 68681728 | bytes 1622016 | tf_op jit(solution)/shard_map/zxri,xzic->rc/dot_general | solution.py:85
  149.9 1.6 copy.60
  154.8 4.4 %collective-permute-start.3 = (bf16[256,2,32]{0,2,1:T(8,128)(2,1)S(1)}, bf16[256,2,32]{0,2,1:T(8,128)(2,1)}, u32[]{:S(2)}, u32[]{:S(2)}) collective-permute-start(bf16[256,2,32]{0,2,1:T(8,128)(2,1)S(1)} %fusion.30), channel_id=1, source_target_pairs={{0,3},{1,0},{2,1},{3,2},{4,7},{5,4},{6,5},{7,6},{8,11},{9,8},{10,9... | collective-permute-start | bytes 98312 | tf_op jit(solution)/shard_map/ppermute | solution.py:212
  159.2 1.9 %collective-permute-start.2 = (bf16[256,2,32]{0,2,1:T(8,128)(2,1)S(1)}, bf16[256,2,32]{0,2,1:T(8,128)(2,1)}, u32[]{:S(2)}, u32[]{:S(2)}) collective-permute-start(bf16[256,2,32]{0,2,1:T(8,128)(2,1)S(1)} %fusion.30), channel_id=1, source_target_pairs={{0,2},{1,3},{2,0},{3,1},{4,6},{5,7},{6,4},{7,5},{8,10},{9,11},{10,... | collective-permute-start | bytes 98312 | tf_op jit(solution)/shard_map/ppermute | solution.py:212
  161.1 2.5 %collective-permute-start.1 = (bf16[256,2,32]{0,2,1:T(8,128)(2,1)S(1)}, bf16[256,2,32]{0,2,1:T(8,128)(2,1)}, u32[]{:S(2)}, u32[]{:S(2)}) collective-permute-start(bf16[256,2,32]{0,2,1:T(8,128)(2,1)S(1)} %fusion.30), channel_id=1, source_target_pairs={{0,1},{1,2},{2,3},{3,0},{4,5},{5,6},{6,7},{7,4},{8,9},{9,10},{10,1... | collective-permute-start | bytes 98312 | tf_op jit(solution)/shard_map/ppermute | solution.py:212
  163.6 1.6 slice.58
  165.2 1.1 convolution_bitcast_fusion.1
  166.4 1.0 slice.59
  167.4 1.0 bitcast_multiply_fusion
  168.4 1.1 subtract_convert_fusion
  (95 shorter events, 20.5 us)
Async XLA Ops:
  6.5 96.4 %copy-start = (bf16[4096,256]{1,0:T(8,128)(2,1)S(1)}, bf16[4096,256]{1,0:T(8,128)(2,1)}, u32[]{:S(2)}) copy-start(bf16[4096,256]{1,0:T(8,128)(2,1)} %param.8) | copy-start | bytes 6291460
  14.8 16.3 %all-to-all-start = ((bf16[8,192,128]{2,1,0:T(8,128)(2,1)}), bf16[8,192,128]{2,1,0:T(8,128)(2,1)S(1)}, u32[]{:S(2)}, u32[]{:S(2)}) async-start(bf16[8,192,128]{2,1,0:T(8,128)(2,1)} %broadcast_select_fusion), calls=%async_computation | async-start | bytes 786432 | tf_op jit(solution)/shard_map/all_to_all | solution.py:119
  21.1 77.0 %all-gather.5.cloned.1.call-start = ((), (), s32[]{:S(2)}) async-start(), calls=%async_computation.2 | async-start | bytes 2359296 | tf_op jit(solution)/shard_map/all_gather | solution.py:141
  47.6 13.9 %copy-start.8 = (f32[8192]{0:T(1024)S(1)}, f32[8192]{0:T(1024)}, u32[]{:S(2)}) copy-start(f32[8192]{0:T(1024)} %param.7) | copy-start | bytes 98308
  48.5 51.7 %all-to-all-start.1 = ((bf16[32,128,64]{1,2,0:T(8,128)(2,1)}), bf16[32,128,64]{1,2,0:T(8,128)(2,1)S(1)}, u32[]{:S(2)}, u32[]{:S(2)}) async-start(bf16[32,128,64]{1,2,0:T(8,128)(2,1)} %bitcast.16), calls=%async_computation.1 | async-start | bytes 1048576 | tf_op jit(solution)/shard_map/all_to_all | solution.py:129
  61.4 84.4 %all-gather.7.cloned.1.call-start = ((), (), s32[]{:S(2)}) async-start(), calls=%async_computation.3 | async-start | bytes 1179648 | tf_op jit(solution)/shard_map/all_gather | solution.py:154
  100.1 5.2 %copy-start.5 = (f32[256]{0:T(256)}, f32[256]{0:T(256)S(1)}, u32[]{:S(2)}) copy-start(f32[256]{0:T(256)S(1)} %multiply_reduce_fusion) | copy-start | bytes 3076
  100.2 2.6 %copy-start.2 = (bf16[32,128,64]{1,2,0:T(8,128)(2,1)}, bf16[32,128,64]{1,2,0:T(8,128)(2,1)S(1)}, u32[]{:S(2)}) copy-start(bf16[32,128,64]{1,2,0:T(8,128)(2,1)S(1)} %all-to-all-done.1) | copy-start | bytes 1572868
  102.9 2.6 %copy-start.6 = (s32[384]{0:T(512)S(1)}, s32[384]{0:T(512)}, u32[]{:S(2)}) copy-start(s32[384]{0:T(512)} %get-tuple-element.32) | copy-start | bytes 4612
  102.9 3.3 %copy-start.7 = (s32[384]{0:T(512)S(1)}, s32[384]{0:T(512)}, u32[]{:S(2)}) copy-start(s32[384]{0:T(512)} %get-tuple-element.22) | copy-start | bytes 4612
  107.0 0.6 copy-start.9
  108.4 16.1 %collective-permute-start = (f32[65792]{0:T(1024)S(1)}, f32[65792]{0:T(1024)S(1)}, u32[]{:S(2)}, u32[]{:S(2)}) collective-permute-start(f32[65792]{0:T(1024)S(1)} %pad_maximum_fusion), channel_id=1, source_target_pairs={{0,32},{32,0},{1,33},{33,1},{2,34},{34,2},{3,35},{35,3},{4,36},{36... | collective-permute-start | bytes 789512 | tf_op jit(solution)/shard_map/ppermute | solution.py:153
  124.5 0.7 copy-start.3
  145.8 2.5 %copy-start.1 = (bf16[32,128,128]{2,1,0:T(8,128)(2,1)S(1)}, bf16[32,128,128]{2,1,0:T(8,128)(2,1)}, u32[]{:S(2)}) copy-start(bf16[32,128,128]{2,1,0:T(8,128)(2,1)} %all-gather.7.cloned.1.call-done) | copy-start | bytes 3145732
  145.8 3.3 %slice-start = ((f32[65792]{0:T(1024)}), f32[16384]{0:T(1024)S(1)}, s32[]{:S(2)}) async-start(f32[65792]{0:T(1024)} %copy-done.3), calls=%async_computation.4 | async-start | bytes 131072 | tf_op jit(solution)/shard_map/slice | solution.py:177
  154.8 14.8 %collective-permute-start.3 = (bf16[256,2,32]{0,2,1:T(8,128)(2,1)S(1)}, bf16[256,2,32]{0,2,1:T(8,128)(2,1)}, u32[]{:S(2)}, u32[]{:S(2)}) collective-permute-start(bf16[256,2,32]{0,2,1:T(8,128)(2,1)S(1)} %fusion.30), channel_id=1, source_target_pairs={{0,3},{1,0},{2,1},{3,2},{4,7},{5,4},{6,5},{7,6},{8,11},{9,8},{10,9... | collective-permute-start | bytes 98312 | tf_op jit(solution)/shard_map/ppermute | solution.py:212
  159.2 10.3 %collective-permute-start.2 = (bf16[256,2,32]{0,2,1:T(8,128)(2,1)S(1)}, bf16[256,2,32]{0,2,1:T(8,128)(2,1)}, u32[]{:S(2)}, u32[]{:S(2)}) collective-permute-start(bf16[256,2,32]{0,2,1:T(8,128)(2,1)S(1)} %fusion.30), channel_id=1, source_target_pairs={{0,2},{1,3},{2,0},{3,1},{4,6},{5,7},{6,4},{7,5},{8,10},{9,11},{10,... | collective-permute-start | bytes 98312 | tf_op jit(solution)/shard_map/ppermute | solution.py:212
  161.1 8.4 %collective-permute-start.1 = (bf16[256,2,32]{0,2,1:T(8,128)(2,1)S(1)}, bf16[256,2,32]{0,2,1:T(8,128)(2,1)}, u32[]{:S(2)}, u32[]{:S(2)}) collective-permute-start(bf16[256,2,32]{0,2,1:T(8,128)(2,1)S(1)} %fusion.30), channel_id=1, source_target_pairs={{0,1},{1,2},{2,3},{3,0},{4,5},{5,6},{6,7},{7,4},{8,9},{9,10},{10,1... | collective-permute-start | bytes 98312 | tf_op jit(solution)/shard_map/ppermute | solution.py:212
  166.3 4.7 %copy-start.11 = (pred[2,2]{1,0:T(4,128)(4,1)S(1)}, pred[2,2]{1,0:T(4,128)(4,1)}, u32[]{:S(2)}) copy-start(pred[2,2]{1,0:T(4,128)(4,1)} %compare_and_fusion.3) | copy-start | bytes 16
  166.4 4.8 %copy-start.4 = (pred[192,256]{1,0:T(8,128)(4,1)S(1)}, pred[192,256]{1,0:T(8,128)(4,1)}, u32[]{:S(2)}) copy-start(pred[192,256]{1,0:T(8,128)(4,1)} %compare_or_fusion) | copy-start | bytes 147460
  169.5 2.4 %copy-start.10 = (pred[192]{0:T(512)(128)(4,1)S(1)}, pred[192]{0:T(512)(128)(4,1)}, u32[]{:S(2)}) copy-start(pred[192]{0:T(512)(128)(4,1)} %copy-done.9) | copy-start | bytes 580
Sparse Core Ops, SparseCore 0:
  46.4 51.6 all-gather.4
  105.6 40.1 all-gather.6

commit v4 on v2

--- a/solution.py
+++ b/solution.py
@@ -11,6 +11,7 @@
 HD = 128
 RESP = 2
 LMAX = 192
+LMIN = 128
 BUFFER = 384
 
 
@@ -102,18 +103,18 @@
     outgoing = jnp.where(
         (targets == my_route[0])[:, None, None], first_block[None], second_block[None]
     ).reshape(rep_count * LMAX, feature_cols)
+    w_half = lax.dynamic_index_in_dim(w_keyval, seq_index, 0, keepdims=False)
+    w_half = w_half.reshape(feature_cols, KVH, 2, 2, 2, quarter)
+    w_half = w_half.transpose(1, 2, 4, 0, 3, 5).reshape(tp_count, feature_cols, kv_cols)
+    w_kv = lax.all_to_all(w_half, ("x", "zh", "zl"), split_axis=0, concat_axis=0, tiled=True)
     incoming = lax.all_to_all(outgoing, "rep", split_axis=0, concat_axis=0, tiled=True)
+    w_kv, incoming = lax.optimization_barrier((w_kv, incoming))
+    w_kv = w_kv.reshape(x_count, z_count, feature_cols, kv_cols)
     all_pos = jnp.arange(BUFFER, dtype=jnp.int32)
     segment, within, source_group, pair_first, source = locate(all_pos, replica, tables)
     valid = segment >= 0
     gathered_idx = jnp.where(valid, source_group * LMAX + all_pos - pair_first, 0)
     assembled = fill_rows(incoming, gathered_idx, valid)
-
-    w_half = lax.dynamic_index_in_dim(w_keyval, seq_index, 0, keepdims=False)
-    w_half = w_half.reshape(feature_cols, KVH, 2, 2, 2, quarter)
-    w_half = w_half.transpose(1, 2, 4, 0, 3, 5).reshape(tp_count, feature_cols, kv_cols)
-    w_kv = lax.all_to_all(w_half, ("x", "zh", "zl"), split_axis=0, concat_axis=0, tiled=True)
-    w_kv = w_kv.reshape(x_count, z_count, feature_cols, kv_cols)
 
     gathered = lax.all_gather(assembled, "x", axis=0, tiled=False)
     gathered = lax.all_gather(gathered, ("zh", "zl"), axis=0, tiled=False)
@@ -127,38 +128,47 @@
     query_part = jnp.einsum("zxri,xzic->rc", scaled, w_q, preferred_element_type=jnp.float32)
     kv_part = jnp.einsum("zxri,xzic->rc", scaled, w_kv, preferred_element_type=jnp.float32)
 
-    query_halves = query_part.reshape(seq_count, local_rows, query_part.shape[1])
+    window = BUFFER - LMIN
+    rest = BUFFER - window
     partner = seq_count - 1 - seq_index
-    to_partner = lax.dynamic_index_in_dim(query_halves, partner, 0, keepdims=False)
-    kv_rows = kv_part.reshape(seq_count, local_rows, kv_cols).transpose(1, 0, 2)
-    square_rows = squares.reshape(seq_count, local_rows).transpose(1, 0)
+    query_cols = query_part.shape[1]
     payload = jnp.concatenate(
-        [to_partner, kv_rows.reshape(local_rows, -1), square_rows], axis=1
+        [
+            lax.dynamic_slice_in_dim(query_part, partner * local_rows, local_rows, 0).reshape(-1),
+            lax.dynamic_slice_in_dim(kv_part, partner * rest, window, 0).reshape(-1),
+            lax.dynamic_slice_in_dim(squares, partner * rest, window),
+        ]
     )
     got = lax.ppermute(payload, "seq", perm=[(0, 1), (1, 0)])
-    query_cols = query_part.shape[1]
-    kv_width = seq_count * kv_cols
-    got_query = got[:, :query_cols]
-    got_kv = got[:, query_cols : query_cols + kv_width].reshape(local_rows, seq_count, kv_cols)
-    got_kv = got_kv.transpose(1, 0, 2).reshape(BUFFER, kv_cols)
-    got_squares = got[:, query_cols + kv_width :].transpose(1, 0).reshape(BUFFER)
-    query_raw = lax.dynamic_index_in_dim(query_halves, seq_index, 0, keepdims=False) + got_query
-    kv_raw = kv_part + got_kv
-    inverse_rms = lax.rsqrt((squares + got_squares) / D + NORM_EPS)
-
-    query_pos = seq_index * local_rows + jnp.arange(local_rows, dtype=jnp.int32)
-    query_seg = lax.dynamic_slice_in_dim(segment, seq_index * local_rows, local_rows)
-    query_within = lax.dynamic_slice_in_dim(within, seq_index * local_rows, local_rows)
-    query_rms = lax.dynamic_slice_in_dim(inverse_rms, seq_index * local_rows, local_rows)
+    q_size = local_rows * query_cols
+    kv_size = window * kv_cols
+    win_at = seq_index * rest
+    query_at = seq_index * local_rows
+    query_raw = lax.dynamic_slice_in_dim(query_part, query_at, local_rows, 0) + got[
+        :q_size
+    ].reshape(local_rows, query_cols)
+    kv_raw = lax.dynamic_slice_in_dim(kv_part, win_at, window, 0) + got[
+        q_size : q_size + kv_size
+    ].reshape(window, kv_cols)
+    win_squares = lax.dynamic_slice_in_dim(squares, win_at, window) + got[q_size + kv_size :]
+    win_rms = lax.rsqrt(win_squares / D + NORM_EPS)
+    query_rms = lax.dynamic_slice_in_dim(win_rms, query_at - win_at, local_rows)
+
+    query_pos = query_at + jnp.arange(local_rows, dtype=jnp.int32)
+    query_seg = lax.dynamic_slice_in_dim(segment, query_at, local_rows)
+    query_within = lax.dynamic_slice_in_dim(within, query_at, local_rows)
     query_valid = query_seg >= 0
     queries = rotary(
         query_rms[:, None, None] * query_raw.reshape(local_rows, head_count, HD), query_within
     ).astype(jnp.bfloat16)
 
-    kv_scaled = (inverse_rms[:, None] * kv_raw).reshape(BUFFER, 2, quarter)
+    key_pos = win_at + jnp.arange(window, dtype=jnp.int32)
+    key_seg = lax.dynamic_slice_in_dim(segment, win_at, window)
+    key_within = lax.dynamic_slice_in_dim(within, win_at, window)
+    kv_scaled = (win_rms[:, None] * kv_raw).reshape(window, 2, quarter)
     freq_index = (sub % 2 * quarter + jnp.arange(quarter, dtype=jnp.int32)).astype(jnp.float32)
     inverse = jnp.power(ROPE_BASE, -2.0 * freq_index / HD)
-    angles = within.astype(jnp.float32)[:, None] * inverse[None, :]
+    angles = key_within.astype(jnp.float32)[:, None] * inverse[None, :]
     cosine = jnp.cos(angles)
     sine_part = jnp.sin(angles)
     lower_half = kv_scaled[:, 0]
@@ -168,19 +178,14 @@
         axis=1,
     )
     piece = jnp.where(sub < 2, roped, kv_scaled).astype(jnp.bfloat16)
-    shifted = [piece] + [
-        lax.ppermute(piece, "zl", perm=[(i, (i + k) % group_size) for i in range(group_size)])
-        for k in range(1, group_size)
-    ]
-    owners = (sub - jnp.arange(group_size, dtype=jnp.int32)) % group_size
-    pieces = jnp.take(jnp.stack(shifted), owners, axis=0)
-    pieces = pieces.reshape(2, 2, BUFFER, 2, quarter).transpose(0, 2, 3, 1, 4)
-    key_part = pieces[0].reshape(BUFFER, HD)
-    value_part = pieces[1].reshape(BUFFER, HD)
+    spread = jnp.broadcast_to(piece[None], (group_size,) + piece.shape)
+    pieces = lax.all_to_all(spread, "zl", split_axis=0, concat_axis=0, tiled=True)
+    pieces = pieces.reshape(2, 2, window, 2, quarter).transpose(0, 2, 3, 1, 4)
+    key_part = pieces[0].reshape(window, HD)
+    value_part = pieces[1].reshape(window, HD)
 
     score_scale = 1.0 / math.sqrt(HD)
-    key_pos = all_pos
-    allowed = (segment[None, :] == query_seg[:, None]) & query_valid[:, None] & (
+    allowed = (key_seg[None, :] == query_seg[:, None]) & query_valid[:, None] & (
         key_pos[None, :] <= query_pos[:, None]
     ) | (key_pos[None, :] == query_pos[:, None])
     scores = (

time: 170 us -> 169 us (level)
  waiting for transfers between devices: 75 us -> 85.8 us
  other arithmetic: 14 us -> 7.45 us
  starting transfers between devices: 31.6 us -> 28.6 us
  matrix products: 6.64 us -> 4.69 us
    all_to_all x1, waiting for transfers between devices: 0.01 us -> 16 us  [local(): lax.all_to_all(w_half, ('x', 'zh', 'zl'), split_axis=0, concat_axis=0, ti...]
    ppermute x3 -> x0, starting transfers between devices: 8.87 us -> none  [local(): lax.ppermute(piece, 'zl', perm=[(i, (i + k) % group_size) for i in range(...]
    ppermute x1, waiting for transfers between devices: 19.9 us -> 12.5 us  [local(): got = lax.ppermute(payload, 'seq', perm=[(0, 1), (1, 0)])]
    all_to_all x0 -> x1, waiting for transfers between devices: none -> 5.53 us  [local(): lax.all_to_all(spread, 'zl', split_axis=0, concat_axis=0, tiled=True)]
    ppermute x3 -> x0, waiting for transfers between devices: 5.03 us -> none  [local(): lax.ppermute(piece, 'zl', perm=[(i, (i + k) % group_size) for i in range(...]
    convert_element_type x2 -> x1, other arithmetic: 4.61 us -> 0.08 us  [local(): angles = key_within.astype(jnp.float32)[:, None] * inverse[None, :]]
    all_to_all x0 -> x1, starting transfers between devices: none -> 3.98 us  [local(): lax.all_to_all(spread, 'zl', split_axis=0, concat_axis=0, tiled=True)]
    all_gather x1, waiting for transfers between devices: 40.3 us -> 44 us  [local(): gathered = lax.all_gather(gathered, ('zh', 'zl'), axis=0, tiled=False)]
  transfers between devices with their start and end apart: 7 -> 5, of which waited for: 5 -> 5; matrix products, arithmetic and copies ran while one was open for 8% -> 3% of each run, Pallas kernels for 0% -> 0%
where the time goes in v4:
time: 169 us; the launch traced here: 166 us
  waiting for transfers between devices  85.8 us (51%)
  starting transfers between devices  28.6 us (17%)
  between operations  17.5 us (10%)
  blocking collectives  13.3 us (8%)
  local copies, waits for them, and re-layouts  8.61 us (5%)
  other arithmetic  7.45 us (4%)
  matrix products  4.69 us (3%)
    all_gather x1, waiting for transfers between devices, local(): gathered = lax.all_gather(gathered, ('zh', 'zl'), axis=0, tiled=False)  44 us
    all_to_all x1, waiting for transfers between devices, local(): lax.all_to_all(w_half, ('x', 'zh', 'zl'), split_axis=0, concat_axis=0, ti...  16 us
    all_gather x1, blocking collectives, local(): gathered = lax.all_gather(assembled, 'x', axis=0, tiled=False)  13.3 us
    all_to_all x1, starting transfers between devices, local(): lax.all_to_all(w_half, ('x', 'zh', 'zl'), split_axis=0, concat_axis=0, ti...  13.2 us
    ppermute x1, waiting for transfers between devices, local(): got = lax.ppermute(payload, 'seq', perm=[(0, 1), (1, 0)])  12.5 us
    all_to_all x1, waiting for transfers between devices, local(): lax.all_to_all(outgoing, 'rep', split_axis=0, concat_axis=0, tiled=True)  7.73 us
    all_to_all x1, starting transfers between devices, local(): lax.all_to_all(outgoing, 'rep', split_axis=0, concat_axis=0, tiled=True)  6.3 us
    all_to_all x1, waiting for transfers between devices, local(): lax.all_to_all(spread, 'zl', split_axis=0, concat_axis=0, tiled=True)  5.53 us
  transfers between devices with their start and end apart: 5, of which 5 were waited for; matrix products, arithmetic and copies ran while one was open for 3% of the time, Pallas kernels for 0%

profile of v4, /device:TPU:56, one launch (start us, length us, event | category | flops | bytes accessed | tf_op | source)
XLA Modules:
  0.0 165.8 jit_solution(4723861605825780930)
XLA Ops:
  6.5 0.9 copy.50
  7.5 0.8 copy.51
  8.4 0.7 select_reduce_fusion.5
  13.6 0.9 constant_dynamic-slice_fusion.2
  14.5 0.9 broadcast_select_fusion
  15.4 6.3 %all-to-all-start.1 = ((bf16[8,192,128]{2,1,0:T(8,128)(2,1)}), bf16[8,192,128]{2,1,0:T(8,128)(2,1)S(1)}, u32[]{:S(2)}, u32[]{:S(2)}) async-start(bf16[8,192,128]{2,1,0:T(8,128)(2,1)} %broadcast_select_fusion), calls=%async_computation.1 | async-start | bytes 786432 | tf_op jit(solution)/shard_map/all_to_all | solution.py:110
  21.7 1.1 constant_dynamic-slice_fusion.3
  23.1 0.9 copy.53
  23.9 7.7 %all-to-all-done.1 = bf16[8,192,128]{2,1,0:T(8,128)(2,1)S(1)} async-done(((bf16[8,192,128]{2,1,0:T(8,128)(2,1)}), bf16[8,192,128]{2,1,0:T(8,128)(2,1)S(1)}, u32[]{:S(2)}, u32[]{:S(2)}) %all-to-all-start.1) | async-done | bytes 393248 | tf_op jit(solution)/shard_map/all_to_all | solution.py:110
  31.6 13.2 %all-to-all-start = ((bf16[32,128,64]{1,2,0:T(8,128)(2,1)}), bf16[32,128,64]{1,2,0:T(8,128)(2,1)S(1)}, u32[]{:S(2)}, u32[]{:S(2)}) async-start(bf16[32,128,64]{1,2,0:T(8,128)(2,1)} %bitcast.2), calls=%async_computation | async-start | bytes 1048576 | tf_op jit(solution)/shard_map/all_to_all | solution.py:109
  44.9 0.7 fusion.40
  45.7 16.0 %all-to-all-done = bf16[32,128,64]{1,2,0:T(8,128)(2,1)S(1)} async-done(((bf16[32,128,64]{1,2,0:T(8,128)(2,1)}), bf16[32,128,64]{1,2,0:T(8,128)(2,1)S(1)}, u32[]{:S(2)}, u32[]{:S(2)}) %all-to-all-start) | async-done | bytes 524320 | tf_op jit(solution)/shard_map/all_to_all | solution.py:109
  61.7 1.4 gather_fusion
  63.4 13.3 %all_gather.10 = bf16[4,384,128]{2,1,0:T(8,128)(2,1)} all-gather(bf16[1,384,128]{2,1,0:T(8,128)(2,1)S(1)} %fusion.14), channel_id=1, replica_groups=mesh['rep'=8,'seq'=2,'x'=4,'zh'=2,'zl'=4] {'x'}, dimensions={0}, use_global_device_ids=true | all-gather | bytes 491520 | tf_op jit(solution)/shard_map/all_gather | solution.py:119
  77.2 44.0 %all-gather.3.cloned.1.call-done = bf16[32,384,128]{2,1,0:T(8,128)(2,1)} async-done(((bf16[4,384,128]{2,1,0:T(8,128)(2,1)}), bf16[32,384,128]{2,1,0:T(8,128)(2,1)}) %all-gather.3.cloned.1.call-update) | async-done | bytes 3145744 | tf_op jit(solution)/shard_map/all_gather | solution.py:120
  121.2 2.7 %multiply_reduce_fusion = f32[384]{0:T(512)S(1)} fusion(bf16[8,4,384,128]{3,2,1,0:T(8,128)(2,1)} %bitcast.64), kind=kLoop, calls=%fused_computation.4 | loop fusion | flops 4718208 | bytes 3147264 | tf_op jit(solution)/shard_map/reduce_sum | solution.py:126
  124.0 1.1 convolution_bitcast_fusion.1
  125.4 2.9 %convolution_bitcast_fusion = f32[384,256]{1,0:T(8,128)S(1)} fusion(bf16[4,8,128,256]{3,2,1,0:T(8,128)(2,1)S(1)} %bitcast.62, f32[8,4,128]{2,0,1:T(8,128)S(1)} %dynamic-slice_bitcast_fusion.1, bf16[32,384,128]{2,1,0:T(8,128)(2,1)} %all-gather.3.cloned.1.call-done), kind=kOutput, calls=%fused_computation.8 | convolution fusion | flops 810024960 | bytes 5652480 | tf_op jit(solution)/shard_map/zxri,xzic->rc/dot_general | solution.py:128
  128.4 5.1 %collective-permute-start = (f32[65792]{0:T(1024)S(1)}, f32[65792]{0:T(1024)S(1)}, u32[]{:S(2)}, u32[]{:S(2)}) collective-permute-start(f32[65792]{0:T(1024)S(1)} %pad_maximum_fusion), channel_id=1, source_target_pairs={{0,32},{32,0},{1,33},{33,1},{2,34},{34,2},{3,35},{35,3},{4,36},{36... | collective-permute-start | bytes 789512 | tf_op jit(solution)/shard_map/ppermute | solution.py:142
  133.9 12.5 %collective-permute-done = f32[65792]{0:T(1024)S(1)} collective-permute-done((f32[65792]{0:T(1024)S(1)}, f32[65792]{0:T(1024)S(1)}, u32[]{:S(2)}, u32[]{:S(2)}) %collective-permute-start) | collective-permute-done | bytes 263200 | tf_op jit(solution)/shard_map/ppermute | solution.py:142
  146.9 0.6 broadcast_in_dim.155
  147.6 4.0 %all-to-all-start.2 = ((bf16[4,256,2,32]{1,3,2,0:T(8,128)(2,1)}), bf16[4,256,2,32]{1,3,2,0:T(8,128)(2,1)S(1)}, u32[]{:S(2)}, u32[]{:S(2)}) async-start(bf16[4,256,2,32]{1,3,2,0:T(8,128)(2,1)} %broadcast_in_dim.155), calls=%async_computation.2 | async-start | bytes 262144 | tf_op jit(solution)/shard_map/all_to_all | solution.py:182
  152.0 5.5 %all-to-all-done.2 = bf16[4,256,2,32]{1,3,2,0:T(8,128)(2,1)S(1)} async-done(((bf16[4,256,2,32]{1,3,2,0:T(8,128)(2,1)}), bf16[4,256,2,32]{1,3,2,0:T(8,128)(2,1)S(1)}, u32[]{:S(2)}, u32[]{:S(2)}) %all-to-all-start.2) | async-done | bytes 131104 | tf_op jit(solution)/shard_map/all_to_all | solution.py:182
  158.3 0.7 bitcast_select_fusion
  (59 shorter events, 4.5 us)
Async XLA Ops:
  6.5 118.8 %copy-start = (bf16[4096,256]{1,0:T(8,128)(2,1)S(1)}, bf16[4096,256]{1,0:T(8,128)(2,1)}, u32[]{:S(2)}) copy-start(bf16[4096,256]{1,0:T(8,128)(2,1)} %param.8) | copy-start | bytes 6291460
  15.4 16.3 %all-to-all-start.1 = ((bf16[8,192,128]{2,1,0:T(8,128)(2,1)}), bf16[8,192,128]{2,1,0:T(8,128)(2,1)S(1)}, u32[]{:S(2)}, u32[]{:S(2)}) async-start(bf16[8,192,128]{2,1,0:T(8,128)(2,1)} %broadcast_select_fusion), calls=%async_computation.1 | async-start | bytes 786432 | tf_op jit(solution)/shard_map/all_to_all | solution.py:110
  23.0 54.0 %copy-start.2 = (f32[8192]{0:T(1024)S(1)}, f32[8192]{0:T(1024)}, u32[]{:S(2)}) copy-start(f32[8192]{0:T(1024)} %param.7) | copy-start | bytes 98308
  31.6 30.1 %all-to-all-start = ((bf16[32,128,64]{1,2,0:T(8,128)(2,1)}), bf16[32,128,64]{1,2,0:T(8,128)(2,1)S(1)}, u32[]{:S(2)}, u32[]{:S(2)}) async-start(bf16[32,128,64]{1,2,0:T(8,128)(2,1)} %bitcast.2), calls=%async_computation | async-start | bytes 1048576 | tf_op jit(solution)/shard_map/all_to_all | solution.py:109
  44.8 76.4 %all-gather.3.cloned.1.call-start = ((), (), s32[]{:S(2)}) async-start(), calls=%async_computation.3 | async-start | bytes 3538944 | tf_op jit(solution)/shard_map/all_gather | solution.py:120
  121.2 2.8 %copy-start.1 = (bf16[32,384,128]{2,1,0:T(8,128)(2,1)S(1)}, bf16[32,384,128]{2,1,0:T(8,128)(2,1)}, u32[]{:S(2)}) copy-start(bf16[32,384,128]{2,1,0:T(8,128)(2,1)} %all-gather.3.cloned.1.call-done) | copy-start | bytes 9437188
  128.4 18.0 %collective-permute-start = (f32[65792]{0:T(1024)S(1)}, f32[65792]{0:T(1024)S(1)}, u32[]{:S(2)}, u32[]{:S(2)}) collective-permute-start(f32[65792]{0:T(1024)S(1)} %pad_maximum_fusion), channel_id=1, source_target_pairs={{0,32},{32,0},{1,33},{33,1},{2,34},{34,2},{3,35},{35,3},{4,36},{36... | collective-permute-start | bytes 789512 | tf_op jit(solution)/shard_map/ppermute | solution.py:142
  147.6 9.9 %all-to-all-start.2 = ((bf16[4,256,2,32]{1,3,2,0:T(8,128)(2,1)}), bf16[4,256,2,32]{1,3,2,0:T(8,128)(2,1)S(1)}, u32[]{:S(2)}, u32[]{:S(2)}) async-start(bf16[4,256,2,32]{1,3,2,0:T(8,128)(2,1)} %broadcast_in_dim.155), calls=%async_computation.2 | async-start | bytes 262144 | tf_op jit(solution)/shard_map/all_to_all | solution.py:182
Sparse Core Ops, SparseCore 0:
  76.8 44.3 all-gather.2

commit v5 on v4

--- a/solution.py
+++ b/solution.py
@@ -108,7 +108,6 @@
     w_half = w_half.transpose(1, 2, 4, 0, 3, 5).reshape(tp_count, feature_cols, kv_cols)
     w_kv = lax.all_to_all(w_half, ("x", "zh", "zl"), split_axis=0, concat_axis=0, tiled=True)
     incoming = lax.all_to_all(outgoing, "rep", split_axis=0, concat_axis=0, tiled=True)
-    w_kv, incoming = lax.optimization_barrier((w_kv, incoming))
     w_kv = w_kv.reshape(x_count, z_count, feature_cols, kv_cols)
     all_pos = jnp.arange(BUFFER, dtype=jnp.int32)
     segment, within, source_group, pair_first, source = locate(all_pos, replica, tables)

time: 169 us -> 154 us (0.911)
  waiting for transfers between devices: 85.8 us -> 71.9 us
  starting transfers between devices: 28.6 us -> 26.6 us
  matrix products: 4.69 us -> 6.58 us
    all_to_all x1, waiting for transfers between devices: 16 us -> 0.01 us  [local(): lax.all_to_all(w_half, ('x', 'zh', 'zl'), split_axis=0, concat_axis=0, ti...]
    all_gather x1, waiting for transfers between devices: 44 us -> 41.4 us  [local(): gathered = lax.all_gather(gathered, ('zh', 'zl'), axis=0, tiled=False)]
    ppermute x1, waiting for transfers between devices: 12.5 us -> 15 us  [local(): got = lax.ppermute(payload, 'seq', perm=[(0, 1), (1, 0)])]
    all_to_all x1, waiting for transfers between devices: 7.73 us -> 9.73 us  [local(): lax.all_to_all(outgoing, 'rep', split_axis=0, concat_axis=0, tiled=True)]
    dot_general x1, matrix products: 1.11 us -> 2.99 us  [local(): jnp.einsum('zxri,xzic->rc', scaled, w_kv, preferred_element_type=jnp.floa...]
  transfers between devices with their start and end apart: 5 -> 5, of which waited for: 5 -> 4; matrix products, arithmetic and copies ran while one was open for 3% -> 4% of each run, Pallas kernels for 0% -> 0%
where the time goes in v5:
time: 154 us; the launch traced here: 151 us
  waiting for transfers between devices  71.9 us (47%)
  starting transfers between devices  26.6 us (17%)
  between operations  17.7 us (11%)
  blocking collectives  13.6 us (9%)
  local copies, waits for them, and re-layouts  8.67 us (6%)
  matrix products  6.58 us (4%)
  other arithmetic  6.14 us (4%)
    all_gather x1, waiting for transfers between devices, local(): gathered = lax.all_gather(gathered, ('zh', 'zl'), axis=0, tiled=False)  41.4 us
    ppermute x1, waiting for transfers between devices, local(): got = lax.ppermute(payload, 'seq', perm=[(0, 1), (1, 0)])  15 us
    all_gather x1, blocking collectives, local(): gathered = lax.all_gather(assembled, 'x', axis=0, tiled=False)  13.6 us
    all_to_all x1, starting transfers between devices, local(): lax.all_to_all(w_half, ('x', 'zh', 'zl'), split_axis=0, concat_axis=0, ti...  12.9 us
    all_to_all x1, waiting for transfers between devices, local(): lax.all_to_all(outgoing, 'rep', split_axis=0, concat_axis=0, tiled=True)  9.73 us
    all_to_all x1, starting transfers between devices, local(): lax.all_to_all(outgoing, 'rep', split_axis=0, concat_axis=0, tiled=True)  6.31 us
    all_to_all x1, waiting for transfers between devices, local(): lax.all_to_all(spread, 'zl', split_axis=0, concat_axis=0, tiled=True)  5.69 us
    all_to_all x1, starting transfers between devices, local(): lax.all_to_all(spread, 'zl', split_axis=0, concat_axis=0, tiled=True)  3.83 us
  transfers between devices with their start and end apart: 5, of which 4 were waited for; matrix products, arithmetic and copies ran while one was open for 4% of the time, Pallas kernels for 0%

profile of v5, /device:TPU:56, one launch (start us, length us, event | category | flops | bytes accessed | tf_op | source)
XLA Modules:
  0.0 151.2 jit_solution(8135080537909034100)
XLA Ops:
  6.5 0.9 copy.50
  7.5 0.8 copy.51
  8.7 0.7 fusion.41
  13.5 0.9 constant_dynamic-slice_fusion.3
  14.4 0.8 broadcast_select_fusion
  15.2 6.3 %all-to-all-start = ((bf16[8,192,128]{2,1,0:T(8,128)(2,1)}), bf16[8,192,128]{2,1,0:T(8,128)(2,1)S(1)}, u32[]{:S(2)}, u32[]{:S(2)}) async-start(bf16[8,192,128]{2,1,0:T(8,128)(2,1)} %broadcast_select_fusion), calls=%async_computation | async-start | bytes 786432 | tf_op jit(solution)/shard_map/all_to_all | solution.py:110
  21.8 9.7 %all-to-all-done = bf16[8,192,128]{2,1,0:T(8,128)(2,1)S(1)} async-done(((bf16[8,192,128]{2,1,0:T(8,128)(2,1)}), bf16[8,192,128]{2,1,0:T(8,128)(2,1)S(1)}, u32[]{:S(2)}, u32[]{:S(2)}) %all-to-all-start) | async-done | bytes 393248 | tf_op jit(solution)/shard_map/all_to_all | solution.py:110
  31.5 1.4 gather_fusion
  33.1 13.6 %all_gather.10 = bf16[4,384,128]{2,1,0:T(8,128)(2,1)} all-gather(bf16[1,384,128]{2,1,0:T(8,128)(2,1)S(1)} %fusion.14), channel_id=1, replica_groups=mesh['rep'=8,'seq'=2,'x'=4,'zh'=2,'zl'=4] {'x'}, dimensions={0}, use_global_device_ids=true | all-gather | bytes 491520 | tf_op jit(solution)/shard_map/all_gather | solution.py:118
  46.8 1.1 constant_dynamic-slice_fusion.1
  48.1 0.9 copy.54
  49.0 12.9 %all-to-all-start.1 = ((bf16[32,128,64]{1,2,0:T(8,128)(2,1)}), bf16[32,128,64]{1,2,0:T(8,128)(2,1)S(1)}, u32[]{:S(2)}, u32[]{:S(2)}) async-start(bf16[32,128,64]{1,2,0:T(8,128)(2,1)} %bitcast.15), calls=%async_computation.1 | async-start | bytes 1048576 | tf_op jit(solution)/shard_map/all_to_all | solution.py:109
  62.4 41.4 %all-gather.3.cloned.1.call-done = bf16[32,384,128]{2,1,0:T(8,128)(2,1)} async-done(((bf16[4,384,128]{2,1,0:T(8,128)(2,1)}), bf16[32,384,128]{2,1,0:T(8,128)(2,1)}) %all-gather.3.cloned.1.call-update) | async-done | bytes 3145744 | tf_op jit(solution)/shard_map/all_gather | solution.py:119
  103.8 2.6 %multiply_reduce_fusion = f32[384]{0:T(512)S(1)} fusion(bf16[8,4,384,128]{3,2,1,0:T(8,128)(2,1)} %bitcast.64), kind=kLoop, calls=%fused_computation.4 | loop fusion | flops 4718208 | bytes 3147264 | tf_op jit(solution)/shard_map/reduce_sum | solution.py:125
  106.5 3.0 %convolution_bitcast_fusion.1 = f32[384,64]{0,1:T(8,128)S(1)} fusion(bf16[4,8,128,64]{2,3,1,0:T(8,128)(2,1)S(1)} %bitcast.69, f32[8,4,128]{2,0,1:T(8,128)S(1)} %dynamic-slice_bitcast_fusion.1, bf16[32,384,128]{2,1,0:T(8,128)(2,1)} %all-gather.3.cloned.1.call-done), kind=kOutput, calls=%fused_computation.13 | convolution fusion | flops 206045184 | bytes 3784704 | tf_op jit(solution)/shard_map/zxri,xzic->rc/dot_general | solution.py:128
  109.7 2.9 %convolution_bitcast_fusion = f32[384,256]{1,0:T(8,128)S(1)} fusion(bf16[4,8,128,256]{3,2,1,0:T(8,128)(2,1)S(1)} %bitcast.62, f32[8,4,128]{2,0,1:T(8,128)S(1)} %dynamic-slice_bitcast_fusion.1, bf16[32,384,128]{2,1,0:T(8,128)(2,1)} %all-gather.3.cloned.1.call-done), kind=kOutput, calls=%fused_computation.8 | convolution fusion | flops 810024960 | bytes 5652480 | tf_op jit(solution)/shard_map/zxri,xzic->rc/dot_general | solution.py:127
  112.7 3.5 %collective-permute-start = (f32[65792]{0:T(1024)S(1)}, f32[65792]{0:T(1024)S(1)}, u32[]{:S(2)}, u32[]{:S(2)}) collective-permute-start(f32[65792]{0:T(1024)S(1)} %pad_maximum_fusion), channel_id=1, source_target_pairs={{0,32},{32,0},{1,33},{33,1},{2,34},{34,2},{3,35},{35,3},{4,36},{36... | collective-permute-start | bytes 789512 | tf_op jit(solution)/shard_map/ppermute | solution.py:141
  116.3 0.4 multiply_cosine_fusion
  116.8 15.0 %collective-permute-done = f32[65792]{0:T(1024)S(1)} collective-permute-done((f32[65792]{0:T(1024)S(1)}, f32[65792]{0:T(1024)S(1)}, u32[]{:S(2)}, u32[]{:S(2)}) %collective-permute-start) | collective-permute-done | bytes 263200 | tf_op jit(solution)/shard_map/ppermute | solution.py:141
  132.3 0.6 broadcast_in_dim.155
  132.9 3.8 %all-to-all-start.2 = ((bf16[4,256,2,32]{1,3,2,0:T(8,128)(2,1)}), bf16[4,256,2,32]{1,3,2,0:T(8,128)(2,1)S(1)}, u32[]{:S(2)}, u32[]{:S(2)}) async-start(bf16[4,256,2,32]{1,3,2,0:T(8,128)(2,1)} %broadcast_in_dim.155), calls=%async_computation.2 | async-start | bytes 262144 | tf_op jit(solution)/shard_map/all_to_all | solution.py:181
  137.1 5.7 %all-to-all-done.2 = bf16[4,256,2,32]{1,3,2,0:T(8,128)(2,1)S(1)} async-done(((bf16[4,256,2,32]{1,3,2,0:T(8,128)(2,1)}), bf16[4,256,2,32]{1,3,2,0:T(8,128)(2,1)S(1)}, u32[]{:S(2)}, u32[]{:S(2)}) %all-to-all-start.2) | async-done | bytes 131104 | tf_op jit(solution)/shard_map/all_to_all | solution.py:181
  142.9 0.5 fusion.42
  143.6 0.7 bitcast_select_fusion
  (57 shorter events, 3.2 us)
Async XLA Ops:
  6.5 103.2 %copy-start = (bf16[4096,256]{1,0:T(8,128)(2,1)S(1)}, bf16[4096,256]{1,0:T(8,128)(2,1)}, u32[]{:S(2)}) copy-start(bf16[4096,256]{1,0:T(8,128)(2,1)} %param.8) | copy-start | bytes 6291460
  15.2 16.3 %all-to-all-start = ((bf16[8,192,128]{2,1,0:T(8,128)(2,1)}), bf16[8,192,128]{2,1,0:T(8,128)(2,1)S(1)}, u32[]{:S(2)}, u32[]{:S(2)}) async-start(bf16[8,192,128]{2,1,0:T(8,128)(2,1)} %broadcast_select_fusion), calls=%async_computation | async-start | bytes 786432 | tf_op jit(solution)/shard_map/all_to_all | solution.py:110
  21.5 82.3 %all-gather.3.cloned.1.call-start = ((), (), s32[]{:S(2)}) async-start(), calls=%async_computation.3 | async-start | bytes 3538944 | tf_op jit(solution)/shard_map/all_gather | solution.py:119
  21.7 40.6 %copy-start.1 = (f32[8192]{0:T(1024)S(1)}, f32[8192]{0:T(1024)}, u32[]{:S(2)}) copy-start(f32[8192]{0:T(1024)} %param.7) | copy-start | bytes 98308
  49.0 57.5 %all-to-all-start.1 = ((bf16[32,128,64]{1,2,0:T(8,128)(2,1)}), bf16[32,128,64]{1,2,0:T(8,128)(2,1)S(1)}, u32[]{:S(2)}, u32[]{:S(2)}) async-start(bf16[32,128,64]{1,2,0:T(8,128)(2,1)} %bitcast.15), calls=%async_computation.1 | async-start | bytes 1048576 | tf_op jit(solution)/shard_map/all_to_all | solution.py:109
  112.7 19.0 %collective-permute-start = (f32[65792]{0:T(1024)S(1)}, f32[65792]{0:T(1024)S(1)}, u32[]{:S(2)}, u32[]{:S(2)}) collective-permute-start(f32[65792]{0:T(1024)S(1)} %pad_maximum_fusion), channel_id=1, source_target_pairs={{0,32},{32,0},{1,33},{33,1},{2,34},{34,2},{3,35},{35,3},{4,36},{36... | collective-permute-start | bytes 789512 | tf_op jit(solution)/shard_map/ppermute | solution.py:141
  132.9 9.9 %all-to-all-start.2 = ((bf16[4,256,2,32]{1,3,2,0:T(8,128)(2,1)}), bf16[4,256,2,32]{1,3,2,0:T(8,128)(2,1)S(1)}, u32[]{:S(2)}, u32[]{:S(2)}) async-start(bf16[4,256,2,32]{1,3,2,0:T(8,128)(2,1)} %broadcast_in_dim.155), calls=%async_computation.2 | async-start | bytes 262144 | tf_op jit(solution)/shard_map/all_to_all | solution.py:181
Sparse Core Ops, SparseCore 0:
  46.9 56.9 all-gather.2

commit v6 on v5

--- a/solution.py
+++ b/solution.py
@@ -93,15 +93,13 @@
     kv_cols = 2 * HD // group_size
     quarter = HD // 4
 
-    tables = response_tables(lengths, routes)
-    flat_len, flat_route, group_of, dest_off, pair_off, src_start = tables
-    my_route = lax.dynamic_slice_in_dim(flat_route, replica * RESP, RESP)
-    my_start = lax.dynamic_slice_in_dim(src_start, replica * RESP, RESP)
-    first_block = lax.dynamic_slice_in_dim(hidden, my_start[0], LMAX, 0)
-    second_block = lax.dynamic_slice_in_dim(hidden, my_start[1], LMAX, 0)
+    my_lengths = lax.dynamic_index_in_dim(lengths, replica, 0, keepdims=False)
+    my_routes = lax.dynamic_index_in_dim(routes, replica, 0, keepdims=False)
+    first_block = hidden[:LMAX]
+    second_block = lax.dynamic_slice_in_dim(hidden, my_lengths[0], LMAX, 0)
     targets = jnp.arange(rep_count, dtype=jnp.int32)
     outgoing = jnp.where(
-        (targets == my_route[0])[:, None, None], first_block[None], second_block[None]
+        (targets == my_routes[0])[:, None, None], first_block[None], second_block[None]
     ).reshape(rep_count * LMAX, feature_cols)
     w_half = lax.dynamic_index_in_dim(w_keyval, seq_index, 0, keepdims=False)
     w_half = w_half.reshape(feature_cols, KVH, 2, 2, 2, quarter)
@@ -109,13 +107,15 @@
     w_kv = lax.all_to_all(w_half, ("x", "zh", "zl"), split_axis=0, concat_axis=0, tiled=True)
     incoming = lax.all_to_all(outgoing, "rep", split_axis=0, concat_axis=0, tiled=True)
     w_kv = w_kv.reshape(x_count, z_count, feature_cols, kv_cols)
+    tables = response_tables(lengths, routes)
     all_pos = jnp.arange(BUFFER, dtype=jnp.int32)
     segment, within, source_group, pair_first, source = locate(all_pos, replica, tables)
     valid = segment >= 0
     gathered_idx = jnp.where(valid, source_group * LMAX + all_pos - pair_first, 0)
     assembled = fill_rows(incoming, gathered_idx, valid)
 
-    gathered = lax.all_gather(assembled, "x", axis=0, tiled=False)
+    spread = jnp.broadcast_to(assembled[None], (x_count,) + assembled.shape)
+    gathered = lax.all_to_all(spread, "x", split_axis=0, concat_axis=0, tiled=True)
     gathered = lax.all_gather(gathered, ("zh", "zl"), axis=0, tiled=False)
     gain_half = lax.dynamic_index_in_dim(
         gain.reshape(seq_count, x_count, z_count, feature_cols), seq_index, 0, keepdims=False

time: 154 us -> 150 us (0.974)
  between operations: 17.7 us -> 15.7 us
  waiting for transfers between devices: 71.9 us -> 70.3 us
    all_gather x1 -> x0, blocking collectives: 13.6 us -> none  [local(): gathered = lax.all_gather(assembled, 'x', axis=0, tiled=False)]
    all_to_all x0 -> x1, blocking collectives: none -> 12.5 us  [local(): lax.all_to_all(spread, 'x', split_axis=0, concat_axis=0, tiled=True)]
    all_to_all x1, waiting for transfers between devices: 9.73 us -> 7.88 us  [local(): lax.all_to_all(outgoing, 'rep', split_axis=0, concat_axis=0, tiled=True)]
    all_to_all x1, starting transfers between devices: 12.9 us -> 11.3 us  [local(): lax.all_to_all(w_half, ('x', 'zh', 'zl'), split_axis=0, concat_axis=0, ti...]
  transfers between devices with their start and end apart: 5 -> 5, of which waited for: 4 -> 4; matrix products, arithmetic and copies ran while one was open for 4% -> 6% of each run, Pallas kernels for 0% -> 0%
where the time goes in v6:
time: 150 us; the launch traced here: 148 us
  waiting for transfers between devices  70.3 us (47%)
  starting transfers between devices  26.2 us (17%)
  between operations  15.7 us (10%)
  blocking collectives  12.5 us (8%)
  local copies, waits for them, and re-layouts  9.69 us (6%)
  other arithmetic  6.72 us (4%)
  matrix products  6.57 us (4%)
    all_gather x1, waiting for transfers between devices, local(): gathered = lax.all_gather(gathered, ('zh', 'zl'), axis=0, tiled=False)  42.8 us
    ppermute x1, waiting for transfers between devices, local(): got = lax.ppermute(payload, 'seq', perm=[(0, 1), (1, 0)])  13.9 us
    all_to_all x1, blocking collectives, local(): lax.all_to_all(spread, 'x', split_axis=0, concat_axis=0, tiled=True)  12.5 us
    all_to_all x1, starting transfers between devices, local(): lax.all_to_all(w_half, ('x', 'zh', 'zl'), split_axis=0, concat_axis=0, ti...  11.3 us
    all_to_all x1, waiting for transfers between devices, local(): lax.all_to_all(outgoing, 'rep', split_axis=0, concat_axis=0, tiled=True)  7.88 us
    all_to_all x1, starting transfers between devices, local(): lax.all_to_all(outgoing, 'rep', split_axis=0, concat_axis=0, tiled=True)  6.31 us
    all_to_all x1, waiting for transfers between devices, local(): lax.all_to_all(spread, 'zl', split_axis=0, concat_axis=0, tiled=True)  5.69 us
    all_to_all x1, starting transfers between devices, local(): lax.all_to_all(spread, 'zl', split_axis=0, concat_axis=0, tiled=True)  5.02 us
  transfers between devices with their start and end apart: 5, of which 4 were waited for; matrix products, arithmetic and copies ran while one was open for 6% of the time, Pallas kernels for 0%

profile of v6, /device:TPU:56, one launch (start us, length us, event | category | flops | bytes accessed | tf_op | source)
XLA Modules:
  0.0 147.7 jit_solution(6518081476527717430)
XLA Ops:
  6.5 0.9 constant_dynamic-slice_fusion.3
  7.5 0.5 slice.56
  8.0 0.6 iota_compare_fusion.3
  11.1 0.9 fusion.48
  12.0 0.8 broadcast_select_fusion
  12.8 6.3 %all-to-all-start = ((bf16[8,192,128]{2,1,0:T(8,128)(2,1)}), bf16[8,192,128]{2,1,0:T(8,128)(2,1)S(1)}, u32[]{:S(2)}, u32[]{:S(2)}) async-start(bf16[8,192,128]{2,1,0:T(8,128)(2,1)} %broadcast_select_fusion), calls=%async_computation | async-start | bytes 786432 | tf_op jit(solution)/shard_map/all_to_all | solution.py:108
  19.1 0.8 copy.69
  19.9 0.8 copy.68
  21.2 7.9 %all-to-all-done = bf16[8,192,128]{2,1,0:T(8,128)(2,1)S(1)} async-done(((bf16[8,192,128]{2,1,0:T(8,128)(2,1)}), bf16[8,192,128]{2,1,0:T(8,128)(2,1)S(1)}, u32[]{:S(2)}, u32[]{:S(2)}) %all-to-all-start) | async-done | bytes 393248 | tf_op jit(solution)/shard_map/all_to_all | solution.py:108
  29.1 1.4 gather_fusion
  30.8 12.5 %all_to_all.24 = bf16[4,384,128]{2,1,0:T(8,128)(2,1)} all-to-all(bf16[4,384,128]{2,1,0:T(8,128)(2,1)S(1)} %broadcast_in_dim.157), channel_id=1, replica_groups=mesh['rep'=8,'seq'=2,'x'=4,'zh'=2,'zl'=4] {'x'}, dimensions={0} | all-to-all | bytes 786432 | tf_op jit(solution)/shard_map/all_to_all | solution.py:118
  43.3 1.1 constant_dynamic-slice_fusion.1
  44.7 0.9 copy.73
  45.5 11.3 %all-to-all-start.2 = ((bf16[32,128,64]{1,2,0:T(8,128)(2,1)}), bf16[32,128,64]{1,2,0:T(8,128)(2,1)S(1)}, u32[]{:S(2)}, u32[]{:S(2)}) async-start(bf16[32,128,64]{1,2,0:T(8,128)(2,1)} %bitcast.13), calls=%async_computation.2 | async-start | bytes 1048576 | tf_op jit(solution)/shard_map/all_to_all | solution.py:107
  57.4 42.8 %all-gather.3.cloned.1.call-done = bf16[32,384,128]{2,1,0:T(8,128)(2,1)} async-done(((bf16[4,384,128]{2,1,0:T(8,128)(2,1)}), bf16[32,384,128]{2,1,0:T(8,128)(2,1)}) %all-gather.3.cloned.1.call-update) | async-done | bytes 3145744 | tf_op jit(solution)/shard_map/all_gather | solution.py:119
  100.2 2.6 %fusion.1 = f32[384]{0:T(512)S(1)} fusion(bf16[8,4,384,128]{3,2,1,0:T(8,128)(2,1)} %bitcast.58), kind=kLoop, calls=%fused_computation.4 | loop fusion | flops 4718208 | bytes 3147264 | tf_op jit(solution)/shard_map/reduce_sum | solution.py:125
  102.9 3.0 %fusion.15 = f32[384,64]{0,1:T(8,128)S(1)} fusion(bf16[4,8,128,64]{2,3,1,0:T(8,128)(2,1)S(1)} %bitcast.63, f32[8,4,128]{2,1,0:T(4,128)S(1)} %copy.70, bf16[32,384,128]{2,1,0:T(8,128)(2,1)} %all-gather.3.cloned.1.call-done), kind=kOutput, calls=%fused_computation.18 | convolution fusion | flops 206045184 | bytes 3784704 | tf_op jit(solution)/shard_map/zxri,xzic->rc/dot_general | solution.py:128
  106.1 2.9 %fusion.9 = f32[384,256]{1,0:T(8,128)S(1)} fusion(bf16[4,8,128,256]{3,2,1,0:T(8,128)(2,1)S(1)} %bitcast.56, f32[8,4,128]{2,1,0:T(4,128)S(1)} %copy.70, bf16[32,384,128]{2,1,0:T(8,128)(2,1)} %all-gather.3.cloned.1.call-done), kind=kOutput, calls=%fused_computation.12 | convolution fusion | flops 810024960 | bytes 5652480 | tf_op jit(solution)/shard_map/zxri,xzic->rc/dot_general | solution.py:127
  109.1 3.5 %collective-permute-start = (f32[65792]{0:T(1024)S(1)}, f32[65792]{0:T(1024)S(1)}, u32[]{:S(2)}, u32[]{:S(2)}) collective-permute-start(f32[65792]{0:T(1024)S(1)} %pad_maximum_fusion), channel_id=1, source_target_pairs={{0,32},{32,0},{1,33},{33,1},{2,34},{34,2},{3,35},{35,3},{4,36},{36... | collective-permute-start | bytes 789512 | tf_op jit(solution)/shard_map/ppermute | solution.py:141
  113.2 13.9 %collective-permute-done = f32[65792]{0:T(1024)S(1)} collective-permute-done((f32[65792]{0:T(1024)S(1)}, f32[65792]{0:T(1024)S(1)}, u32[]{:S(2)}, u32[]{:S(2)}) %collective-permute-start) | collective-permute-done | bytes 263200 | tf_op jit(solution)/shard_map/ppermute | solution.py:141
  127.6 0.6 broadcast_in_dim.158
  128.3 5.0 %all-to-all-start.3 = ((bf16[4,256,2,32]{1,3,2,0:T(8,128)(2,1)}), bf16[4,256,2,32]{1,3,2,0:T(8,128)(2,1)S(1)}, u32[]{:S(2)}, u32[]{:S(2)}) async-start(bf16[4,256,2,32]{1,3,2,0:T(8,128)(2,1)} %broadcast_in_dim.158), calls=%async_computation.3 | async-start | bytes 262144 | tf_op jit(solution)/shard_map/all_to_all | solution.py:181
  133.7 5.7 %all-to-all-done.3 = bf16[4,256,2,32]{1,3,2,0:T(8,128)(2,1)S(1)} async-done(((bf16[4,256,2,32]{1,3,2,0:T(8,128)(2,1)}), bf16[4,256,2,32]{1,3,2,0:T(8,128)(2,1)S(1)}, u32[]{:S(2)}, u32[]{:S(2)}) %all-to-all-start.3) | async-done | bytes 131104 | tf_op jit(solution)/shard_map/all_to_all | solution.py:181
  140.1 0.7 bitcast_select_fusion
  (59 shorter events, 4.5 us)
Async XLA Ops:
  6.5 99.6 %copy-start = (bf16[4096,256]{1,0:T(8,128)(2,1)S(1)}, bf16[4096,256]{1,0:T(8,128)(2,1)}, u32[]{:S(2)}) copy-start(bf16[4096,256]{1,0:T(8,128)(2,1)} %param.8) | copy-start | bytes 6291460
  12.8 16.3 %all-to-all-start = ((bf16[8,192,128]{2,1,0:T(8,128)(2,1)}), bf16[8,192,128]{2,1,0:T(8,128)(2,1)S(1)}, u32[]{:S(2)}, u32[]{:S(2)}) async-start(bf16[8,192,128]{2,1,0:T(8,128)(2,1)} %broadcast_select_fusion), calls=%async_computation | async-start | bytes 786432 | tf_op jit(solution)/shard_map/all_to_all | solution.py:108
  19.1 81.1 %all-gather.3.cloned.1.call-start = ((), (), s32[]{:S(2)}) async-start(), calls=%async_computation.4 | async-start | bytes 3538944 | tf_op jit(solution)/shard_map/all_gather | solution.py:119
  30.5 26.3 %copy-start.1 = (f32[8192]{0:T(1024)S(1)}, f32[8192]{0:T(1024)}, u32[]{:S(2)}) copy-start(f32[8192]{0:T(1024)} %param.7) | copy-start | bytes 98308
  45.5 57.3 %all-to-all-start.2 = ((bf16[32,128,64]{1,2,0:T(8,128)(2,1)}), bf16[32,128,64]{1,2,0:T(8,128)(2,1)S(1)}, u32[]{:S(2)}, u32[]{:S(2)}) async-start(bf16[32,128,64]{1,2,0:T(8,128)(2,1)} %bitcast.13), calls=%async_computation.2 | async-start | bytes 1048576 | tf_op jit(solution)/shard_map/all_to_all | solution.py:107
  109.1 18.0 %collective-permute-start = (f32[65792]{0:T(1024)S(1)}, f32[65792]{0:T(1024)S(1)}, u32[]{:S(2)}, u32[]{:S(2)}) collective-permute-start(f32[65792]{0:T(1024)S(1)} %pad_maximum_fusion), channel_id=1, source_target_pairs={{0,32},{32,0},{1,33},{33,1},{2,34},{34,2},{3,35},{35,3},{4,36},{36... | collective-permute-start | bytes 789512 | tf_op jit(solution)/shard_map/ppermute | solution.py:141
  128.3 11.1 %all-to-all-start.3 = ((bf16[4,256,2,32]{1,3,2,0:T(8,128)(2,1)}), bf16[4,256,2,32]{1,3,2,0:T(8,128)(2,1)S(1)}, u32[]{:S(2)}, u32[]{:S(2)}) async-start(bf16[4,256,2,32]{1,3,2,0:T(8,128)(2,1)} %broadcast_in_dim.158), calls=%async_computation.3 | async-start | bytes 262144 | tf_op jit(solution)/shard_map/all_to_all | solution.py:181
Sparse Core Ops, SparseCore 0:
  43.4 56.7 all-gather.2

commit v7 on v6

--- a/solution.py
+++ b/solution.py
@@ -124,8 +124,14 @@
     scaled = (gathered_f * gain_half.transpose(1, 0, 2)[:, :, None, :]).astype(jnp.bfloat16)
     squares = jnp.sum(gathered_f * gathered_f, axis=(0, 1, 3))
     w_q = w_query.reshape(x_count, z_count, feature_cols, w_query.shape[1])
-    query_part = jnp.einsum("zxri,xzic->rc", scaled, w_q, preferred_element_type=jnp.float32)
-    kv_part = jnp.einsum("zxri,xzic->rc", scaled, w_kv, preferred_element_type=jnp.float32)
+    both = jnp.einsum(
+        "zxri,xzic->rc",
+        scaled,
+        jnp.concatenate([w_q, w_kv], axis=3),
+        preferred_element_type=jnp.float32,
+    )
+    query_part = both[:, : w_q.shape[3]]
+    kv_part = both[:, w_q.shape[3] :]
 
     window = BUFFER - LMIN
     rest = BUFFER - window

time: 150 us -> 152 us (1.013)
  local copies, waits for them, and re-layouts: 9.69 us -> 15.3 us
  waiting for transfers between devices: 70.3 us -> 67.9 us
  matrix products: 6.57 us -> 4.96 us
    all_gather x1, waiting for transfers between devices: 42.8 us -> 22 us  [local(): gathered = lax.all_gather(gathered, ('zh', 'zl'), axis=0, tiled=False)]
    all_to_all x1, waiting for transfers between devices: 0.01 us -> 18.3 us  [local(): lax.all_to_all(w_half, ('x', 'zh', 'zl'), split_axis=0, concat_axis=0, ti...]
    reshape x0 -> x2, local copies, waits for them, and re-layouts: none -> 2.57 us  [the longest x1 2.45 us: local(): w_q = w_query.reshape(x_count, z_count, feature_cols, w_query.shape[1])]
    unnamed x9 -> x10, local copies, waits for them, and re-layouts: 1.91 us -> 3.66 us
    dot_general x2 -> x1, matrix products: 5.85 us -> 4.24 us  [local(): jnp.einsum('zxri,xzic->rc', scaled, jnp.concatenate([w_q, w_kv], axis=3),...]
  transfers between devices with their start and end apart: 5 -> 5, of which waited for: 4 -> 5; matrix products, arithmetic and copies ran while one was open for 6% -> 7% of each run, Pallas kernels for 0% -> 0%
where the time goes in v7:
time: 152 us; the launch traced here: 150 us
  waiting for transfers between devices  67.9 us (45%)
  starting transfers between devices  26.3 us (17%)
  between operations  15.9 us (10%)
  local copies, waits for them, and re-layouts  15.3 us (10%)
  blocking collectives  12.6 us (8%)
  other arithmetic  6.86 us (5%)
  matrix products  4.96 us (3%)
    all_gather x1, waiting for transfers between devices, local(): gathered = lax.all_gather(gathered, ('zh', 'zl'), axis=0, tiled=False)  22 us
    all_to_all x1, waiting for transfers between devices, local(): lax.all_to_all(w_half, ('x', 'zh', 'zl'), split_axis=0, concat_axis=0, ti...  18.3 us
    ppermute x1, waiting for transfers between devices, local(): got = lax.ppermute(payload, 'seq', perm=[(0, 1), (1, 0)])  14 us
    all_to_all x1, blocking collectives, local(): lax.all_to_all(spread, 'x', split_axis=0, concat_axis=0, tiled=True)  12.6 us
    all_to_all x1, starting transfers between devices, local(): lax.all_to_all(w_half, ('x', 'zh', 'zl'), split_axis=0, concat_axis=0, ti...  11.4 us
    all_to_all x1, waiting for transfers between devices, local(): lax.all_to_all(outgoing, 'rep', split_axis=0, concat_axis=0, tiled=True)  7.88 us
    all_to_all x1, starting transfers between devices, local(): lax.all_to_all(outgoing, 'rep', split_axis=0, concat_axis=0, tiled=True)  6.31 us
    all_to_all x1, waiting for transfers between devices, local(): lax.all_to_all(spread, 'zl', split_axis=0, concat_axis=0, tiled=True)  5.85 us
  transfers between devices with their start and end apart: 5, of which 5 were waited for; matrix products, arithmetic and copies ran while one was open for 7% of the time, Pallas kernels for 0%

profile of v7, /device:TPU:56, one launch (start us, length us, event | category | flops | bytes accessed | tf_op | source)
XLA Modules:
  0.0 149.8 jit_solution(8393441225412854043)
XLA Ops:
  6.5 0.9 constant_dynamic-slice_fusion.4
  9.9 0.6 iota_compare_fusion.3
  11.2 0.9 fusion.49
  12.1 0.8 broadcast_select_fusion
  13.0 6.3 %all-to-all-start = ((bf16[8,192,128]{2,1,0:T(8,128)(2,1)}), bf16[8,192,128]{2,1,0:T(8,128)(2,1)S(1)}, u32[]{:S(2)}, u32[]{:S(2)}) async-start(bf16[8,192,128]{2,1,0:T(8,128)(2,1)} %broadcast_select_fusion), calls=%async_computation | async-start | bytes 786432 | tf_op jit(solution)/shard_map/all_to_all | solution.py:108
  19.3 0.8 copy.77
  20.0 0.8 copy.76
  21.4 7.9 %all-to-all-done = bf16[8,192,128]{2,1,0:T(8,128)(2,1)S(1)} async-done(((bf16[8,192,128]{2,1,0:T(8,128)(2,1)}), bf16[8,192,128]{2,1,0:T(8,128)(2,1)S(1)}, u32[]{:S(2)}, u32[]{:S(2)}) %all-to-all-start) | async-done | bytes 393248 | tf_op jit(solution)/shard_map/all_to_all | solution.py:108
  29.2 1.4 gather_fusion
  30.9 12.6 %all_to_all.24 = bf16[4,384,128]{2,1,0:T(8,128)(2,1)} all-to-all(bf16[4,384,128]{2,1,0:T(8,128)(2,1)S(1)} %broadcast_in_dim.157), channel_id=1, replica_groups=mesh['rep'=8,'seq'=2,'x'=4,'zh'=2,'zl'=4] {'x'}, dimensions={0} | all-to-all | bytes 786432 | tf_op jit(solution)/shard_map/all_to_all | solution.py:118
  43.6 0.9 constant_dynamic-slice_fusion.2
  44.5 2.0 %copy.98 = bf16[1,128,2048]{1,2,0:T(8,128)(2,1)} copy(bf16[1,128,2048]{2,1,0:T(8,128)(2,1)} %constant_dynamic-slice_fusion.2) | data formatting | bytes 1048576
  46.5 1.9 %copy.80 = bf16[8,2,2,128,2,32]{3,5,4,2,1,0:T(8,128)(2,1)} copy(bf16[8,2,2,128,2,32]{3,5,2,4,1,0:T(8,128)(2,1)} %bitcast.47) | data formatting | bytes 1048576 | tf_op jit(solution)/shard_map/transpose | solution.py:106
  48.4 11.4 %all-to-all-start.2 = ((bf16[32,128,64]{1,2,0:T(8,128)(2,1)}), bf16[32,128,64]{1,2,0:T(8,128)(2,1)}, u32[]{:S(2)}, u32[]{:S(2)}) async-start(bf16[32,128,64]{1,2,0:T(8,128)(2,1)} %bitcast.46), calls=%async_computation.2 | async-start | bytes 1048576 | tf_op jit(solution)/shard_map/all_to_all | solution.py:107
  60.0 2.4 %copy.81 = bf16[4,8,128,256]{2,3,1,0:T(8,128)(2,1)} copy(bf16[4,8,128,256]{3,2,1,0:T(8,128)(2,1)S(1)} %bitcast.45) | data formatting | bytes 4194304 | tf_op jit(solution)/shard_map/reshape | solution.py:126
  62.9 18.3 %all-to-all-done.2 = bf16[32,128,64]{1,2,0:T(8,128)(2,1)} async-done(((bf16[32,128,64]{1,2,0:T(8,128)(2,1)}), bf16[32,128,64]{1,2,0:T(8,128)(2,1)}, u32[]{:S(2)}, u32[]{:S(2)}) %all-to-all-start.2) | async-done | bytes 524320 | tf_op jit(solution)/shard_map/all_to_all | solution.py:107
  81.2 22.0 %all-gather.3.cloned.1.call-done = bf16[32,384,128]{2,1,0:T(8,128)(2,1)} async-done(((bf16[4,384,128]{2,1,0:T(8,128)(2,1)}), bf16[32,384,128]{2,1,0:T(8,128)(2,1)}) %all-gather.3.cloned.1.call-update) | async-done | bytes 3145744 | tf_op jit(solution)/shard_map/all_gather | solution.py:119
  103.1 4.2 %fusion.9 = f32[384,320]{0,1:T(8,128)S(1)} fusion(bf16[4,8,128,64]{2,3,1,0:T(8,128)(2,1)} %bitcast.12, bf16[4,8,128,256]{2,3,1,0:T(8,128)(2,1)} %copy.81, f32[8,4,128]{2,1,0:T(4,128)S(1)} %copy.78, bf16[32,384,128]{2,1,0:T(8,128)(2,1)} %all-gather.3.cloned.1.call-done), kind=kOutput, calls=%fused_computation.12 | convolution fusion | flops 1016594432 | bytes 6275072 | tf_op jit(solution)/shard_map/zxri,xzic->rc/dot_general | solution.py:127
  108.0 2.6 %fusion.1 = f32[384]{0:T(512)S(1)} fusion(bf16[8,4,384,128]{3,2,1,0:T(8,128)(2,1)} %bitcast.44), kind=kLoop, calls=%fused_computation.4 | loop fusion | flops 4718208 | bytes 3147264 | tf_op jit(solution)/shard_map/reduce_sum | solution.py:125
  110.7 3.5 %collective-permute-start = (f32[65792]{0:T(1024)S(1)}, f32[65792]{0:T(1024)S(1)}, u32[]{:S(2)}, u32[]{:S(2)}) collective-permute-start(f32[65792]{0:T(1024)S(1)} %pad_maximum_fusion), channel_id=1, source_target_pairs={{0,32},{32,0},{1,33},{33,1},{2,34},{34,2},{3,35},{35,3},{4,36},{36... | collective-permute-start | bytes 789512 | tf_op jit(solution)/shard_map/ppermute | solution.py:147
  114.7 14.0 %collective-permute-done = f32[65792]{0:T(1024)S(1)} collective-permute-done((f32[65792]{0:T(1024)S(1)}, f32[65792]{0:T(1024)S(1)}, u32[]{:S(2)}, u32[]{:S(2)}) %collective-permute-start) | collective-permute-done | bytes 263200 | tf_op jit(solution)/shard_map/ppermute | solution.py:147
  130.4 5.0 %all-to-all-start.3 = ((bf16[4,256,2,32]{1,3,2,0:T(8,128)(2,1)}), bf16[4,256,2,32]{1,3,2,0:T(8,128)(2,1)S(1)}, u32[]{:S(2)}, u32[]{:S(2)}) async-start(bf16[4,256,2,32]{1,3,2,0:T(8,128)(2,1)} %broadcast_in_dim.158), calls=%async_computation.3 | async-start | bytes 262144 | tf_op jit(solution)/shard_map/all_to_all | solution.py:187
  135.6 5.8 %all-to-all-done.3 = bf16[4,256,2,32]{1,3,2,0:T(8,128)(2,1)S(1)} async-done(((bf16[4,256,2,32]{1,3,2,0:T(8,128)(2,1)}), bf16[4,256,2,32]{1,3,2,0:T(8,128)(2,1)S(1)}, u32[]{:S(2)}, u32[]{:S(2)}) %all-to-all-start.3) | async-done | bytes 131104 | tf_op jit(solution)/shard_map/all_to_all | solution.py:187
  142.2 0.7 bitcast_select_fusion
  (67 shorter events, 6.1 us)
Async XLA Ops:
  6.5 37.1 %copy-start = (bf16[2,128,2048]{2,1,0:T(8,128)(2,1)S(1)}, bf16[2,128,2048]{2,1,0:T(8,128)(2,1)}, u32[]{:S(2)}) copy-start(bf16[2,128,2048]{2,1,0:T(8,128)(2,1)} %param.9) | copy-start | bytes 3145732
  13.0 16.3 %all-to-all-start = ((bf16[8,192,128]{2,1,0:T(8,128)(2,1)}), bf16[8,192,128]{2,1,0:T(8,128)(2,1)S(1)}, u32[]{:S(2)}, u32[]{:S(2)}) async-start(bf16[8,192,128]{2,1,0:T(8,128)(2,1)} %broadcast_select_fusion), calls=%async_computation | async-start | bytes 786432 | tf_op jit(solution)/shard_map/all_to_all | solution.py:108
  19.3 83.8 %all-gather.3.cloned.1.call-start = ((), (), s32[]{:S(2)}) async-start(), calls=%async_computation.4 | async-start | bytes 3538944 | tf_op jit(solution)/shard_map/all_gather | solution.py:119
  30.7 29.2 %copy-start.2 = (f32[8192]{0:T(1024)S(1)}, f32[8192]{0:T(1024)}, u32[]{:S(2)}) copy-start(f32[8192]{0:T(1024)} %param.7) | copy-start | bytes 98308
  30.7 29.2 %copy-start.1 = (bf16[4096,256]{1,0:T(8,128)(2,1)S(1)}, bf16[4096,256]{1,0:T(8,128)(2,1)}, u32[]{:S(2)}) copy-start(bf16[4096,256]{1,0:T(8,128)(2,1)} %param.8) | copy-start | bytes 6291460
  48.4 32.7 %all-to-all-start.2 = ((bf16[32,128,64]{1,2,0:T(8,128)(2,1)}), bf16[32,128,64]{1,2,0:T(8,128)(2,1)}, u32[]{:S(2)}, u32[]{:S(2)}) async-start(bf16[32,128,64]{1,2,0:T(8,128)(2,1)} %bitcast.46), calls=%async_computation.2 | async-start | bytes 1048576 | tf_op jit(solution)/shard_map/all_to_all | solution.py:107
  110.7 18.0 %collective-permute-start = (f32[65792]{0:T(1024)S(1)}, f32[65792]{0:T(1024)S(1)}, u32[]{:S(2)}, u32[]{:S(2)}) collective-permute-start(f32[65792]{0:T(1024)S(1)} %pad_maximum_fusion), channel_id=1, source_target_pairs={{0,32},{32,0},{1,33},{33,1},{2,34},{34,2},{3,35},{35,3},{4,36},{36... | collective-permute-start | bytes 789512 | tf_op jit(solution)/shard_map/ppermute | solution.py:147
  130.4 11.1 %all-to-all-start.3 = ((bf16[4,256,2,32]{1,3,2,0:T(8,128)(2,1)}), bf16[4,256,2,32]{1,3,2,0:T(8,128)(2,1)S(1)}, u32[]{:S(2)}, u32[]{:S(2)}) async-start(bf16[4,256,2,32]{1,3,2,0:T(8,128)(2,1)} %broadcast_in_dim.158), calls=%async_computation.3 | async-start | bytes 262144 | tf_op jit(solution)/shard_map/all_to_all | solution.py:187
Sparse Core Ops, SparseCore 0:
  43.7 59.3 all-gather.2

commit v8 on v6

--- a/solution.py
+++ b/solution.py
@@ -101,12 +101,7 @@
     outgoing = jnp.where(
         (targets == my_routes[0])[:, None, None], first_block[None], second_block[None]
     ).reshape(rep_count * LMAX, feature_cols)
-    w_half = lax.dynamic_index_in_dim(w_keyval, seq_index, 0, keepdims=False)
-    w_half = w_half.reshape(feature_cols, KVH, 2, 2, 2, quarter)
-    w_half = w_half.transpose(1, 2, 4, 0, 3, 5).reshape(tp_count, feature_cols, kv_cols)
-    w_kv = lax.all_to_all(w_half, ("x", "zh", "zl"), split_axis=0, concat_axis=0, tiled=True)
     incoming = lax.all_to_all(outgoing, "rep", split_axis=0, concat_axis=0, tiled=True)
-    w_kv = w_kv.reshape(x_count, z_count, feature_cols, kv_cols)
     tables = response_tables(lengths, routes)
     all_pos = jnp.arange(BUFFER, dtype=jnp.int32)
     segment, within, source_group, pair_first, source = locate(all_pos, replica, tables)
@@ -125,31 +120,35 @@
     squares = jnp.sum(gathered_f * gathered_f, axis=(0, 1, 3))
     w_q = w_query.reshape(x_count, z_count, feature_cols, w_query.shape[1])
     query_part = jnp.einsum("zxri,xzic->rc", scaled, w_q, preferred_element_type=jnp.float32)
-    kv_part = jnp.einsum("zxri,xzic->rc", scaled, w_kv, preferred_element_type=jnp.float32)
 
     window = BUFFER - LMIN
     rest = BUFFER - window
     partner = seq_count - 1 - seq_index
     query_cols = query_part.shape[1]
+    win_at = seq_index * rest
+    query_at = seq_index * local_rows
     payload = jnp.concatenate(
         [
-            lax.dynamic_slice_in_dim(query_part, partner * local_rows, local_rows, 0).reshape(-1),
-            lax.dynamic_slice_in_dim(kv_part, partner * rest, window, 0).reshape(-1),
-            lax.dynamic_slice_in_dim(squares, partner * rest, window),
-        ]
+            lax.dynamic_slice_in_dim(query_part, partner * local_rows, local_rows, 0),
+            lax.dynamic_slice_in_dim(squares, partner * rest, window).reshape(-1, query_cols),
+        ],
+        axis=0,
     )
     got = lax.ppermute(payload, "seq", perm=[(0, 1), (1, 0)])
-    q_size = local_rows * query_cols
-    kv_size = window * kv_cols
-    win_at = seq_index * rest
-    query_at = seq_index * local_rows
-    query_raw = lax.dynamic_slice_in_dim(query_part, query_at, local_rows, 0) + got[
-        :q_size
-    ].reshape(local_rows, query_cols)
-    kv_raw = lax.dynamic_slice_in_dim(kv_part, win_at, window, 0) + got[
-        q_size : q_size + kv_size
-    ].reshape(window, kv_cols)
-    win_squares = lax.dynamic_slice_in_dim(squares, win_at, window) + got[q_size + kv_size :]
+
+    w_half = lax.dynamic_index_in_dim(w_keyval, seq_index, 0, keepdims=False)
+    w_half = w_half.reshape(feature_cols, KVH, 2, 2, 2, quarter)
+    w_half = w_half.transpose(1, 2, 4, 0, 3, 5).reshape(tp_count, feature_cols, kv_cols)
+    w_half, scaled = lax.optimization_barrier((w_half, scaled))
+    w_kv = lax.all_to_all(w_half, ("x", "zh", "zl"), split_axis=0, concat_axis=0, tiled=True)
+    w_kv = w_kv.reshape(x_count, z_count, feature_cols, kv_cols)
+    kv_part = jnp.einsum("zxri,xzic->rc", scaled, w_kv, preferred_element_type=jnp.float32)
+    got_kv = lax.ppermute(
+        lax.dynamic_slice_in_dim(kv_part, partner * rest, window, 0), "seq", perm=[(0, 1), (1, 0)]
+    )
+    query_raw = lax.dynamic_slice_in_dim(query_part, query_at, local_rows, 0) + got[:local_rows]
+    kv_raw = lax.dynamic_slice_in_dim(kv_part, win_at, window, 0) + got_kv
+    win_squares = lax.dynamic_slice_in_dim(squares, win_at, window) + got[local_rows:].reshape(-1)
     win_rms = lax.rsqrt(win_squares / D + NORM_EPS)
     query_rms = lax.dynamic_slice_in_dim(win_rms, query_at - win_at, local_rows)
 

time: 150 us -> 160 us (1.067)
  waiting for transfers between devices: 70.3 us -> 78.6 us
  other arithmetic: 6.72 us -> 9.5 us
    ppermute x0 -> x1, waiting for transfers between devices: none -> 6.83 us  [local(): lax.ppermute(lax.dynamic_slice_in_dim(kv_part, partner * rest, window, 0)...]
    all_to_all x1, starting transfers between devices: 11.3 us -> 6.94 us  [local(): lax.all_to_all(w_half, ('x', 'zh', 'zl'), split_axis=0, concat_axis=0, ti...]
    all_gather x1, waiting for transfers between devices: 42.8 us -> 46.9 us  [local(): gathered = lax.all_gather(gathered, ('zh', 'zl'), axis=0, tiled=False)]
    ppermute x0 -> x1, starting transfers between devices: none -> 3.18 us  [local(): lax.ppermute(lax.dynamic_slice_in_dim(kv_part, partner * rest, window, 0)...]
    ppermute x1, waiting for transfers between devices: 13.9 us -> 11.2 us  [local(): got = lax.ppermute(payload, 'seq', perm=[(0, 1), (1, 0)])]
    convert_element_type x0 -> x1, other arithmetic: none -> 2.65 us  [local(): (gathered_f * gain_half.transpose(1, 0, 2)[:, :, None, :]).astype(jnp.bfl...]
  transfers between devices with their start and end apart: 5 -> 6, of which waited for: 4 -> 5; matrix products, arithmetic and copies ran while one was open for 6% -> 5% of each run, Pallas kernels for 0% -> 0%
where the time goes in v8:
time: 160 us; the launch traced here: 158 us
  waiting for transfers between devices  78.6 us (49%)
  starting transfers between devices  26.1 us (16%)
  between operations  15.8 us (10%)
  blocking collectives  12.5 us (8%)
  other arithmetic  9.5 us (6%)
  local copies, waits for them, and re-layouts  9.36 us (6%)
  matrix products  6.53 us (4%)
    all_gather x1, waiting for transfers between devices, local(): gathered = lax.all_gather(gathered, ('zh', 'zl'), axis=0, tiled=False)  46.9 us
    all_to_all x1, blocking collectives, local(): lax.all_to_all(spread, 'x', split_axis=0, concat_axis=0, tiled=True)  12.5 us
    ppermute x1, waiting for transfers between devices, local(): got = lax.ppermute(payload, 'seq', perm=[(0, 1), (1, 0)])  11.2 us
    all_to_all x1, waiting for transfers between devices, local(): lax.all_to_all(outgoing, 'rep', split_axis=0, concat_axis=0, tiled=True)  7.88 us
    all_to_all x1, starting transfers between devices, local(): lax.all_to_all(w_half, ('x', 'zh', 'zl'), split_axis=0, concat_axis=0, ti...  6.94 us
    ppermute x1, waiting for transfers between devices, local(): lax.ppermute(lax.dynamic_slice_in_dim(kv_part, partner * rest, window, 0)...  6.83 us
    all_to_all x1, starting transfers between devices, local(): lax.all_to_all(outgoing, 'rep', split_axis=0, concat_axis=0, tiled=True)  6.31 us
    all_to_all x1, waiting for transfers between devices, local(): lax.all_to_all(spread, 'zl', split_axis=0, concat_axis=0, tiled=True)  5.79 us
  transfers between devices with their start and end apart: 6, of which 5 were waited for; matrix products, arithmetic and copies ran while one was open for 5% of the time, Pallas kernels for 0%

profile of v8, /device:TPU:56, one launch (start us, length us, event | category | flops | bytes accessed | tf_op | source)
XLA Modules:
  0.0 158.4 jit_solution(16265811858222778212)
XLA Ops:
  6.5 0.9 constant_dynamic-slice_fusion.4
  11.3 0.9 fusion.46
  12.2 0.8 broadcast_select_fusion
  13.0 6.3 %all-to-all-start = ((bf16[8,192,128]{2,1,0:T(8,128)(2,1)}), bf16[8,192,128]{2,1,0:T(8,128)(2,1)S(1)}, u32[]{:S(2)}, u32[]{:S(2)}) async-start(bf16[8,192,128]{2,1,0:T(8,128)(2,1)} %broadcast_select_fusion), calls=%async_computation | async-start | bytes 786432 | tf_op jit(solution)/shard_map/all_to_all | solution.py:104
  19.4 0.8 copy.61
  20.1 0.8 copy.60
  21.4 7.9 %all-to-all-done = bf16[8,192,128]{2,1,0:T(8,128)(2,1)S(1)} async-done(((bf16[8,192,128]{2,1,0:T(8,128)(2,1)}), bf16[8,192,128]{2,1,0:T(8,128)(2,1)S(1)}, u32[]{:S(2)}, u32[]{:S(2)}) %all-to-all-start) | async-done | bytes 393248 | tf_op jit(solution)/shard_map/all_to_all | solution.py:104
  29.3 1.4 gather_fusion
  31.0 12.5 %all_to_all.24 = bf16[4,384,128]{2,1,0:T(8,128)(2,1)} all-to-all(bf16[4,384,128]{2,1,0:T(8,128)(2,1)S(1)} %broadcast_in_dim.157), channel_id=1, replica_groups=mesh['rep'=8,'seq'=2,'x'=4,'zh'=2,'zl'=4] {'x'}, dimensions={0} | all-to-all | bytes 786432 | tf_op jit(solution)/shard_map/all_to_all | solution.py:113
  43.6 1.1 constant_dynamic-slice_fusion.1
  45.0 0.9 copy.66
  46.6 46.9 %all-gather.3.cloned.1.call-done = bf16[32,384,128]{2,1,0:T(8,128)(2,1)} async-done(((bf16[4,384,128]{2,1,0:T(8,128)(2,1)}), bf16[32,384,128]{2,1,0:T(8,128)(2,1)}) %all-gather.3.cloned.1.call-update) | async-done | bytes 3145744 | tf_op jit(solution)/shard_map/all_gather | solution.py:114
  93.5 2.7 %fusion.1 = f32[384]{0:T(512)S(1)} fusion(bf16[8,4,384,128]{3,2,1,0:T(8,128)(2,1)} %bitcast.52), kind=kLoop, calls=%fused_computation.4 | loop fusion | flops 4718208 | bytes 3147264 | tf_op jit(solution)/shard_map/reduce_sum | solution.py:120
  96.3 2.6 %fusion.2 = bf16[8,4,384,128]{3,2,1,0:T(8,128)(2,1)} fusion(f32[8,4,128]{2,1,0:T(4,128)S(1)} %copy.62, bf16[32,384,128]{2,1,0:T(8,128)(2,1)S(1)} %copy-done.1), kind=kLoop, calls=%fused_computation.5 | loop fusion | flops 4718592 | bytes 6307840 | tf_op jit(solution)/shard_map/convert_element_type | solution.py:119
  99.0 6.9 %all-to-all-start.2 = ((bf16[32,128,64]{1,2,0:T(8,128)(2,1)}), bf16[32,128,64]{1,2,0:T(8,128)(2,1)S(1)}, u32[]{:S(2)}, u32[]{:S(2)}) async-start(bf16[32,128,64]{1,2,0:T(8,128)(2,1)} %bitcast.16), calls=%async_computation.2 | async-start | bytes 1048576 | tf_op jit(solution)/shard_map/all_to_all | solution.py:143
  106.0 2.9 %fusion.9 = f32[384,256]{1,0:T(8,128)S(1)} fusion(bf16[4,8,128,256]{3,2,1,0:T(8,128)(2,1)S(1)} %bitcast.51, bf16[8,4,384,128]{3,2,1,0:T(8,128)(2,1)} %fusion.2), kind=kOutput, calls=%fused_computation.12 | convolution fusion | flops 805306368 | bytes 5636096 | tf_op jit(solution)/shard_map/zxri,xzic->rc/dot_general | solution.py:122
  108.9 5.1 %collective-permute-start = (f32[193,256]{1,0:T(8,128)S(1)}, f32[193,256]{1,0:T(8,128)S(1)}, u32[]{:S(2)}, u32[]{:S(2)}) collective-permute-start(f32[193,256]{1,0:T(8,128)S(1)} %pad_maximum_fusion), channel_id=1, source_target_pairs={{0,32},{32,0},{1,33},{33,1},{2,34},{34,2},{3,35},{35,3},{4,36},{36... | collective-permute-start | bytes 592904 | tf_op jit(solution)/shard_map/ppermute | solution.py:137
  114.2 11.2 %collective-permute-done = f32[193,256]{1,0:T(8,128)S(1)} collective-permute-done((f32[193,256]{1,0:T(8,128)S(1)}, f32[193,256]{1,0:T(8,128)S(1)}, u32[]{:S(2)}, u32[]{:S(2)}) %collective-permute-start) | collective-permute-done | bytes 197664 | tf_op jit(solution)/shard_map/ppermute | solution.py:137
  125.5 3.0 %fusion.15 = f32[384,64]{0,1:T(8,128)S(1)} fusion(bf16[4,8,128,64]{2,3,1,0:T(8,128)(2,1)S(1)} %bitcast.57, bf16[8,4,384,128]{3,2,1,0:T(8,128)(2,1)} %fusion.2), kind=kOutput, calls=%fused_computation.18 | convolution fusion | flops 201326592 | bytes 3768320 | tf_op jit(solution)/shard_map/zxri,xzic->rc/dot_general | solution.py:145
  128.5 3.2 %collective-permute-start.1 = (f32[256,64]{0,1:T(8,128)S(1)}, f32[256,64]{0,1:T(8,128)S(1)}, u32[]{:S(2)}, u32[]{:S(2)}) collective-permute-start(f32[256,64]{0,1:T(8,128)S(1)} %constant_dynamic-slice_fusion), channel_id=1, source_target_pairs={{0,32},{32,0},{1,33},{33,1},{2,34},{34,2},{3,35},{35,3},{4,36},{36... | collective-permute-start | bytes 196616 | tf_op jit(solution)/shard_map/ppermute | solution.py:146
  131.8 6.8 %collective-permute-done.1 = f32[256,64]{0,1:T(8,128)S(1)} collective-permute-done((f32[256,64]{0,1:T(8,128)S(1)}, f32[256,64]{0,1:T(8,128)S(1)}, u32[]{:S(2)}, u32[]{:S(2)}) %collective-permute-start.1) | collective-permute-done | bytes 65568 | tf_op jit(solution)/shard_map/ppermute | solution.py:146
  139.5 4.6 %all-to-all-start.3 = ((bf16[4,256,2,32]{1,3,2,0:T(8,128)(2,1)}), bf16[4,256,2,32]{1,3,2,0:T(8,128)(2,1)S(1)}, u32[]{:S(2)}, u32[]{:S(2)}) async-start(bf16[4,256,2,32]{1,3,2,0:T(8,128)(2,1)} %broadcast_in_dim.158), calls=%async_computation.3 | async-start | bytes 262144 | tf_op jit(solution)/shard_map/all_to_all | solution.py:180
  144.2 5.8 %all-to-all-done.3 = bf16[4,256,2,32]{1,3,2,0:T(8,128)(2,1)S(1)} async-done(((bf16[4,256,2,32]{1,3,2,0:T(8,128)(2,1)}), bf16[4,256,2,32]{1,3,2,0:T(8,128)(2,1)S(1)}, u32[]{:S(2)}, u32[]{:S(2)}) %all-to-all-start.3) | async-done | bytes 131104 | tf_op jit(solution)/shard_map/all_to_all | solution.py:180
  150.8 0.7 bitcast_select_fusion
  (57 shorter events, 5.9 us)
Async XLA Ops:
  6.5 99.5 %copy-start = (bf16[4096,256]{1,0:T(8,128)(2,1)S(1)}, bf16[4096,256]{1,0:T(8,128)(2,1)}, u32[]{:S(2)}) copy-start(bf16[4096,256]{1,0:T(8,128)(2,1)} %param.8) | copy-start | bytes 6291460
  6.5 37.0 %copy-start.2 = (f32[8192]{0:T(1024)S(1)}, f32[8192]{0:T(1024)}, u32[]{:S(2)}) copy-start(f32[8192]{0:T(1024)} %param.7) | copy-start | bytes 98308
  13.0 16.3 %all-to-all-start = ((bf16[8,192,128]{2,1,0:T(8,128)(2,1)}), bf16[8,192,128]{2,1,0:T(8,128)(2,1)S(1)}, u32[]{:S(2)}, u32[]{:S(2)}) async-start(bf16[8,192,128]{2,1,0:T(8,128)(2,1)} %broadcast_select_fusion), calls=%async_computation | async-start | bytes 786432 | tf_op jit(solution)/shard_map/all_to_all | solution.py:104
  19.3 74.2 %all-gather.3.cloned.1.call-start = ((), (), s32[]{:S(2)}) async-start(), calls=%async_computation.4 | async-start | bytes 3538944 | tf_op jit(solution)/shard_map/all_gather | solution.py:114
  93.5 2.8 %copy-start.1 = (bf16[32,384,128]{2,1,0:T(8,128)(2,1)S(1)}, bf16[32,384,128]{2,1,0:T(8,128)(2,1)}, u32[]{:S(2)}) copy-start(bf16[32,384,128]{2,1,0:T(8,128)(2,1)} %all-gather.3.cloned.1.call-done) | copy-start | bytes 9437188
  99.0 26.6 %all-to-all-start.2 = ((bf16[32,128,64]{1,2,0:T(8,128)(2,1)}), bf16[32,128,64]{1,2,0:T(8,128)(2,1)S(1)}, u32[]{:S(2)}, u32[]{:S(2)}) async-start(bf16[32,128,64]{1,2,0:T(8,128)(2,1)} %bitcast.16), calls=%async_computation.2 | async-start | bytes 1048576 | tf_op jit(solution)/shard_map/all_to_all | solution.py:143
  108.9 16.4 %collective-permute-start = (f32[193,256]{1,0:T(8,128)S(1)}, f32[193,256]{1,0:T(8,128)S(1)}, u32[]{:S(2)}, u32[]{:S(2)}) collective-permute-start(f32[193,256]{1,0:T(8,128)S(1)} %pad_maximum_fusion), channel_id=1, source_target_pairs={{0,32},{32,0},{1,33},{33,1},{2,34},{34,2},{3,35},{35,3},{4,36},{36... | collective-permute-start | bytes 592904 | tf_op jit(solution)/shard_map/ppermute | solution.py:137
  128.5 10.1 %collective-permute-start.1 = (f32[256,64]{0,1:T(8,128)S(1)}, f32[256,64]{0,1:T(8,128)S(1)}, u32[]{:S(2)}, u32[]{:S(2)}) collective-permute-start(f32[256,64]{0,1:T(8,128)S(1)} %constant_dynamic-slice_fusion), channel_id=1, source_target_pairs={{0,32},{32,0},{1,33},{33,1},{2,34},{34,2},{3,35},{35,3},{4,36},{36... | collective-permute-start | bytes 196616 | tf_op jit(solution)/shard_map/ppermute | solution.py:146
  139.5 10.5 %all-to-all-start.3 = ((bf16[4,256,2,32]{1,3,2,0:T(8,128)(2,1)}), bf16[4,256,2,32]{1,3,2,0:T(8,128)(2,1)S(1)}, u32[]{:S(2)}, u32[]{:S(2)}) async-start(bf16[4,256,2,32]{1,3,2,0:T(8,128)(2,1)} %broadcast_in_dim.158), calls=%async_computation.3 | async-start | bytes 262144 | tf_op jit(solution)/shard_map/all_to_all | solution.py:180
Sparse Core Ops, SparseCore 0:
  43.6 49.8 all-gather.2

commit v9 on v6

--- a/solution.py
+++ b/solution.py
@@ -101,10 +101,18 @@
     outgoing = jnp.where(
         (targets == my_routes[0])[:, None, None], first_block[None], second_block[None]
     ).reshape(rep_count * LMAX, feature_cols)
+    core = replica % 2
+    eighth = quarter // 2
     w_half = lax.dynamic_index_in_dim(w_keyval, seq_index, 0, keepdims=False)
-    w_half = w_half.reshape(feature_cols, KVH, 2, 2, 2, quarter)
-    w_half = w_half.transpose(1, 2, 4, 0, 3, 5).reshape(tp_count, feature_cols, kv_cols)
-    w_kv = lax.all_to_all(w_half, ("x", "zh", "zl"), split_axis=0, concat_axis=0, tiled=True)
+    w_half = w_half.reshape(feature_cols, KVH, 2, 2, 2, 2, eighth)
+    w_half = lax.dynamic_index_in_dim(w_half, core, 5, keepdims=False)
+    w_half = w_half.transpose(1, 2, 4, 0, 3, 5).reshape(tp_count, feature_cols, kv_cols // 2)
+    w_mine = lax.all_to_all(w_half, ("x", "zh", "zl"), split_axis=0, concat_axis=0, tiled=True)
+    w_other = lax.ppermute(
+        w_mine, "rep", perm=[(i, i + 1 - 2 * (i % 2)) for i in range(rep_count)]
+    )
+    w_kv = jnp.where(core == 0, jnp.stack([w_mine, w_other]), jnp.stack([w_other, w_mine]))
+    w_kv = w_kv.reshape(2, tp_count, feature_cols, 2, eighth).transpose(1, 2, 3, 0, 4)
     incoming = lax.all_to_all(outgoing, "rep", split_axis=0, concat_axis=0, tiled=True)
     w_kv = w_kv.reshape(x_count, z_count, feature_cols, kv_cols)
     tables = response_tables(lengths, routes)

time: 150 us -> 143 us (0.953)
  waiting for transfers between devices: 70.3 us -> 64.6 us
  other arithmetic: 6.72 us -> 4.91 us
    all_gather x1, waiting for transfers between devices: 42.8 us -> 21.4 us  [local(): gathered = lax.all_gather(gathered, ('zh', 'zl'), axis=0, tiled=False)]
    all_to_all x1, waiting for transfers between devices: 0.01 us -> 12.9 us  [local(): lax.all_to_all(w_half, ('x', 'zh', 'zl'), split_axis=0, concat_axis=0, ti...]
    ppermute x0 -> x1, starting transfers between devices: none -> 1.91 us  [local(): lax.ppermute(w_mine, 'rep', perm=[(i, i + 1 - 2 * (i % 2)) for i in range...]
    reduce_sum x1, other arithmetic: 2.58 us -> 0.7 us  [local(): squares = jnp.sum(gathered_f * gathered_f, axis=(0, 1, 3))]
    all_to_all x1, starting transfers between devices: 5.02 us -> 3.32 us  [local(): lax.all_to_all(spread, 'zl', split_axis=0, concat_axis=0, tiled=True)]
  transfers between devices with their start and end apart: 5 -> 6, of which waited for: 4 -> 6; matrix products, arithmetic and copies ran while one was open for 6% -> 4% of each run, Pallas kernels for 0% -> 0%
where the time goes in v9:
time: 143 us; the launch traced here: 141 us
  waiting for transfers between devices  64.6 us (45%)
  starting transfers between devices  26.7 us (19%)
  between operations  15.9 us (11%)
  blocking collectives  12.5 us (9%)
  local copies, waits for them, and re-layouts  9.68 us (7%)
  matrix products  6.72 us (5%)
  other arithmetic  4.91 us (3%)
    all_gather x1, waiting for transfers between devices, local(): gathered = lax.all_gather(gathered, ('zh', 'zl'), axis=0, tiled=False)  21.4 us
    ppermute x1, waiting for transfers between devices, local(): got = lax.ppermute(payload, 'seq', perm=[(0, 1), (1, 0)])  15.1 us
    all_to_all x1, waiting for transfers between devices, local(): lax.all_to_all(w_half, ('x', 'zh', 'zl'), split_axis=0, concat_axis=0, ti...  12.9 us
    all_to_all x1, blocking collectives, local(): lax.all_to_all(spread, 'x', split_axis=0, concat_axis=0, tiled=True)  12.5 us
    all_to_all x1, starting transfers between devices, local(): lax.all_to_all(w_half, ('x', 'zh', 'zl'), split_axis=0, concat_axis=0, ti...  11.3 us
    all_to_all x1, waiting for transfers between devices, local(): lax.all_to_all(outgoing, 'rep', split_axis=0, concat_axis=0, tiled=True)  7.88 us
    all_to_all x1, starting transfers between devices, local(): lax.all_to_all(outgoing, 'rep', split_axis=0, concat_axis=0, tiled=True)  6.31 us
    all_to_all x1, waiting for transfers between devices, local(): lax.all_to_all(spread, 'zl', split_axis=0, concat_axis=0, tiled=True)  6.05 us
  transfers between devices with their start and end apart: 6, of which 6 were waited for; matrix products, arithmetic and copies ran while one was open for 4% of the time, Pallas kernels for 0%

profile of v9, /device:TPU:56, one launch (start us, length us, event | category | flops | bytes accessed | tf_op | source)
XLA Modules:
  0.0 141.1 jit_solution(12428793262559186454)
XLA Ops:
  6.5 0.9 constant_dynamic-slice_fusion.3
  11.3 0.9 fusion.49
  12.2 0.8 broadcast_select_fusion
  13.0 6.3 %all-to-all-start = ((bf16[8,192,128]{2,1,0:T(8,128)(2,1)}), bf16[8,192,128]{2,1,0:T(8,128)(2,1)S(1)}, u32[]{:S(2)}, u32[]{:S(2)}) async-start(bf16[8,192,128]{2,1,0:T(8,128)(2,1)} %broadcast_select_fusion), calls=%async_computation | async-start | bytes 786432 | tf_op jit(solution)/shard_map/all_to_all | solution.py:116
  19.3 0.8 copy.72
  20.1 0.8 copy.71
  21.4 7.9 %all-to-all-done = bf16[8,192,128]{2,1,0:T(8,128)(2,1)S(1)} async-done(((bf16[8,192,128]{2,1,0:T(8,128)(2,1)}), bf16[8,192,128]{2,1,0:T(8,128)(2,1)S(1)}, u32[]{:S(2)}, u32[]{:S(2)}) %all-to-all-start) | async-done | bytes 393248 | tf_op jit(solution)/shard_map/all_to_all | solution.py:116
  29.3 1.4 %gather_fusion = bf16[384,128]{1,0:T(8,128)(2,1)S(1)} fusion(bf16[1536,128]{1,0:T(8,128)(2,1)S(1)} %bitcast.63, s32[1024]{0:T(1024)S(1)} %pad_clamp_fusion), kind=kCustom, calls=%fused_computation | custom fusion | bytes 198144 | tf_op jit(solution)/shard_map/jit(_take)/gather | solution.py:76
  31.0 12.5 %all_to_all.24 = bf16[4,384,128]{2,1,0:T(8,128)(2,1)} all-to-all(bf16[4,384,128]{2,1,0:T(8,128)(2,1)S(1)} %broadcast_in_dim.157), channel_id=1, replica_groups=mesh['rep'=8,'seq'=2,'x'=4,'zh'=2,'zl'=4] {'x'}, dimensions={0} | all-to-all | bytes 786432 | tf_op jit(solution)/shard_map/all_to_all | solution.py:126
  43.5 1.1 constant_dynamic-slice_fusion.1
  44.9 0.7 copy.76
  45.6 11.3 %all-to-all-start.2 = ((bf16[32,128,32]{1,2,0:T(8,128)(2,1)}), bf16[32,128,32]{1,2,0:T(8,128)(2,1)S(1)}, u32[]{:S(2)}, u32[]{:S(2)}) async-start(bf16[32,128,32]{1,2,0:T(8,128)(2,1)} %bitcast.14), calls=%async_computation.2 | async-start | bytes 524288 | tf_op jit(solution)/shard_map/all_to_all | solution.py:110
  57.2 12.9 %all-to-all-done.2 = bf16[32,128,32]{1,2,0:T(8,128)(2,1)S(1)} async-done(((bf16[32,128,32]{1,2,0:T(8,128)(2,1)}), bf16[32,128,32]{1,2,0:T(8,128)(2,1)S(1)}, u32[]{:S(2)}, u32[]{:S(2)}) %all-to-all-start.2) | async-done | bytes 262176 | tf_op jit(solution)/shard_map/all_to_all | solution.py:110
  70.1 1.9 %collective-permute-start = (bf16[32,128,32]{1,2,0:T(8,128)(2,1)S(1)}, bf16[32,128,32]{1,2,0:T(8,128)(2,1)S(1)}, u32[]{:S(2)}, u32[]{:S(2)}) collective-permute-start(bf16[32,128,32]{1,2,0:T(8,128)(2,1)S(1)} %all-to-all-done.2), channel_id=1, source_target_pairs={{0,64},{64,0},{128,192},{192,128},{256,320},{320,256},{384,448},{4... | collective-permute-start | bytes 786440 | tf_op jit(solution)/shard_map/ppermute | solution.py:111
  72.3 1.2 collective-permute-done
  73.7 21.4 %all-gather.3.cloned.1.call-done = bf16[32,384,128]{2,1,0:T(8,128)(2,1)} async-done(((bf16[4,384,128]{2,1,0:T(8,128)(2,1)}), bf16[32,384,128]{2,1,0:T(8,128)(2,1)}) %all-gather.3.cloned.1.call-update) | async-done | bytes 3145744 | tf_op jit(solution)/shard_map/all_gather | solution.py:127
  95.1 3.0 %fusion.15 = f32[384,64]{0,1:T(8,128)S(1)} fusion(bf16[4,8,128,64]{2,3,1,0:T(8,128)(2,1)S(1)} %bitcast.70, f32[8,4,128]{2,1,0:T(4,128)S(1)} %copy.73, bf16[32,384,128]{2,1,0:T(8,128)(2,1)} %all-gather.3.cloned.1.call-done), kind=kOutput, calls=%fused_computation.18 | convolution fusion | flops 206045184 | bytes 3784704 | tf_op jit(solution)/shard_map/zxri,xzic->rc/dot_general | solution.py:136
  98.3 3.0 %fusion.9 = f32[384,256]{1,0:T(8,128)S(1)} fusion(bf16[4,8,128,256]{3,2,1,0:T(8,128)(2,1)S(1)} %bitcast.62, f32[8,4,128]{2,1,0:T(4,128)S(1)} %copy.73, bf16[32,384,128]{2,1,0:T(8,128)(2,1)} %all-gather.3.cloned.1.call-done), kind=kOutput, calls=%fused_computation.12 | convolution fusion | flops 810024960 | bytes 5652480 | tf_op jit(solution)/shard_map/zxri,xzic->rc/dot_general | solution.py:135
  101.5 0.7 fusion.1
  102.3 3.9 %collective-permute-start.1 = (f32[65792]{0:T(1024)S(1)}, f32[65792]{0:T(1024)S(1)}, u32[]{:S(2)}, u32[]{:S(2)}) collective-permute-start(f32[65792]{0:T(1024)S(1)} %pad_maximum_fusion), channel_id=1, source_target_pairs={{0,32},{32,0},{1,33},{33,1},{2,34},{34,2},{3,35},{35,3},{4,36},{36... | collective-permute-start | bytes 789512 | tf_op jit(solution)/shard_map/ppermute | solution.py:149
  106.7 15.1 %collective-permute-done.1 = f32[65792]{0:T(1024)S(1)} collective-permute-done((f32[65792]{0:T(1024)S(1)}, f32[65792]{0:T(1024)S(1)}, u32[]{:S(2)}, u32[]{:S(2)}) %collective-permute-start.1) | collective-permute-done | bytes 263200 | tf_op jit(solution)/shard_map/ppermute | solution.py:149
  123.1 3.3 %all-to-all-start.3 = ((bf16[4,256,2,32]{1,3,2,0:T(8,128)(2,1)}), bf16[4,256,2,32]{1,3,2,0:T(8,128)(2,1)S(1)}, u32[]{:S(2)}, u32[]{:S(2)}) async-start(bf16[4,256,2,32]{1,3,2,0:T(8,128)(2,1)} %broadcast_in_dim.158), calls=%async_computation.3 | async-start | bytes 262144 | tf_op jit(solution)/shard_map/all_to_all | solution.py:189
  126.7 6.1 %all-to-all-done.3 = bf16[4,256,2,32]{1,3,2,0:T(8,128)(2,1)S(1)} async-done(((bf16[4,256,2,32]{1,3,2,0:T(8,128)(2,1)}), bf16[4,256,2,32]{1,3,2,0:T(8,128)(2,1)S(1)}, u32[]{:S(2)}, u32[]{:S(2)}) %all-to-all-start.3) | async-done | bytes 131104 | tf_op jit(solution)/shard_map/all_to_all | solution.py:189
  133.5 0.7 bitcast_select_fusion
  (66 shorter events, 6.5 us)
Async XLA Ops:
  6.5 91.8 %copy-start = (bf16[4096,256]{1,0:T(8,128)(2,1)S(1)}, bf16[4096,256]{1,0:T(8,128)(2,1)}, u32[]{:S(2)}) copy-start(bf16[4096,256]{1,0:T(8,128)(2,1)} %param.8) | copy-start | bytes 6291460
  13.0 16.3 %all-to-all-start = ((bf16[8,192,128]{2,1,0:T(8,128)(2,1)}), bf16[8,192,128]{2,1,0:T(8,128)(2,1)S(1)}, u32[]{:S(2)}, u32[]{:S(2)}) async-start(bf16[8,192,128]{2,1,0:T(8,128)(2,1)} %broadcast_select_fusion), calls=%async_computation | async-start | bytes 786432 | tf_op jit(solution)/shard_map/all_to_all | solution.py:116
  19.3 75.8 %all-gather.3.cloned.1.call-start = ((), (), s32[]{:S(2)}) async-start(), calls=%async_computation.4 | async-start | bytes 3538944 | tf_op jit(solution)/shard_map/all_gather | solution.py:127
  29.3 27.9 %copy-start.2 = (f32[8192]{0:T(1024)S(1)}, f32[8192]{0:T(1024)}, u32[]{:S(2)}) copy-start(f32[8192]{0:T(1024)} %param.7) | copy-start | bytes 98308
  45.6 24.5 %all-to-all-start.2 = ((bf16[32,128,32]{1,2,0:T(8,128)(2,1)}), bf16[32,128,32]{1,2,0:T(8,128)(2,1)S(1)}, u32[]{:S(2)}, u32[]{:S(2)}) async-start(bf16[32,128,32]{1,2,0:T(8,128)(2,1)} %bitcast.14), calls=%async_computation.2 | async-start | bytes 524288 | tf_op jit(solution)/shard_map/all_to_all | solution.py:110
  70.1 3.4 %collective-permute-start = (bf16[32,128,32]{1,2,0:T(8,128)(2,1)S(1)}, bf16[32,128,32]{1,2,0:T(8,128)(2,1)S(1)}, u32[]{:S(2)}, u32[]{:S(2)}) collective-permute-start(bf16[32,128,32]{1,2,0:T(8,128)(2,1)S(1)} %all-to-all-done.2), channel_id=1, source_target_pairs={{0,64},{64,0},{128,192},{192,128},{256,320},{320,256},{384,448},{4... | collective-permute-start | bytes 786440 | tf_op jit(solution)/shard_map/ppermute | solution.py:111
  98.3 3.2 %copy-start.1 = (bf16[32,384,128]{2,1,0:T(8,128)(2,1)S(1)}, bf16[32,384,128]{2,1,0:T(8,128)(2,1)}, u32[]{:S(2)}) copy-start(bf16[32,384,128]{2,1,0:T(8,128)(2,1)} %all-gather.3.cloned.1.call-done) | copy-start | bytes 9437188
  102.3 19.5 %collective-permute-start.1 = (f32[65792]{0:T(1024)S(1)}, f32[65792]{0:T(1024)S(1)}, u32[]{:S(2)}, u32[]{:S(2)}) collective-permute-start(f32[65792]{0:T(1024)S(1)} %pad_maximum_fusion), channel_id=1, source_target_pairs={{0,32},{32,0},{1,33},{33,1},{2,34},{34,2},{3,35},{35,3},{4,36},{36... | collective-permute-start | bytes 789512 | tf_op jit(solution)/shard_map/ppermute | solution.py:149
  123.1 9.6 %all-to-all-start.3 = ((bf16[4,256,2,32]{1,3,2,0:T(8,128)(2,1)}), bf16[4,256,2,32]{1,3,2,0:T(8,128)(2,1)S(1)}, u32[]{:S(2)}, u32[]{:S(2)}) async-start(bf16[4,256,2,32]{1,3,2,0:T(8,128)(2,1)} %broadcast_in_dim.158), calls=%async_computation.3 | async-start | bytes 262144 | tf_op jit(solution)/shard_map/all_to_all | solution.py:189
Sparse Core Ops, SparseCore 0:
  43.6 51.4 all-gather.2

commit v10 on v6

--- a/solution.py
+++ b/solution.py
@@ -101,10 +101,15 @@
     outgoing = jnp.where(
         (targets == my_routes[0])[:, None, None], first_block[None], second_block[None]
     ).reshape(rep_count * LMAX, feature_cols)
+    slice_cols = quarter // rep_count
     w_half = lax.dynamic_index_in_dim(w_keyval, seq_index, 0, keepdims=False)
-    w_half = w_half.reshape(feature_cols, KVH, 2, 2, 2, quarter)
-    w_half = w_half.transpose(1, 2, 4, 0, 3, 5).reshape(tp_count, feature_cols, kv_cols)
-    w_kv = lax.all_to_all(w_half, ("x", "zh", "zl"), split_axis=0, concat_axis=0, tiled=True)
+    w_half = w_half.reshape(feature_cols, KVH, 2, 2, 2, rep_count, slice_cols)
+    w_half = lax.dynamic_index_in_dim(w_half, replica, 5, keepdims=False)
+    w_half = w_half.transpose(1, 2, 4, 0, 3, 5).reshape(tp_count, feature_cols, 2 * slice_cols)
+    w_mine = lax.all_to_all(w_half, ("x", "zh", "zl"), split_axis=0, concat_axis=0, tiled=True)
+    w_spread = jnp.broadcast_to(w_mine[None], (rep_count,) + w_mine.shape)
+    w_kv = lax.all_to_all(w_spread, "rep", split_axis=0, concat_axis=0, tiled=True)
+    w_kv = w_kv.reshape(rep_count, tp_count, feature_cols, 2, slice_cols).transpose(1, 2, 3, 0, 4)
     incoming = lax.all_to_all(outgoing, "rep", split_axis=0, concat_axis=0, tiled=True)
     w_kv = w_kv.reshape(x_count, z_count, feature_cols, kv_cols)
     tables = response_tables(lengths, routes)

time: 150 us -> 141 us (0.940)
  the two profiles are of different devices: /device:TPU:56 before, /device:TPU:16 now
where the time goes in v10:
time: 141 us
  waiting for transfers between devices  48.4 us (34%)
  blocking collectives  29.2 us (21%)
  starting transfers between devices  25.5 us (18%)
  between operations  15.9 us (11%)
  local copies, waits for them, and re-layouts  10.2 us (7%)
  matrix products  6.72 us (5%)
  other arithmetic  4.83 us (3%)
    all_to_all x1, blocking collectives, local(): lax.all_to_all(w_half, ('x', 'zh', 'zl'), split_axis=0, concat_axis=0, ti...  18.1 us
    ppermute x1, waiting for transfers between devices, local(): got = lax.ppermute(payload, 'seq', perm=[(0, 1), (1, 0)])  13.6 us
    all_to_all x1, waiting for transfers between devices, local(): lax.all_to_all(w_spread, 'rep', split_axis=0, concat_axis=0, tiled=True)  11.5 us
    all_to_all x1, blocking collectives, local(): lax.all_to_all(spread, 'x', split_axis=0, concat_axis=0, tiled=True)  11.1 us
    all_gather x1, waiting for transfers between devices, local(): gathered = lax.all_gather(gathered, ('zh', 'zl'), axis=0, tiled=False)  10.1 us
    all_to_all x1, starting transfers between devices, local(): lax.all_to_all(outgoing, 'rep', split_axis=0, concat_axis=0, tiled=True)  9.08 us
    all_to_all x1, waiting for transfers between devices, local(): lax.all_to_all(outgoing, 'rep', split_axis=0, concat_axis=0, tiled=True)  7.2 us
    all_to_all x1, starting transfers between devices, local(): lax.all_to_all(w_spread, 'rep', split_axis=0, concat_axis=0, tiled=True)  6.79 us
  transfers between devices with their start and end apart: 5, of which 5 were waited for; matrix products, arithmetic and copies ran while one was open for 4% of the time, Pallas kernels for 0%

profile of v10, /device:TPU:16, one launch (start us, length us, event | category | flops | bytes accessed | tf_op | source)
XLA Modules:
  0.0 140.6 jit_solution(11991589208334938467)
XLA Ops:
  6.5 0.9 constant_dynamic-slice_fusion.4
  9.9 0.6 iota_compare_fusion.3
  11.3 0.9 fusion.48
  12.2 0.8 broadcast_select_fusion
  13.0 9.1 %all-to-all-start = ((bf16[8,192,128]{2,1,0:T(8,128)(2,1)}), bf16[8,192,128]{2,1,0:T(8,128)(2,1)S(1)}, u32[]{:S(2)}, u32[]{:S(2)}) async-start(bf16[8,192,128]{2,1,0:T(8,128)(2,1)} %broadcast_select_fusion), calls=%async_computation | async-start | bytes 786432 | tf_op jit(solution)/shard_map/all_to_all | solution.py:113
  22.1 0.8 copy.82
  22.9 0.8 copy.81
  24.2 7.2 %all-to-all-done = bf16[8,192,128]{2,1,0:T(8,128)(2,1)S(1)} async-done(((bf16[8,192,128]{2,1,0:T(8,128)(2,1)}), bf16[8,192,128]{2,1,0:T(8,128)(2,1)S(1)}, u32[]{:S(2)}, u32[]{:S(2)}) %all-to-all-start) | async-done | bytes 393248 | tf_op jit(solution)/shard_map/all_to_all | solution.py:113
  31.4 1.4 %gather_fusion = bf16[384,128]{1,0:T(8,128)(2,1)S(1)} fusion(bf16[1536,128]{1,0:T(8,128)(2,1)S(1)} %bitcast.63, s32[1024]{0:T(1024)S(1)} %pad_clamp_fusion), kind=kCustom, calls=%fused_computation | custom fusion | bytes 198144 | tf_op jit(solution)/shard_map/jit(_take)/gather | solution.py:76
  33.1 11.1 %all_to_all.29 = bf16[4,384,128]{2,1,0:T(8,128)(2,1)} all-to-all(bf16[4,384,128]{2,1,0:T(8,128)(2,1)S(1)} %broadcast_in_dim.163), channel_id=1, replica_groups=mesh['rep'=8,'seq'=2,'x'=4,'zh'=2,'zl'=4] {'x'}, dimensions={0} | all-to-all | bytes 786432 | tf_op jit(solution)/shard_map/all_to_all | solution.py:123
  44.2 1.1 constant_dynamic-slice_fusion.2
  45.7 18.1 %all_to_all.30 = bf16[32,128,8]{1,2,0:T(8,128)(2,1)S(1)} all-to-all(bf16[32,128,8]{1,2,0:T(8,128)(2,1)S(1)} %bitcast.73), channel_id=1, replica_groups=mesh['rep'=8,'seq'=2,'x'=4,'zh'=2,'zl'=4] {'x','zh','zl'}, dimensions={0} | all-to-all | bytes 131072 | tf_op jit(solution)/shard_map/all_to_all | solution.py:109
  63.8 0.9 broadcast_in_dim.164
  64.7 6.8 %all-to-all-start.3 = ((bf16[8,32,128,8]{2,1,3,0:T(8,128)(2,1)}), bf16[8,32,128,8]{2,1,3,0:T(8,128)(2,1)S(1)}, u32[]{:S(2)}, u32[]{:S(2)}) async-start(bf16[8,32,128,8]{2,1,3,0:T(8,128)(2,1)} %broadcast_in_dim.164), calls=%async_computation.3 | async-start | bytes 1048576 | tf_op jit(solution)/shard_map/all_to_all | solution.py:111
  72.0 11.5 %all-to-all-done.3 = bf16[8,32,128,8]{2,1,3,0:T(8,128)(2,1)S(1)} async-done(((bf16[8,32,128,8]{2,1,3,0:T(8,128)(2,1)}), bf16[8,32,128,8]{2,1,3,0:T(8,128)(2,1)S(1)}, u32[]{:S(2)}, u32[]{:S(2)}) %all-to-all-start.3) | async-done | bytes 524320 | tf_op jit(solution)/shard_map/all_to_all | solution.py:111
  83.9 10.1 %all-gather.3.cloned.1.call-done = bf16[32,384,128]{2,1,0:T(8,128)(2,1)} async-done(((bf16[4,384,128]{2,1,0:T(8,128)(2,1)}), bf16[32,384,128]{2,1,0:T(8,128)(2,1)}) %all-gather.3.cloned.1.call-update) | async-done | bytes 3145744 | tf_op jit(solution)/shard_map/all_gather | solution.py:124
  94.0 3.0 %fusion.15 = f32[384,64]{0,1:T(8,128)S(1)} fusion(bf16[4,8,128,64]{2,3,1,0:T(8,128)(2,1)S(1)} %bitcast.70, f32[8,4,128]{2,1,0:T(4,128)S(1)} %copy.83, bf16[32,384,128]{2,1,0:T(8,128)(2,1)} %all-gather.3.cloned.1.call-done), kind=kOutput, calls=%fused_computation.18 | convolution fusion | flops 206045184 | bytes 3784704 | tf_op jit(solution)/shard_map/zxri,xzic->rc/dot_general | solution.py:133
  97.2 3.0 %fusion.9 = f32[384,256]{1,0:T(8,128)S(1)} fusion(bf16[4,8,128,256]{3,2,1,0:T(8,128)(2,1)S(1)} %bitcast.62, f32[8,4,128]{2,1,0:T(4,128)S(1)} %copy.83, bf16[32,384,128]{2,1,0:T(8,128)(2,1)} %all-gather.3.cloned.1.call-done), kind=kOutput, calls=%fused_computation.12 | convolution fusion | flops 810024960 | bytes 5652480 | tf_op jit(solution)/shard_map/zxri,xzic->rc/dot_general | solution.py:132
  100.4 0.7 fusion.1
  101.2 5.6 %collective-permute-start = (f32[65792]{0:T(1024)S(1)}, f32[65792]{0:T(1024)S(1)}, u32[]{:S(2)}, u32[]{:S(2)}) collective-permute-start(f32[65792]{0:T(1024)S(1)} %pad_maximum_fusion), channel_id=1, source_target_pairs={{0,32},{32,0},{1,33},{33,1},{2,34},{34,2},{3,35},{35,3},{4,36},{36... | collective-permute-start | bytes 789512 | tf_op jit(solution)/shard_map/ppermute | solution.py:146
  107.2 13.6 %collective-permute-done = f32[65792]{0:T(1024)S(1)} collective-permute-done((f32[65792]{0:T(1024)S(1)}, f32[65792]{0:T(1024)S(1)}, u32[]{:S(2)}, u32[]{:S(2)}) %collective-permute-start) | collective-permute-done | bytes 263200 | tf_op jit(solution)/shard_map/ppermute | solution.py:146
  122.1 4.0 %all-to-all-start.4 = ((bf16[4,256,2,32]{1,3,2,0:T(8,128)(2,1)}), bf16[4,256,2,32]{1,3,2,0:T(8,128)(2,1)S(1)}, u32[]{:S(2)}, u32[]{:S(2)}) async-start(bf16[4,256,2,32]{1,3,2,0:T(8,128)(2,1)} %broadcast_in_dim.165), calls=%async_computation.4 | async-start | bytes 262144 | tf_op jit(solution)/shard_map/all_to_all | solution.py:186
  126.4 5.8 %all-to-all-done.4 = bf16[4,256,2,32]{1,3,2,0:T(8,128)(2,1)S(1)} async-done(((bf16[4,256,2,32]{1,3,2,0:T(8,128)(2,1)}), bf16[4,256,2,32]{1,3,2,0:T(8,128)(2,1)S(1)}, u32[]{:S(2)}, u32[]{:S(2)}) %all-to-all-start.4) | async-done | bytes 131104 | tf_op jit(solution)/shard_map/all_to_all | solution.py:186
  133.0 0.7 bitcast_select_fusion
  (67 shorter events, 6.1 us)
Async XLA Ops:
  6.5 90.6 %copy-start = (bf16[4096,256]{1,0:T(8,128)(2,1)S(1)}, bf16[4096,256]{1,0:T(8,128)(2,1)}, u32[]{:S(2)}) copy-start(bf16[4096,256]{1,0:T(8,128)(2,1)} %param.8) | copy-start | bytes 6291460
  13.0 18.4 %all-to-all-start = ((bf16[8,192,128]{2,1,0:T(8,128)(2,1)}), bf16[8,192,128]{2,1,0:T(8,128)(2,1)S(1)}, u32[]{:S(2)}, u32[]{:S(2)}) async-start(bf16[8,192,128]{2,1,0:T(8,128)(2,1)} %broadcast_select_fusion), calls=%async_computation | async-start | bytes 786432 | tf_op jit(solution)/shard_map/all_to_all | solution.py:113
  22.1 71.8 %all-gather.3.cloned.1.call-start = ((), (), s32[]{:S(2)}) async-start(), calls=%async_computation.5 | async-start | bytes 3538944 | tf_op jit(solution)/shard_map/all_gather | solution.py:124
  32.8 38.7 %copy-start.2 = (f32[8192]{0:T(1024)S(1)}, f32[8192]{0:T(1024)}, u32[]{:S(2)}) copy-start(f32[8192]{0:T(1024)} %param.7) | copy-start | bytes 98308
  64.7 18.9 %all-to-all-start.3 = ((bf16[8,32,128,8]{2,1,3,0:T(8,128)(2,1)}), bf16[8,32,128,8]{2,1,3,0:T(8,128)(2,1)S(1)}, u32[]{:S(2)}, u32[]{:S(2)}) async-start(bf16[8,32,128,8]{2,1,3,0:T(8,128)(2,1)} %broadcast_in_dim.164), calls=%async_computation.3 | async-start | bytes 1048576 | tf_op jit(solution)/shard_map/all_to_all | solution.py:111
  97.2 3.2 %copy-start.1 = (bf16[32,384,128]{2,1,0:T(8,128)(2,1)S(1)}, bf16[32,384,128]{2,1,0:T(8,128)(2,1)}, u32[]{:S(2)}) copy-start(bf16[32,384,128]{2,1,0:T(8,128)(2,1)} %all-gather.3.cloned.1.call-done) | copy-start | bytes 9437188
  101.2 19.7 %collective-permute-start = (f32[65792]{0:T(1024)S(1)}, f32[65792]{0:T(1024)S(1)}, u32[]{:S(2)}, u32[]{:S(2)}) collective-permute-start(f32[65792]{0:T(1024)S(1)} %pad_maximum_fusion), channel_id=1, source_target_pairs={{0,32},{32,0},{1,33},{33,1},{2,34},{34,2},{3,35},{35,3},{4,36},{36... | collective-permute-start | bytes 789512 | tf_op jit(solution)/shard_map/ppermute | solution.py:146
  122.1 10.1 %all-to-all-start.4 = ((bf16[4,256,2,32]{1,3,2,0:T(8,128)(2,1)}), bf16[4,256,2,32]{1,3,2,0:T(8,128)(2,1)S(1)}, u32[]{:S(2)}, u32[]{:S(2)}) async-start(bf16[4,256,2,32]{1,3,2,0:T(8,128)(2,1)} %broadcast_in_dim.165), calls=%async_computation.4 | async-start | bytes 262144 | tf_op jit(solution)/shard_map/all_to_all | solution.py:186
Sparse Core Ops, SparseCore 0:
  44.3 49.5 all-gather.2

commit v11 on v10

--- a/solution.py
+++ b/solution.py
@@ -129,8 +129,14 @@
     scaled = (gathered_f * gain_half.transpose(1, 0, 2)[:, :, None, :]).astype(jnp.bfloat16)
     squares = jnp.sum(gathered_f * gathered_f, axis=(0, 1, 3))
     w_q = w_query.reshape(x_count, z_count, feature_cols, w_query.shape[1])
-    query_part = jnp.einsum("zxri,xzic->rc", scaled, w_q, preferred_element_type=jnp.float32)
-    kv_part = jnp.einsum("zxri,xzic->rc", scaled, w_kv, preferred_element_type=jnp.float32)
+    both = jnp.einsum(
+        "zxri,xzic->rc",
+        scaled,
+        jnp.concatenate([w_q, w_kv], axis=3),
+        preferred_element_type=jnp.float32,
+    )
+    query_part = both[:, : w_q.shape[3]]
+    kv_part = both[:, w_q.shape[3] :]
 
     window = BUFFER - LMIN
     rest = BUFFER - window

time: 141 us -> 142 us (level)
  the two profiles are of different devices: /device:TPU:16 before, /device:TPU:56 now
where the time goes in v11:
time: 142 us
  waiting for transfers between devices  42.2 us (30%)
  blocking collectives  34 us (24%)
  starting transfers between devices  21.3 us (15%)
  local copies, waits for them, and re-layouts  16.5 us (12%)
  between operations  15.9 us (11%)
  other arithmetic  6.86 us (5%)
  matrix products  4.8 us (3%)
    all_to_all x1, blocking collectives, local(): lax.all_to_all(w_half, ('x', 'zh', 'zl'), split_axis=0, concat_axis=0, ti...  21.4 us
    ppermute x1, waiting for transfers between devices, local(): got = lax.ppermute(payload, 'seq', perm=[(0, 1), (1, 0)])  14.4 us
    all_to_all x1, blocking collectives, local(): lax.all_to_all(spread, 'x', split_axis=0, concat_axis=0, tiled=True)  12.6 us
    all_to_all x1, waiting for transfers between devices, local(): lax.all_to_all(w_spread, 'rep', split_axis=0, concat_axis=0, tiled=True)  9.88 us
    all_to_all x1, waiting for transfers between devices, local(): lax.all_to_all(outgoing, 'rep', split_axis=0, concat_axis=0, tiled=True)  7.88 us
    all_to_all x1, starting transfers between devices, local(): lax.all_to_all(outgoing, 'rep', split_axis=0, concat_axis=0, tiled=True)  6.31 us
    all_to_all x1, starting transfers between devices, local(): lax.all_to_all(w_spread, 'rep', split_axis=0, concat_axis=0, tiled=True)  6.01 us
    all_to_all x1, waiting for transfers between devices, local(): lax.all_to_all(spread, 'zl', split_axis=0, concat_axis=0, tiled=True)  5.85 us
  transfers between devices with their start and end apart: 5, of which 5 were waited for; matrix products, arithmetic and copies ran while one was open for 8% of the time, Pallas kernels for 0%

profile of v11, /device:TPU:56, one launch (start us, length us, event | category | flops | bytes accessed | tf_op | source)
XLA Modules:
  0.0 141.6 jit_solution(13843088682236137427)
XLA Ops:
  6.5 0.9 constant_dynamic-slice_fusion.5
  11.2 0.9 fusion.49
  12.1 0.8 broadcast_select_fusion
  13.0 6.3 %all-to-all-start = ((bf16[8,192,128]{2,1,0:T(8,128)(2,1)}), bf16[8,192,128]{2,1,0:T(8,128)(2,1)S(1)}, u32[]{:S(2)}, u32[]{:S(2)}) async-start(bf16[8,192,128]{2,1,0:T(8,128)(2,1)} %broadcast_select_fusion), calls=%async_computation | async-start | bytes 786432 | tf_op jit(solution)/shard_map/all_to_all | solution.py:113
  19.3 0.8 copy.90
  21.4 7.9 %all-to-all-done = bf16[8,192,128]{2,1,0:T(8,128)(2,1)S(1)} async-done(((bf16[8,192,128]{2,1,0:T(8,128)(2,1)}), bf16[8,192,128]{2,1,0:T(8,128)(2,1)S(1)}, u32[]{:S(2)}, u32[]{:S(2)}) %all-to-all-start) | async-done | bytes 393248 | tf_op jit(solution)/shard_map/all_to_all | solution.py:113
  29.2 1.4 %gather_fusion = bf16[384,128]{1,0:T(8,128)(2,1)S(1)} fusion(bf16[1536,128]{1,0:T(8,128)(2,1)S(1)} %bitcast.49, s32[1024]{0:T(1024)S(1)} %pad_clamp_fusion), kind=kCustom, calls=%fused_computation | custom fusion | bytes 198144 | tf_op jit(solution)/shard_map/jit(_take)/gather | solution.py:76
  30.9 12.6 %all_to_all.29 = bf16[4,384,128]{2,1,0:T(8,128)(2,1)} all-to-all(bf16[4,384,128]{2,1,0:T(8,128)(2,1)S(1)} %broadcast_in_dim.163), channel_id=1, replica_groups=mesh['rep'=8,'seq'=2,'x'=4,'zh'=2,'zl'=4] {'x'}, dimensions={0} | all-to-all | bytes 786432 | tf_op jit(solution)/shard_map/all_to_all | solution.py:123
  43.6 0.8 constant_dynamic-slice_fusion.3
  44.5 2.1 %copy.114 = bf16[1,128,2048]{1,2,0:T(8,128)(2,1)} copy(bf16[1,128,2048]{2,1,0:T(8,128)(2,1)} %constant_dynamic-slice_fusion.3) | data formatting | bytes 1048576
  46.5 0.9 constant_dynamic-slice_fusion.2
  47.5 21.4 %all_to_all.30 = bf16[32,128,8]{1,2,0:T(8,128)(2,1)S(1)} all-to-all(bf16[32,128,8]{1,2,0:T(8,128)(2,1)S(1)} %bitcast.61), channel_id=1, replica_groups=mesh['rep'=8,'seq'=2,'x'=4,'zh'=2,'zl'=4] {'x','zh','zl'}, dimensions={0} | all-to-all | bytes 131072 | tf_op jit(solution)/shard_map/all_to_all | solution.py:109
  68.9 0.9 broadcast_in_dim.164
  69.8 6.0 %all-to-all-start.3 = ((bf16[8,32,128,8]{2,1,3,0:T(8,128)(2,1)}), bf16[8,32,128,8]{2,1,3,0:T(8,128)(2,1)}, u32[]{:S(2)}, u32[]{:S(2)}) async-start(bf16[8,32,128,8]{2,1,3,0:T(8,128)(2,1)} %broadcast_in_dim.164), calls=%async_computation.3 | async-start | bytes 1048576 | tf_op jit(solution)/shard_map/all_to_all | solution.py:111
  75.8 2.4 %copy.97 = bf16[4,8,128,256]{2,3,1,0:T(8,128)(2,1)} copy(bf16[4,8,128,256]{3,2,1,0:T(8,128)(2,1)S(1)} %bitcast.51) | data formatting | bytes 4194304 | tf_op jit(solution)/shard_map/reshape | solution.py:131
  78.8 9.9 %all-to-all-done.3 = bf16[8,32,128,8]{2,1,3,0:T(8,128)(2,1)} async-done(((bf16[8,32,128,8]{2,1,3,0:T(8,128)(2,1)}), bf16[8,32,128,8]{2,1,3,0:T(8,128)(2,1)}, u32[]{:S(2)}, u32[]{:S(2)}) %all-to-all-start.3) | async-done | bytes 524320 | tf_op jit(solution)/shard_map/all_to_all | solution.py:111
  88.6 1.3 copy.96
  90.0 4.2 %all-gather.3.cloned.1.call-done = bf16[32,384,128]{2,1,0:T(8,128)(2,1)} async-done(((bf16[4,384,128]{2,1,0:T(8,128)(2,1)}), bf16[32,384,128]{2,1,0:T(8,128)(2,1)}) %all-gather.3.cloned.1.call-update) | async-done | bytes 3145744 | tf_op jit(solution)/shard_map/all_gather | solution.py:124
  94.1 4.1 %fusion.9 = f32[384,320]{0,1:T(8,128)S(1)} fusion(bf16[4,8,128,64]{2,3,1,0:T(8,128)(2,1)S(1)} %bitcast.58, bf16[4,8,128,256]{2,3,1,0:T(8,128)(2,1)} %copy.97, f32[8,4,128]{2,1,0:T(4,128)S(1)} %copy.91, bf16[32,384,128]{2,1,0:T(8,128)(2,1)} %all-gather.3.cloned.1.call-done), kind=kOutput, calls=%fused_computation.12 | convolution fusion | flops 1016594432 | bytes 6275072 | tf_op jit(solution)/shard_map/zxri,xzic->rc/dot_general | solution.py:132
  98.8 2.6 %fusion.1 = f32[384]{0:T(512)S(1)} fusion(bf16[8,4,384,128]{3,2,1,0:T(8,128)(2,1)} %bitcast.50), kind=kLoop, calls=%fused_computation.4 | loop fusion | flops 4718208 | bytes 3147264 | tf_op jit(solution)/shard_map/reduce_sum | solution.py:130
  101.5 4.7 %collective-permute-start = (f32[65792]{0:T(1024)S(1)}, f32[65792]{0:T(1024)S(1)}, u32[]{:S(2)}, u32[]{:S(2)}) collective-permute-start(f32[65792]{0:T(1024)S(1)} %pad_maximum_fusion), channel_id=1, source_target_pairs={{0,32},{32,0},{1,33},{33,1},{2,34},{34,2},{3,35},{35,3},{4,36},{36... | collective-permute-start | bytes 789512 | tf_op jit(solution)/shard_map/ppermute | solution.py:152
  106.7 14.4 %collective-permute-done = f32[65792]{0:T(1024)S(1)} collective-permute-done((f32[65792]{0:T(1024)S(1)}, f32[65792]{0:T(1024)S(1)}, u32[]{:S(2)}, u32[]{:S(2)}) %collective-permute-start) | collective-permute-done | bytes 263200 | tf_op jit(solution)/shard_map/ppermute | solution.py:152
  122.9 4.3 %all-to-all-start.4 = ((bf16[4,256,2,32]{1,3,2,0:T(8,128)(2,1)}), bf16[4,256,2,32]{1,3,2,0:T(8,128)(2,1)S(1)}, u32[]{:S(2)}, u32[]{:S(2)}) async-start(bf16[4,256,2,32]{1,3,2,0:T(8,128)(2,1)} %broadcast_in_dim.165), calls=%async_computation.4 | async-start | bytes 262144 | tf_op jit(solution)/shard_map/all_to_all | solution.py:192
  127.4 5.8 %all-to-all-done.4 = bf16[4,256,2,32]{1,3,2,0:T(8,128)(2,1)S(1)} async-done(((bf16[4,256,2,32]{1,3,2,0:T(8,128)(2,1)}), bf16[4,256,2,32]{1,3,2,0:T(8,128)(2,1)S(1)}, u32[]{:S(2)}, u32[]{:S(2)}) %all-to-all-start.4) | async-done | bytes 131104 | tf_op jit(solution)/shard_map/all_to_all | solution.py:192
  (73 shorter events, 8.3 us)
Async XLA Ops:
  6.5 37.1 %copy-start = (bf16[2,128,2048]{2,1,0:T(8,128)(2,1)S(1)}, bf16[2,128,2048]{2,1,0:T(8,128)(2,1)}, u32[]{:S(2)}) copy-start(bf16[2,128,2048]{2,1,0:T(8,128)(2,1)} %param.9) | copy-start | bytes 3145732
  13.0 16.3 %all-to-all-start = ((bf16[8,192,128]{2,1,0:T(8,128)(2,1)}), bf16[8,192,128]{2,1,0:T(8,128)(2,1)S(1)}, u32[]{:S(2)}, u32[]{:S(2)}) async-start(bf16[8,192,128]{2,1,0:T(8,128)(2,1)} %broadcast_select_fusion), calls=%async_computation | async-start | bytes 786432 | tf_op jit(solution)/shard_map/all_to_all | solution.py:113
  19.3 74.8 %all-gather.3.cloned.1.call-start = ((), (), s32[]{:S(2)}) async-start(), calls=%async_computation.5 | async-start | bytes 3538944 | tf_op jit(solution)/shard_map/all_gather | solution.py:124
  30.7 45.1 %copy-start.2 = (f32[8192]{0:T(1024)S(1)}, f32[8192]{0:T(1024)}, u32[]{:S(2)}) copy-start(f32[8192]{0:T(1024)} %param.7) | copy-start | bytes 98308
  30.9 44.9 %copy-start.1 = (bf16[4096,256]{1,0:T(8,128)(2,1)S(1)}, bf16[4096,256]{1,0:T(8,128)(2,1)}, u32[]{:S(2)}) copy-start(bf16[4096,256]{1,0:T(8,128)(2,1)} %param.8) | copy-start | bytes 6291460
  69.8 18.9 %all-to-all-start.3 = ((bf16[8,32,128,8]{2,1,3,0:T(8,128)(2,1)}), bf16[8,32,128,8]{2,1,3,0:T(8,128)(2,1)}, u32[]{:S(2)}, u32[]{:S(2)}) async-start(bf16[8,32,128,8]{2,1,3,0:T(8,128)(2,1)} %broadcast_in_dim.164), calls=%async_computation.3 | async-start | bytes 1048576 | tf_op jit(solution)/shard_map/all_to_all | solution.py:111
  101.5 19.6 %collective-permute-start = (f32[65792]{0:T(1024)S(1)}, f32[65792]{0:T(1024)S(1)}, u32[]{:S(2)}, u32[]{:S(2)}) collective-permute-start(f32[65792]{0:T(1024)S(1)} %pad_maximum_fusion), channel_id=1, source_target_pairs={{0,32},{32,0},{1,33},{33,1},{2,34},{34,2},{3,35},{35,3},{4,36},{36... | collective-permute-start | bytes 789512 | tf_op jit(solution)/shard_map/ppermute | solution.py:152
  122.9 10.4 %all-to-all-start.4 = ((bf16[4,256,2,32]{1,3,2,0:T(8,128)(2,1)}), bf16[4,256,2,32]{1,3,2,0:T(8,128)(2,1)S(1)}, u32[]{:S(2)}, u32[]{:S(2)}) async-start(bf16[4,256,2,32]{1,3,2,0:T(8,128)(2,1)} %broadcast_in_dim.165), calls=%async_computation.4 | async-start | bytes 262144 | tf_op jit(solution)/shard_map/all_to_all | solution.py:192
Sparse Core Ops, SparseCore 0:
  43.7 50.3 all-gather.2

commit v12 on v10

--- a/solution.py
+++ b/solution.py
@@ -139,22 +139,26 @@
     payload = jnp.concatenate(
         [
             lax.dynamic_slice_in_dim(query_part, partner * local_rows, local_rows, 0).reshape(-1),
-            lax.dynamic_slice_in_dim(kv_part, partner * rest, window, 0).reshape(-1),
             lax.dynamic_slice_in_dim(squares, partner * rest, window),
         ]
     )
     got = lax.ppermute(payload, "seq", perm=[(0, 1), (1, 0)])
+
+    by_window = jnp.stack([kv_part[:window], kv_part[rest:]])
+    kv_send = jnp.broadcast_to(
+        by_window[:, None], (seq_count, group_size, window, kv_cols)
+    ).reshape(seq_count * group_size, window, kv_cols)
+    kv_got = lax.all_to_all(kv_send, ("seq", "zl"), split_axis=0, concat_axis=0, tiled=True)
+    kv_got = kv_got.reshape(seq_count, group_size, window, kv_cols)
     q_size = local_rows * query_cols
-    kv_size = window * kv_cols
     win_at = seq_index * rest
     query_at = seq_index * local_rows
     query_raw = lax.dynamic_slice_in_dim(query_part, query_at, local_rows, 0) + got[
         :q_size
     ].reshape(local_rows, query_cols)
-    kv_raw = lax.dynamic_slice_in_dim(kv_part, win_at, window, 0) + got[
-        q_size : q_size + kv_size
-    ].reshape(window, kv_cols)
-    win_squares = lax.dynamic_slice_in_dim(squares, win_at, window) + got[q_size + kv_size :]
+    own_first = seq_index == 0
+    kv_raw = jnp.where(own_first, kv_got[0] + kv_got[1], kv_got[1] + kv_got[0])
+    win_squares = lax.dynamic_slice_in_dim(squares, win_at, window) + got[q_size:]
     win_rms = lax.rsqrt(win_squares / D + NORM_EPS)
     query_rms = lax.dynamic_slice_in_dim(win_rms, query_at - win_at, local_rows)
 
@@ -169,24 +173,10 @@
     key_pos = win_at + jnp.arange(window, dtype=jnp.int32)
     key_seg = lax.dynamic_slice_in_dim(segment, win_at, window)
     key_within = lax.dynamic_slice_in_dim(within, win_at, window)
-    kv_scaled = (win_rms[:, None] * kv_raw).reshape(window, 2, quarter)
-    freq_index = (sub % 2 * quarter + jnp.arange(quarter, dtype=jnp.int32)).astype(jnp.float32)
-    inverse = jnp.power(ROPE_BASE, -2.0 * freq_index / HD)
-    angles = key_within.astype(jnp.float32)[:, None] * inverse[None, :]
-    cosine = jnp.cos(angles)
-    sine_part = jnp.sin(angles)
-    lower_half = kv_scaled[:, 0]
-    upper_half = kv_scaled[:, 1]
-    roped = jnp.stack(
-        [lower_half * cosine - upper_half * sine_part, upper_half * cosine + lower_half * sine_part],
-        axis=1,
-    )
-    piece = jnp.where(sub < 2, roped, kv_scaled).astype(jnp.bfloat16)
-    spread = jnp.broadcast_to(piece[None], (group_size,) + piece.shape)
-    pieces = lax.all_to_all(spread, "zl", split_axis=0, concat_axis=0, tiled=True)
-    pieces = pieces.reshape(2, 2, window, 2, quarter).transpose(0, 2, 3, 1, 4)
-    key_part = pieces[0].reshape(window, HD)
-    value_part = pieces[1].reshape(window, HD)
+    kv_scaled = win_rms[None, :, None] * kv_raw
+    kv_scaled = kv_scaled.reshape(2, 2, window, 2, quarter).transpose(0, 2, 3, 1, 4)
+    key_part = rotary(kv_scaled[0].reshape(window, 1, HD), key_within)[:, 0].astype(jnp.bfloat16)
+    value_part = kv_scaled[1].reshape(window, HD).astype(jnp.bfloat16)
 
     score_scale = 1.0 / math.sqrt(HD)
     allowed = (key_seg[None, :] == query_seg[:, None]) & query_valid[:, None] & (

time: 141 us -> 143 us (1.014)
  the two profiles are of different devices: /device:TPU:16 before, /device:TPU:56 now
where the time goes in v12:
time: 143 us; the launch traced here: 142 us
  waiting for transfers between devices  47 us (33%)
  blocking collectives  33.6 us (23%)
  starting transfers between devices  23 us (16%)
  between operations  15.7 us (11%)
  local copies, waits for them, and re-layouts  10 us (7%)
  other arithmetic  7.94 us (6%)
  matrix products  4.71 us (3%)
    all_to_all x1, blocking collectives, local(): lax.all_to_all(w_half, ('x', 'zh', 'zl'), split_axis=0, concat_axis=0, ti...  21.1 us
    ppermute x1, waiting for transfers between devices, local(): got = lax.ppermute(payload, 'seq', perm=[(0, 1), (1, 0)])  19.1 us
    all_to_all x1, blocking collectives, local(): lax.all_to_all(spread, 'x', split_axis=0, concat_axis=0, tiled=True)  12.5 us
    all_to_all x1, waiting for transfers between devices, local(): lax.all_to_all(w_spread, 'rep', split_axis=0, concat_axis=0, tiled=True)  12 us
    all_to_all x1, starting transfers between devices, local(): lax.all_to_all(kv_send, ('seq', 'zl'), split_axis=0, concat_axis=0, tiled...  9.24 us
    all_gather x1, waiting for transfers between devices, local(): gathered = lax.all_gather(gathered, ('zh', 'zl'), axis=0, tiled=False)  7.96 us
    all_to_all x1, waiting for transfers between devices, local(): lax.all_to_all(outgoing, 'rep', split_axis=0, concat_axis=0, tiled=True)  7.88 us
    all_to_all x1, starting transfers between devices, local(): lax.all_to_all(outgoing, 'rep', split_axis=0, concat_axis=0, tiled=True)  6.31 us
  transfers between devices with their start and end apart: 5, of which 4 were waited for; matrix products, arithmetic and copies ran while one was open for 8% of the time, Pallas kernels for 0%

profile of v12, /device:TPU:56, one launch (start us, length us, event | category | flops | bytes accessed | tf_op | source)
XLA Modules:
  0.0 142.0 jit_solution(16252983941441886783)
XLA Ops:
  6.5 0.9 constant_dynamic-slice_fusion.2
  11.1 0.9 fusion.50
  12.0 0.8 broadcast_select_fusion
  12.8 6.3 %all-to-all-start = ((bf16[8,192,128]{2,1,0:T(8,128)(2,1)}), bf16[8,192,128]{2,1,0:T(8,128)(2,1)S(1)}, u32[]{:S(2)}, u32[]{:S(2)}) async-start(bf16[8,192,128]{2,1,0:T(8,128)(2,1)} %broadcast_select_fusion), calls=%async_computation | async-start | bytes 786432 | tf_op jit(solution)/shard_map/all_to_all | solution.py:113
  19.1 0.8 copy.95
  19.9 0.8 copy.94
  21.2 7.9 %all-to-all-done = bf16[8,192,128]{2,1,0:T(8,128)(2,1)S(1)} async-done(((bf16[8,192,128]{2,1,0:T(8,128)(2,1)}), bf16[8,192,128]{2,1,0:T(8,128)(2,1)S(1)}, u32[]{:S(2)}, u32[]{:S(2)}) %all-to-all-start) | async-done | bytes 393248 | tf_op jit(solution)/shard_map/all_to_all | solution.py:113
  29.1 1.4 %gather_fusion = bf16[384,128]{1,0:T(8,128)(2,1)S(1)} fusion(bf16[1536,128]{1,0:T(8,128)(2,1)S(1)} %bitcast.75, s32[1024]{0:T(1024)S(1)} %pad_clamp_fusion), kind=kCustom, calls=%fused_computation | custom fusion | bytes 198144 | tf_op jit(solution)/shard_map/jit(_take)/gather | solution.py:76
  30.8 12.5 %all_to_all.29 = bf16[4,384,128]{2,1,0:T(8,128)(2,1)} all-to-all(bf16[4,384,128]{2,1,0:T(8,128)(2,1)S(1)} %broadcast_in_dim.165), channel_id=1, replica_groups=mesh['rep'=8,'seq'=2,'x'=4,'zh'=2,'zl'=4] {'x'}, dimensions={0} | all-to-all | bytes 786432 | tf_op jit(solution)/shard_map/all_to_all | solution.py:123
  43.3 1.1 constant_dynamic-slice_fusion
  44.8 21.1 %all_to_all.30 = bf16[32,128,8]{1,2,0:T(8,128)(2,1)S(1)} all-to-all(bf16[32,128,8]{1,2,0:T(8,128)(2,1)S(1)} %bitcast.84), channel_id=1, replica_groups=mesh['rep'=8,'seq'=2,'x'=4,'zh'=2,'zl'=4] {'x','zh','zl'}, dimensions={0} | all-to-all | bytes 131072 | tf_op jit(solution)/shard_map/all_to_all | solution.py:109
  65.9 0.9 broadcast_in_dim.166
  66.8 5.6 %all-to-all-start.3 = ((bf16[8,32,128,8]{2,1,3,0:T(8,128)(2,1)}), bf16[8,32,128,8]{2,1,3,0:T(8,128)(2,1)S(1)}, u32[]{:S(2)}, u32[]{:S(2)}) async-start(bf16[8,32,128,8]{2,1,3,0:T(8,128)(2,1)} %broadcast_in_dim.166), calls=%async_computation.3 | async-start | bytes 1048576 | tf_op jit(solution)/shard_map/all_to_all | solution.py:111
  73.2 12.0 %all-to-all-done.3 = bf16[8,32,128,8]{2,1,3,0:T(8,128)(2,1)S(1)} async-done(((bf16[8,32,128,8]{2,1,3,0:T(8,128)(2,1)}), bf16[8,32,128,8]{2,1,3,0:T(8,128)(2,1)S(1)}, u32[]{:S(2)}, u32[]{:S(2)}) %all-to-all-start.3) | async-done | bytes 524320 | tf_op jit(solution)/shard_map/all_to_all | solution.py:111
  85.4 8.0 %all-gather.3.cloned.1.call-done = bf16[32,384,128]{2,1,0:T(8,128)(2,1)} async-done(((bf16[4,384,128]{2,1,0:T(8,128)(2,1)}), bf16[32,384,128]{2,1,0:T(8,128)(2,1)}) %all-gather.3.cloned.1.call-update) | async-done | bytes 3145744 | tf_op jit(solution)/shard_map/all_gather | solution.py:124
  93.4 3.0 %fusion.15 = f32[384,64]{0,1:T(8,128)S(1)} fusion(bf16[4,8,128,64]{2,3,1,0:T(8,128)(2,1)S(1)} %bitcast.81, f32[8,4,128]{2,1,0:T(4,128)S(1)} %copy.96, bf16[32,384,128]{2,1,0:T(8,128)(2,1)} %all-gather.3.cloned.1.call-done), kind=kOutput, calls=%fused_computation.18 | convolution fusion | flops 206045184 | bytes 3784704 | tf_op jit(solution)/shard_map/zxri,xzic->rc/dot_general | solution.py:133
  96.4 0.8 broadcast_in_dim.167
  97.2 9.2 %all-to-all-start.4 = ((f32[8,256,64]{1,2,0:T(8,128)}), f32[8,256,64]{1,2,0:T(8,128)S(1)}, u32[]{:S(2)}, u32[]{:S(2)}) async-start(f32[8,256,64]{1,2,0:T(8,128)} %bitcast.24), calls=%async_computation.4 | async-start | bytes 1048576 | tf_op jit(solution)/shard_map/all_to_all | solution.py:151
  106.5 2.7 %fusion.1 = f32[384]{0:T(512)S(1)} fusion(bf16[8,4,384,128]{3,2,1,0:T(8,128)(2,1)} %bitcast.76), kind=kLoop, calls=%fused_computation.4 | loop fusion | flops 4718208 | bytes 3147264 | tf_op jit(solution)/shard_map/reduce_sum | solution.py:130
  109.3 1.0 fusion.9
  110.6 1.9 %collective-permute-start = (f32[49408]{0:T(1024)S(1)}, f32[49408]{0:T(1024)S(1)}, u32[]{:S(2)}, u32[]{:S(2)}) collective-permute-start(f32[49408]{0:T(1024)S(1)} %pad_maximum_fusion), channel_id=1, source_target_pairs={{0,32},{32,0},{1,33},{33,1},{2,34},{34,2},{3,35},{35,3},{4,36},{36... | collective-permute-start | bytes 592904 | tf_op jit(solution)/shard_map/ppermute | solution.py:145
  112.7 19.1 %collective-permute-done = f32[49408]{0:T(1024)S(1)} collective-permute-done((f32[49408]{0:T(1024)S(1)}, f32[49408]{0:T(1024)S(1)}, u32[]{:S(2)}, u32[]{:S(2)}) %collective-permute-start) | collective-permute-done | bytes 197664 | tf_op jit(solution)/shard_map/ppermute | solution.py:145
  132.1 1.0 bitcast_multiply_fusion
  134.4 0.7 bitcast_select_fusion
  (65 shorter events, 5.8 us)
Async XLA Ops:
  6.5 102.7 %copy-start = (bf16[4096,256]{1,0:T(8,128)(2,1)S(1)}, bf16[4096,256]{1,0:T(8,128)(2,1)}, u32[]{:S(2)}) copy-start(bf16[4096,256]{1,0:T(8,128)(2,1)} %param.8) | copy-start | bytes 6291460
  12.8 16.3 %all-to-all-start = ((bf16[8,192,128]{2,1,0:T(8,128)(2,1)}), bf16[8,192,128]{2,1,0:T(8,128)(2,1)S(1)}, u32[]{:S(2)}, u32[]{:S(2)}) async-start(bf16[8,192,128]{2,1,0:T(8,128)(2,1)} %broadcast_select_fusion), calls=%async_computation | async-start | bytes 786432 | tf_op jit(solution)/shard_map/all_to_all | solution.py:113
  19.1 74.3 %all-gather.3.cloned.1.call-start = ((), (), s32[]{:S(2)}) async-start(), calls=%async_computation.5 | async-start | bytes 3538944 | tf_op jit(solution)/shard_map/all_gather | solution.py:124
  30.5 41.9 %copy-start.3 = (f32[8192]{0:T(1024)S(1)}, f32[8192]{0:T(1024)}, u32[]{:S(2)}) copy-start(f32[8192]{0:T(1024)} %param.7) | copy-start | bytes 98308
  66.8 18.3 %all-to-all-start.3 = ((bf16[8,32,128,8]{2,1,3,0:T(8,128)(2,1)}), bf16[8,32,128,8]{2,1,3,0:T(8,128)(2,1)S(1)}, u32[]{:S(2)}, u32[]{:S(2)}) async-start(bf16[8,32,128,8]{2,1,3,0:T(8,128)(2,1)} %broadcast_in_dim.166), calls=%async_computation.3 | async-start | bytes 1048576 | tf_op jit(solution)/shard_map/all_to_all | solution.py:111
  97.2 36.0 %all-to-all-start.4 = ((f32[8,256,64]{1,2,0:T(8,128)}), f32[8,256,64]{1,2,0:T(8,128)S(1)}, u32[]{:S(2)}, u32[]{:S(2)}) async-start(f32[8,256,64]{1,2,0:T(8,128)} %bitcast.24), calls=%async_computation.4 | async-start | bytes 1048576 | tf_op jit(solution)/shard_map/all_to_all | solution.py:151
  106.5 2.8 %copy-start.1 = (bf16[32,384,128]{2,1,0:T(8,128)(2,1)S(1)}, bf16[32,384,128]{2,1,0:T(8,128)(2,1)}, u32[]{:S(2)}) copy-start(bf16[32,384,128]{2,1,0:T(8,128)(2,1)} %all-gather.3.cloned.1.call-done) | copy-start | bytes 9437188
  110.3 21.5 %copy-start.2 = (f32[384,256]{1,0:T(8,128)}, f32[384,256]{1,0:T(8,128)S(1)}, u32[]{:S(2)}) copy-start(f32[384,256]{1,0:T(8,128)S(1)} %fusion.9) | copy-start | bytes 1179652
  110.6 21.2 %collective-permute-start = (f32[49408]{0:T(1024)S(1)}, f32[49408]{0:T(1024)S(1)}, u32[]{:S(2)}, u32[]{:S(2)}) collective-permute-start(f32[49408]{0:T(1024)S(1)} %pad_maximum_fusion), channel_id=1, source_target_pairs={{0,32},{32,0},{1,33},{33,1},{2,34},{34,2},{3,35},{35,3},{4,36},{36... | collective-permute-start | bytes 592904 | tf_op jit(solution)/shard_map/ppermute | solution.py:145
Sparse Core Ops, SparseCore 0:
  43.4 49.9 all-gather.2

commit v13 on v10

--- a/solution.py
+++ b/solution.py
@@ -129,31 +129,31 @@
     scaled = (gathered_f * gain_half.transpose(1, 0, 2)[:, :, None, :]).astype(jnp.bfloat16)
     squares = jnp.sum(gathered_f * gathered_f, axis=(0, 1, 3))
     w_q = w_query.reshape(x_count, z_count, feature_cols, w_query.shape[1])
-    query_part = jnp.einsum("zxri,xzic->rc", scaled, w_q, preferred_element_type=jnp.float32)
-    kv_part = jnp.einsum("zxri,xzic->rc", scaled, w_kv, preferred_element_type=jnp.float32)
+
+    def project(first, count, weights):
+        rows = lax.dynamic_slice_in_dim(scaled, first, count, 2)
+        return jnp.einsum("zxri,xzic->rc", rows, weights, preferred_element_type=jnp.float32)
 
     window = BUFFER - LMIN
     rest = BUFFER - window
     partner = seq_count - 1 - seq_index
-    query_cols = query_part.shape[1]
     payload = jnp.concatenate(
         [
-            lax.dynamic_slice_in_dim(query_part, partner * local_rows, local_rows, 0).reshape(-1),
-            lax.dynamic_slice_in_dim(kv_part, partner * rest, window, 0).reshape(-1),
+            project(partner * local_rows, local_rows, w_q).reshape(-1),
+            project(partner * rest, window, w_kv).reshape(-1),
             lax.dynamic_slice_in_dim(squares, partner * rest, window),
         ]
     )
     got = lax.ppermute(payload, "seq", perm=[(0, 1), (1, 0)])
+    query_cols = w_q.shape[3]
     q_size = local_rows * query_cols
     kv_size = window * kv_cols
     win_at = seq_index * rest
     query_at = seq_index * local_rows
-    query_raw = lax.dynamic_slice_in_dim(query_part, query_at, local_rows, 0) + got[
-        :q_size
-    ].reshape(local_rows, query_cols)
-    kv_raw = lax.dynamic_slice_in_dim(kv_part, win_at, window, 0) + got[
-        q_size : q_size + kv_size
-    ].reshape(window, kv_cols)
+    query_raw = project(query_at, local_rows, w_q) + got[:q_size].reshape(local_rows, query_cols)
+    kv_raw = project(win_at, window, w_kv) + got[q_size : q_size + kv_size].reshape(
+        window, kv_cols
+    )
     win_squares = lax.dynamic_slice_in_dim(squares, win_at, window) + got[q_size + kv_size :]
     win_rms = lax.rsqrt(win_squares / D + NORM_EPS)
     query_rms = lax.dynamic_slice_in_dim(win_rms, query_at - win_at, local_rows)

time: 141 us -> 144 us (1.021)
  blocking collectives: 29.2 us -> 11.1 us
  starting transfers between devices: 25.5 us -> 33.7 us
  waiting for transfers between devices: 48.4 us -> 55.2 us
  other arithmetic: 4.83 us -> 8.55 us
  local copies, waits for them, and re-layouts: 10.2 us -> 13.9 us
  matrix products: 6.72 us -> 4.89 us
    all_to_all x1 -> x0, blocking collectives: 18.1 us -> none  [local(): lax.all_to_all(w_half, ('x', 'zh', 'zl'), split_axis=0, concat_axis=0, ti...]
    all_to_all x0 -> x1, waiting for transfers between devices: none -> 9.99 us  [local(): lax.all_to_all(w_half, ('x', 'zh', 'zl'), split_axis=0, concat_axis=0, ti...]
    all_to_all x0 -> x1, starting transfers between devices: none -> 8.29 us  [local(): lax.all_to_all(w_half, ('x', 'zh', 'zl'), split_axis=0, concat_axis=0, ti...]
    unnamed x11 -> x16, local copies, waits for them, and re-layouts: 1.92 us -> 4.26 us
    reduce_sum x1, other arithmetic: 0.7 us -> 2.73 us  [local(): squares = jnp.sum(gathered_f * gathered_f, axis=(0, 1, 3))]
    dot_general x2 -> x4, matrix products: 6 us -> 4.17 us  [project(): jnp.einsum('zxri,xzic->rc', rows, weights, preferred_element_type=jnp.flo...]
  transfers between devices with their start and end apart: 5 -> 6, of which waited for: 5 -> 6; matrix products, arithmetic and copies ran while one was open for 4% -> 6% of each run, Pallas kernels for 0% -> 0%
where the time goes in v13:
time: 144 us; the launch traced here: 143 us
  waiting for transfers between devices  55.2 us (38%)
  starting transfers between devices  33.7 us (23%)
  between operations  15.7 us (11%)
  local copies, waits for them, and re-layouts  13.9 us (10%)
  blocking collectives  11.1 us (8%)
  other arithmetic  8.55 us (6%)
  matrix products  4.89 us (3%)
    ppermute x1, waiting for transfers between devices, local(): got = lax.ppermute(payload, 'seq', perm=[(0, 1), (1, 0)])  12.8 us
    all_to_all x1, waiting for transfers between devices, local(): lax.all_to_all(w_spread, 'rep', split_axis=0, concat_axis=0, tiled=True)  11.2 us
    all_to_all x1, blocking collectives, local(): lax.all_to_all(spread, 'x', split_axis=0, concat_axis=0, tiled=True)  11.1 us
    all_to_all x1, waiting for transfers between devices, local(): lax.all_to_all(w_half, ('x', 'zh', 'zl'), split_axis=0, concat_axis=0, ti...  9.99 us
    all_gather x1, waiting for transfers between devices, local(): gathered = lax.all_gather(gathered, ('zh', 'zl'), axis=0, tiled=False)  9.26 us
    all_to_all x1, starting transfers between devices, local(): lax.all_to_all(outgoing, 'rep', split_axis=0, concat_axis=0, tiled=True)  9.08 us
    all_to_all x1, starting transfers between devices, local(): lax.all_to_all(w_half, ('x', 'zh', 'zl'), split_axis=0, concat_axis=0, ti...  8.29 us
    all_to_all x1, waiting for transfers between devices, local(): lax.all_to_all(outgoing, 'rep', split_axis=0, concat_axis=0, tiled=True)  7.2 us
  transfers between devices with their start and end apart: 6, of which 6 were waited for; matrix products, arithmetic and copies ran while one was open for 6% of the time, Pallas kernels for 0%

profile of v13, /device:TPU:16, one launch (start us, length us, event | category | flops | bytes accessed | tf_op | source)
XLA Modules:
  0.0 143.0 jit_solution(8056082137340380836)
XLA Ops:
  6.5 0.9 constant_dynamic-slice_fusion.3
  11.1 0.9 fusion.61
  12.0 0.8 broadcast_select_fusion
  12.8 9.1 %all-to-all-start = ((bf16[8,192,128]{2,1,0:T(8,128)(2,1)}), bf16[8,192,128]{2,1,0:T(8,128)(2,1)S(1)}, u32[]{:S(2)}, u32[]{:S(2)}) async-start(bf16[8,192,128]{2,1,0:T(8,128)(2,1)} %broadcast_select_fusion), calls=%async_computation | async-start | bytes 786432 | tf_op jit(solution)/shard_map/all_to_all | solution.py:113
  24.0 7.2 %all-to-all-done = bf16[8,192,128]{2,1,0:T(8,128)(2,1)S(1)} async-done(((bf16[8,192,128]{2,1,0:T(8,128)(2,1)}), bf16[8,192,128]{2,1,0:T(8,128)(2,1)S(1)}, u32[]{:S(2)}, u32[]{:S(2)}) %all-to-all-start) | async-done | bytes 393248 | tf_op jit(solution)/shard_map/all_to_all | solution.py:113
  31.2 1.4 %gather_fusion = bf16[384,128]{1,0:T(8,128)(2,1)S(1)} fusion(bf16[1536,128]{1,0:T(8,128)(2,1)S(1)} %bitcast.71, s32[1024]{0:T(1024)S(1)} %pad_clamp_fusion), kind=kCustom, calls=%fused_computation | custom fusion | bytes 198144 | tf_op jit(solution)/shard_map/jit(_take)/gather | solution.py:76
  32.9 11.1 %all_to_all.29 = bf16[4,384,128]{2,1,0:T(8,128)(2,1)} all-to-all(bf16[4,384,128]{2,1,0:T(8,128)(2,1)S(1)} %broadcast_in_dim.163), channel_id=1, replica_groups=mesh['rep'=8,'seq'=2,'x'=4,'zh'=2,'zl'=4] {'x'}, dimensions={0} | all-to-all | bytes 786432 | tf_op jit(solution)/shard_map/all_to_all | solution.py:123
  44.0 1.1 constant_dynamic-slice_fusion.1
  46.1 8.3 %all-to-all-start.2 = ((bf16[32,128,8]{1,2,0:T(8,128)(2,1)}), bf16[32,128,8]{1,2,0:T(8,128)(2,1)S(1)}, u32[]{:S(2)}, u32[]{:S(2)}) async-start(bf16[32,128,8]{1,2,0:T(8,128)(2,1)} %bitcast.14), calls=%async_computation.2 | async-start | bytes 131072 | tf_op jit(solution)/shard_map/all_to_all | solution.py:109
  54.4 10.0 %all-to-all-done.2 = bf16[32,128,8]{1,2,0:T(8,128)(2,1)S(1)} async-done(((bf16[32,128,8]{1,2,0:T(8,128)(2,1)}), bf16[32,128,8]{1,2,0:T(8,128)(2,1)S(1)}, u32[]{:S(2)}, u32[]{:S(2)}) %all-to-all-start.2) | async-done | bytes 65568 | tf_op jit(solution)/shard_map/all_to_all | solution.py:109
  64.5 0.9 broadcast_in_dim.164
  65.3 6.8 %all-to-all-start.3 = ((bf16[8,32,128,8]{2,1,3,0:T(8,128)(2,1)}), bf16[8,32,128,8]{2,1,3,0:T(8,128)(2,1)S(1)}, u32[]{:S(2)}, u32[]{:S(2)}) async-start(bf16[8,32,128,8]{2,1,3,0:T(8,128)(2,1)} %broadcast_in_dim.164), calls=%async_computation.3 | async-start | bytes 1048576 | tf_op jit(solution)/shard_map/all_to_all | solution.py:111
  73.1 11.2 %all-to-all-done.3 = bf16[8,32,128,8]{2,1,3,0:T(8,128)(2,1)S(1)} async-done(((bf16[8,32,128,8]{2,1,3,0:T(8,128)(2,1)}), bf16[8,32,128,8]{2,1,3,0:T(8,128)(2,1)S(1)}, u32[]{:S(2)}, u32[]{:S(2)}) %all-to-all-start.3) | async-done | bytes 524320 | tf_op jit(solution)/shard_map/all_to_all | solution.py:111
  84.5 9.3 %all-gather.3.cloned.1.call-done = bf16[32,384,128]{2,1,0:T(8,128)(2,1)} async-done(((bf16[4,384,128]{2,1,0:T(8,128)(2,1)}), bf16[32,384,128]{2,1,0:T(8,128)(2,1)}) %all-gather.3.cloned.1.call-update) | async-done | bytes 3145744 | tf_op jit(solution)/shard_map/all_gather | solution.py:124
  93.8 2.7 %multiply_reduce_fusion = f32[384]{0:T(512)S(1)} fusion(bf16[8,4,384,128]{3,2,1,0:T(8,128)(2,1)} %bitcast.68), kind=kLoop, calls=%fused_computation.4 | loop fusion | flops 4718208 | bytes 3147264 | tf_op jit(solution)/shard_map/reduce_sum | solution.py:130
  96.6 1.0 fusion.1
  97.6 1.6 %copy-done.1 = bf16[8,4,384,128]{3,2,0,1:T(8,128)(2,1)} copy-done((bf16[8,4,384,128]{3,2,0,1:T(8,128)(2,1)}, bf16[8,4,384,128]{3,2,0,1:T(8,128)(2,1)S(1)}, u32[]{:S(2)}) %copy-start.1) | copy-done | bytes 3145752
  100.1 2.1 %fusion.14 = f32[24,2,8,128]{3,2,1,0:T(8,128)S(1)} fusion(bf16[4,8,128,256]{3,2,1,0:T(8,128)(2,1)S(1)} %bitcast.66, bf16[8,4,384,128]{3,2,0,1:T(8,128)(2,1)} %copy-done.1, s32[]{:T(128)S(6)} %select_n.160), kind=kOutput, calls=%fused_computation.19 | convolution fusion | flops 402653184 | bytes 3866628 | tf_op jit(solution)/shard_map/zxri,xzic->rc/dot_general | solution.py:135
  102.3 5.6 %collective-permute-start = (f32[65792]{0:T(1024)S(1)}, f32[65792]{0:T(1024)S(1)}, u32[]{:S(2)}, u32[]{:S(2)}) collective-permute-start(f32[65792]{0:T(1024)S(1)} %pad_maximum_fusion), channel_id=1, source_target_pairs={{0,32},{32,0},{1,33},{33,1},{2,34},{34,2},{3,35},{35,3},{4,36},{36... | collective-permute-start | bytes 789512 | tf_op jit(solution)/shard_map/ppermute | solution.py:147
  109.3 12.8 %collective-permute-done = f32[65792]{0:T(1024)S(1)} collective-permute-done((f32[65792]{0:T(1024)S(1)}, f32[65792]{0:T(1024)S(1)}, u32[]{:S(2)}, u32[]{:S(2)}) %collective-permute-start) | collective-permute-done | bytes 263200 | tf_op jit(solution)/shard_map/ppermute | solution.py:147
  122.9 0.8 fusion.51
  124.6 4.0 %all-to-all-start.4 = ((bf16[4,256,2,32]{1,3,2,0:T(8,128)(2,1)}), bf16[4,256,2,32]{1,3,2,0:T(8,128)(2,1)S(1)}, u32[]{:S(2)}, u32[]{:S(2)}) async-start(bf16[4,256,2,32]{1,3,2,0:T(8,128)(2,1)} %broadcast_in_dim.165), calls=%async_computation.4 | async-start | bytes 262144 | tf_op jit(solution)/shard_map/all_to_all | solution.py:186
  128.7 0.9 slice.72
  129.9 4.8 %all-to-all-done.4 = bf16[4,256,2,32]{1,3,2,0:T(8,128)(2,1)S(1)} async-done(((bf16[4,256,2,32]{1,3,2,0:T(8,128)(2,1)}), bf16[4,256,2,32]{1,3,2,0:T(8,128)(2,1)S(1)}, u32[]{:S(2)}, u32[]{:S(2)}) %all-to-all-start.4) | async-done | bytes 131104 | tf_op jit(solution)/shard_map/all_to_all | solution.py:186
  (73 shorter events, 12.1 us)
Async XLA Ops:
  6.5 93.5 %copy-start = (bf16[4096,256]{1,0:T(8,128)(2,1)S(1)}, bf16[4096,256]{1,0:T(8,128)(2,1)}, u32[]{:S(2)}) copy-start(bf16[4096,256]{1,0:T(8,128)(2,1)} %param.8) | copy-start | bytes 6291460
  12.8 18.4 %all-to-all-start = ((bf16[8,192,128]{2,1,0:T(8,128)(2,1)}), bf16[8,192,128]{2,1,0:T(8,128)(2,1)S(1)}, u32[]{:S(2)}, u32[]{:S(2)}) async-start(bf16[8,192,128]{2,1,0:T(8,128)(2,1)} %broadcast_select_fusion), calls=%async_computation | async-start | bytes 786432 | tf_op jit(solution)/shard_map/all_to_all | solution.py:113
  21.9 71.8 %all-gather.3.cloned.1.call-start = ((), (), s32[]{:S(2)}) async-start(), calls=%async_computation.5 | async-start | bytes 3538944 | tf_op jit(solution)/shard_map/all_gather | solution.py:124
  32.6 39.8 %copy-start.5 = (f32[8192]{0:T(1024)S(1)}, f32[8192]{0:T(1024)}, u32[]{:S(2)}) copy-start(f32[8192]{0:T(1024)} %param.7) | copy-start | bytes 98308
  46.1 18.4 %all-to-all-start.2 = ((bf16[32,128,8]{1,2,0:T(8,128)(2,1)}), bf16[32,128,8]{1,2,0:T(8,128)(2,1)S(1)}, u32[]{:S(2)}, u32[]{:S(2)}) async-start(bf16[32,128,8]{1,2,0:T(8,128)(2,1)} %bitcast.14), calls=%async_computation.2 | async-start | bytes 131072 | tf_op jit(solution)/shard_map/all_to_all | solution.py:109
  65.3 18.9 %all-to-all-start.3 = ((bf16[8,32,128,8]{2,1,3,0:T(8,128)(2,1)}), bf16[8,32,128,8]{2,1,3,0:T(8,128)(2,1)S(1)}, u32[]{:S(2)}, u32[]{:S(2)}) async-start(bf16[8,32,128,8]{2,1,3,0:T(8,128)(2,1)} %broadcast_in_dim.164), calls=%async_computation.3 | async-start | bytes 1048576 | tf_op jit(solution)/shard_map/all_to_all | solution.py:111
  93.8 2.8 %copy-start.3 = (bf16[32,384,128]{2,1,0:T(8,128)(2,1)S(1)}, bf16[32,384,128]{2,1,0:T(8,128)(2,1)}, u32[]{:S(2)}) copy-start(bf16[32,384,128]{2,1,0:T(8,128)(2,1)} %all-gather.3.cloned.1.call-done) | copy-start | bytes 9437188
  97.6 1.7 %copy-start.1 = (bf16[8,4,384,128]{3,2,0,1:T(8,128)(2,1)}, bf16[8,4,384,128]{3,2,0,1:T(8,128)(2,1)S(1)}, u32[]{:S(2)}) copy-start(bf16[8,4,384,128]{3,2,0,1:T(8,128)(2,1)S(1)} %fusion.1) | copy-start | bytes 9437188
  100.0 7.9 %copy-start.2 = (bf16[8,4,384,128]{3,2,0,1:T(8,128)(2,1)S(1)}, bf16[8,4,384,128]{3,2,0,1:T(8,128)(2,1)}, u32[]{:S(2)}) copy-start(bf16[8,4,384,128]{3,2,0,1:T(8,128)(2,1)} %copy-done.1) | copy-start | bytes 9437188
  102.3 19.7 %collective-permute-start = (f32[65792]{0:T(1024)S(1)}, f32[65792]{0:T(1024)S(1)}, u32[]{:S(2)}, u32[]{:S(2)}) collective-permute-start(f32[65792]{0:T(1024)S(1)} %pad_maximum_fusion), channel_id=1, source_target_pairs={{0,32},{32,0},{1,33},{33,1},{2,34},{34,2},{3,35},{35,3},{4,36},{36... | collective-permute-start | bytes 789512 | tf_op jit(solution)/shard_map/ppermute | solution.py:147
  122.1 0.7 copy-start.4
  124.6 10.0 %all-to-all-start.4 = ((bf16[4,256,2,32]{1,3,2,0:T(8,128)(2,1)}), bf16[4,256,2,32]{1,3,2,0:T(8,128)(2,1)S(1)}, u32[]{:S(2)}, u32[]{:S(2)}) async-start(bf16[4,256,2,32]{1,3,2,0:T(8,128)(2,1)} %broadcast_in_dim.165), calls=%async_computation.4 | async-start | bytes 262144 | tf_op jit(solution)/shard_map/all_to_all | solution.py:186
Sparse Core Ops, SparseCore 0:
  44.1 49.5 all-gather.2

commit v14 on v10

--- a/solution.py
+++ b/solution.py
@@ -93,14 +93,15 @@
     kv_cols = 2 * HD // group_size
     quarter = HD // 4
 
-    my_lengths = lax.dynamic_index_in_dim(lengths, replica, 0, keepdims=False)
-    my_routes = lax.dynamic_index_in_dim(routes, replica, 0, keepdims=False)
-    first_block = hidden[:LMAX]
-    second_block = lax.dynamic_slice_in_dim(hidden, my_lengths[0], LMAX, 0)
+    block = BUFFER - LMIN
     targets = jnp.arange(rep_count, dtype=jnp.int32)
+    groups = jnp.arange(routes.shape[0], dtype=jnp.int32)
+    to_first = jnp.any(
+        (groups[:, None] == replica) & (routes[:, 0][:, None] == targets[None, :]), axis=0
+    )
     outgoing = jnp.where(
-        (targets == my_routes[0])[:, None, None], first_block[None], second_block[None]
-    ).reshape(rep_count * LMAX, feature_cols)
+        to_first[:, None, None], hidden[None, :block], hidden[None, BUFFER - block :]
+    ).reshape(rep_count * block, feature_cols)
     slice_cols = quarter // rep_count
     w_half = lax.dynamic_index_in_dim(w_keyval, seq_index, 0, keepdims=False)
     w_half = w_half.reshape(feature_cols, KVH, 2, 2, 2, rep_count, slice_cols)
@@ -116,7 +117,11 @@
     all_pos = jnp.arange(BUFFER, dtype=jnp.int32)
     segment, within, source_group, pair_first, source = locate(all_pos, replica, tables)
     valid = segment >= 0
-    gathered_idx = jnp.where(valid, source_group * LMAX + all_pos - pair_first, 0)
+    flat_route = tables[1]
+    own_route = jnp.take(flat_route, jnp.maximum(segment, 0))
+    first_route = jnp.take(flat_route, source_group * RESP)
+    block_start = jnp.where(own_route == first_route, 0, BUFFER - block)
+    gathered_idx = jnp.where(valid, source_group * block + within + source - block_start, 0)
     assembled = fill_rows(incoming, gathered_idx, valid)
 
     spread = jnp.broadcast_to(assembled[None], (x_count,) + assembled.shape)

time: 141 us -> 140 us (level)
  other arithmetic: 4.83 us -> 14.3 us
  waiting for transfers between devices: 48.4 us -> 41.2 us
  between operations: 15.9 us -> 13.8 us
    and x1, other arithmetic: 0.01 us -> 10 us  [fill_rows(): taken = jnp.take(table, indices.reshape(-1), axis=0)]
    all_to_all x1, waiting for transfers between devices: 7.2 us -> 0.01 us  [local(): lax.all_to_all(outgoing, 'rep', split_axis=0, concat_axis=0, tiled=True)]
  transfers between devices with their start and end apart: 5 -> 5, of which waited for: 5 -> 4; matrix products, arithmetic and copies ran while one was open for 4% -> 12% of each run, Pallas kernels for 0% -> 0%
where the time goes in v14:
time: 140 us
  waiting for transfers between devices  41.2 us (29%)
  blocking collectives  29.8 us (21%)
  starting transfers between devices  24.2 us (17%)
  other arithmetic  14.3 us (10%)
  between operations  13.8 us (10%)
  local copies, waits for them, and re-layouts  9.71 us (7%)
  matrix products  6.72 us (5%)
    all_to_all x1, blocking collectives, local(): lax.all_to_all(w_half, ('x', 'zh', 'zl'), split_axis=0, concat_axis=0, ti...  18.1 us
    ppermute x1, waiting for transfers between devices, local(): got = lax.ppermute(payload, 'seq', perm=[(0, 1), (1, 0)])  13.6 us
    all_to_all x1, blocking collectives, local(): lax.all_to_all(spread, 'x', split_axis=0, concat_axis=0, tiled=True)  11.7 us
    all_to_all x1, waiting for transfers between devices, local(): lax.all_to_all(w_spread, 'rep', split_axis=0, concat_axis=0, tiled=True)  11.5 us
    all_gather x1, waiting for transfers between devices, local(): gathered = lax.all_gather(gathered, ('zh', 'zl'), axis=0, tiled=False)  10.1 us
    and x1, other arithmetic, fill_rows(): taken = jnp.take(table, indices.reshape(-1), axis=0)  10 us
    all_to_all x1, starting transfers between devices, local(): lax.all_to_all(outgoing, 'rep', split_axis=0, concat_axis=0, tiled=True)  9.12 us
    all_to_all x1, waiting for transfers between devices, local(): lax.all_to_all(spread, 'zl', split_axis=0, concat_axis=0, tiled=True)  5.85 us
  transfers between devices with their start and end apart: 5, of which 4 were waited for; matrix products, arithmetic and copies ran while one was open for 12% of the time, Pallas kernels for 0%

profile of v14, /device:TPU:16, one launch (start us, length us, event | category | flops | bytes accessed | tf_op | source)
XLA Modules:
  0.0 139.7 jit_solution(7918037243025874463)
XLA Ops:
  6.5 0.8 slice_bitcast_fusion
  7.4 0.9 fusion.50
  8.4 0.9 broadcast_select_fusion
  9.3 9.1 %all-to-all-start = ((bf16[8,256,128]{2,1,0:T(8,128)(2,1)}), bf16[8,256,128]{2,1,0:T(8,128)(2,1)S(1)}, u32[]{:S(2)}, u32[]{:S(2)}) async-start(bf16[8,256,128]{2,1,0:T(8,128)(2,1)} %broadcast_select_fusion), calls=%async_computation | async-start | bytes 1048576 | tf_op jit(solution)/shard_map/all_to_all | solution.py:114
  18.4 0.8 copy.81
  19.2 0.8 copy.82
  20.3 0.7 fusion.51
  21.1 10.0 %compare_and_fusion = (pred[384]{0:T(512)(128)(4,1)S(1)}, s32[384]{0:T(512)S(1)}) fusion(pred[384]{0:T(512)(128)(4,1)S(1)} %get-tuple-element.15, s32[384]{0:T(512)S(1)} %get-tuple-element.7, s32[]{:T(128)} %bitcast.15, s32[]{:T(128)} %bitcast.14, s32[]{:T(128)} %bitcast.13, s32[]{:T(128)} %bitcast.12, s32[]{:T(128)} %bitcast.11, s32[]{:T(128)} %bitcast.10, ...), kind=kLoop, calls=%fused_computation.70 | loop fusion | flops 33408 | bytes 8512 | tf_op jit(solution)/shard_map/jit(_take)/and | solution.py:76
  31.2 1.4 %gather_fusion = bf16[384,128]{1,0:T(8,128)(2,1)S(1)} fusion(bf16[2048,128]{1,0:T(8,128)(2,1)S(1)} %bitcast.95, s32[1024]{0:T(1024)S(1)} %pad_clamp_fusion), kind=kCustom, calls=%fused_computation | custom fusion | bytes 198144 | tf_op jit(solution)/shard_map/jit(_take)/gather | solution.py:76
  32.9 11.7 %all_to_all.29 = bf16[4,384,128]{2,1,0:T(8,128)(2,1)} all-to-all(bf16[4,384,128]{2,1,0:T(8,128)(2,1)S(1)} %broadcast_in_dim.181), channel_id=1, replica_groups=mesh['rep'=8,'seq'=2,'x'=4,'zh'=2,'zl'=4] {'x'}, dimensions={0} | all-to-all | bytes 786432 | tf_op jit(solution)/shard_map/all_to_all | solution.py:128
  44.6 1.1 constant_dynamic-slice_fusion.2
  46.1 18.1 %all_to_all.30 = bf16[32,128,8]{1,2,0:T(8,128)(2,1)S(1)} all-to-all(bf16[32,128,8]{1,2,0:T(8,128)(2,1)S(1)} %bitcast.105), channel_id=1, replica_groups=mesh['rep'=8,'seq'=2,'x'=4,'zh'=2,'zl'=4] {'x','zh','zl'}, dimensions={0} | all-to-all | bytes 131072 | tf_op jit(solution)/shard_map/all_to_all | solution.py:110
  64.2 0.9 broadcast_in_dim.182
  65.0 5.5 %all-to-all-start.3 = ((bf16[8,32,128,8]{2,1,3,0:T(8,128)(2,1)}), bf16[8,32,128,8]{2,1,3,0:T(8,128)(2,1)S(1)}, u32[]{:S(2)}, u32[]{:S(2)}) async-start(bf16[8,32,128,8]{2,1,3,0:T(8,128)(2,1)} %broadcast_in_dim.182), calls=%async_computation.3 | async-start | bytes 1048576 | tf_op jit(solution)/shard_map/all_to_all | solution.py:112
  71.1 11.5 %all-to-all-done.3 = bf16[8,32,128,8]{2,1,3,0:T(8,128)(2,1)S(1)} async-done(((bf16[8,32,128,8]{2,1,3,0:T(8,128)(2,1)}), bf16[8,32,128,8]{2,1,3,0:T(8,128)(2,1)S(1)}, u32[]{:S(2)}, u32[]{:S(2)}) %all-to-all-start.3) | async-done | bytes 524320 | tf_op jit(solution)/shard_map/all_to_all | solution.py:112
  82.9 10.1 %all-gather.3.cloned.1.call-done = bf16[32,384,128]{2,1,0:T(8,128)(2,1)} async-done(((bf16[4,384,128]{2,1,0:T(8,128)(2,1)}), bf16[32,384,128]{2,1,0:T(8,128)(2,1)}) %all-gather.3.cloned.1.call-update) | async-done | bytes 3145744 | tf_op jit(solution)/shard_map/all_gather | solution.py:129
  93.1 3.0 %fusion.15 = f32[384,64]{0,1:T(8,128)S(1)} fusion(bf16[4,8,128,64]{2,3,1,0:T(8,128)(2,1)S(1)} %bitcast.102, f32[8,4,128]{2,1,0:T(4,128)S(1)} %copy.83, bf16[32,384,128]{2,1,0:T(8,128)(2,1)} %all-gather.3.cloned.1.call-done), kind=kOutput, calls=%fused_computation.18 | convolution fusion | flops 206045184 | bytes 3784704 | tf_op jit(solution)/shard_map/zxri,xzic->rc/dot_general | solution.py:138
  96.3 3.0 %fusion.9 = f32[384,256]{1,0:T(8,128)S(1)} fusion(bf16[4,8,128,256]{3,2,1,0:T(8,128)(2,1)S(1)} %bitcast.94, f32[8,4,128]{2,1,0:T(4,128)S(1)} %copy.83, bf16[32,384,128]{2,1,0:T(8,128)(2,1)} %all-gather.3.cloned.1.call-done), kind=kOutput, calls=%fused_computation.12 | convolution fusion | flops 810024960 | bytes 5652480 | tf_op jit(solution)/shard_map/zxri,xzic->rc/dot_general | solution.py:137
  99.5 0.7 fusion.1
  100.3 5.6 %collective-permute-start = (f32[65792]{0:T(1024)S(1)}, f32[65792]{0:T(1024)S(1)}, u32[]{:S(2)}, u32[]{:S(2)}) collective-permute-start(f32[65792]{0:T(1024)S(1)} %pad_maximum_fusion), channel_id=1, source_target_pairs={{0,32},{32,0},{1,33},{33,1},{2,34},{34,2},{3,35},{35,3},{4,36},{36... | collective-permute-start | bytes 789512 | tf_op jit(solution)/shard_map/ppermute | solution.py:151
  106.3 13.6 %collective-permute-done = f32[65792]{0:T(1024)S(1)} collective-permute-done((f32[65792]{0:T(1024)S(1)}, f32[65792]{0:T(1024)S(1)}, u32[]{:S(2)}, u32[]{:S(2)}) %collective-permute-start) | collective-permute-done | bytes 263200 | tf_op jit(solution)/shard_map/ppermute | solution.py:151
  121.2 4.0 %all-to-all-start.4 = ((bf16[4,256,2,32]{1,3,2,0:T(8,128)(2,1)}), bf16[4,256,2,32]{1,3,2,0:T(8,128)(2,1)S(1)}, u32[]{:S(2)}, u32[]{:S(2)}) async-start(bf16[4,256,2,32]{1,3,2,0:T(8,128)(2,1)} %broadcast_in_dim.183), calls=%async_computation.4 | async-start | bytes 262144 | tf_op jit(solution)/shard_map/all_to_all | solution.py:191
  125.5 5.8 %all-to-all-done.4 = bf16[4,256,2,32]{1,3,2,0:T(8,128)(2,1)S(1)} async-done(((bf16[4,256,2,32]{1,3,2,0:T(8,128)(2,1)}), bf16[4,256,2,32]{1,3,2,0:T(8,128)(2,1)S(1)}, u32[]{:S(2)}, u32[]{:S(2)}) %all-to-all-start.4) | async-done | bytes 131104 | tf_op jit(solution)/shard_map/all_to_all | solution.py:191
  132.1 0.7 bitcast_select_fusion
  (65 shorter events, 5.0 us)
Async XLA Ops:
  6.5 89.7 %copy-start = (bf16[4096,256]{1,0:T(8,128)(2,1)S(1)}, bf16[4096,256]{1,0:T(8,128)(2,1)}, u32[]{:S(2)}) copy-start(bf16[4096,256]{1,0:T(8,128)(2,1)} %param.10) | copy-start | bytes 6291460
  9.3 21.9 %all-to-all-start = ((bf16[8,256,128]{2,1,0:T(8,128)(2,1)}), bf16[8,256,128]{2,1,0:T(8,128)(2,1)S(1)}, u32[]{:S(2)}, u32[]{:S(2)}) async-start(bf16[8,256,128]{2,1,0:T(8,128)(2,1)} %broadcast_select_fusion), calls=%async_computation | async-start | bytes 1048576 | tf_op jit(solution)/shard_map/all_to_all | solution.py:114
  18.4 74.7 %all-gather.3.cloned.1.call-start = ((), (), s32[]{:S(2)}) async-start(), calls=%async_computation.5 | async-start | bytes 3538944 | tf_op jit(solution)/shard_map/all_gather | solution.py:129
  32.6 38.0 %copy-start.2 = (f32[8192]{0:T(1024)S(1)}, f32[8192]{0:T(1024)}, u32[]{:S(2)}) copy-start(f32[8192]{0:T(1024)} %param.9) | copy-start | bytes 98308
  65.0 17.6 %all-to-all-start.3 = ((bf16[8,32,128,8]{2,1,3,0:T(8,128)(2,1)}), bf16[8,32,128,8]{2,1,3,0:T(8,128)(2,1)S(1)}, u32[]{:S(2)}, u32[]{:S(2)}) async-start(bf16[8,32,128,8]{2,1,3,0:T(8,128)(2,1)} %broadcast_in_dim.182), calls=%async_computation.3 | async-start | bytes 1048576 | tf_op jit(solution)/shard_map/all_to_all | solution.py:112
  96.3 3.2 %copy-start.1 = (bf16[32,384,128]{2,1,0:T(8,128)(2,1)S(1)}, bf16[32,384,128]{2,1,0:T(8,128)(2,1)}, u32[]{:S(2)}) copy-start(bf16[32,384,128]{2,1,0:T(8,128)(2,1)} %all-gather.3.cloned.1.call-done) | copy-start | bytes 9437188
  100.3 19.7 %collective-permute-start = (f32[65792]{0:T(1024)S(1)}, f32[65792]{0:T(1024)S(1)}, u32[]{:S(2)}, u32[]{:S(2)}) collective-permute-start(f32[65792]{0:T(1024)S(1)} %pad_maximum_fusion), channel_id=1, source_target_pairs={{0,32},{32,0},{1,33},{33,1},{2,34},{34,2},{3,35},{35,3},{4,36},{36... | collective-permute-start | bytes 789512 | tf_op jit(solution)/shard_map/ppermute | solution.py:151
  121.2 10.1 %all-to-all-start.4 = ((bf16[4,256,2,32]{1,3,2,0:T(8,128)(2,1)}), bf16[4,256,2,32]{1,3,2,0:T(8,128)(2,1)S(1)}, u32[]{:S(2)}, u32[]{:S(2)}) async-start(bf16[4,256,2,32]{1,3,2,0:T(8,128)(2,1)} %broadcast_in_dim.183), calls=%async_computation.4 | async-start | bytes 262144 | tf_op jit(solution)/shard_map/all_to_all | solution.py:191
Sparse Core Ops, SparseCore 0:
  44.7 48.2 all-gather.2

commit v15 on v14

--- a/solution.py
+++ b/solution.py
@@ -117,11 +117,15 @@
     all_pos = jnp.arange(BUFFER, dtype=jnp.int32)
     segment, within, source_group, pair_first, source = locate(all_pos, replica, tables)
     valid = segment >= 0
-    flat_route = tables[1]
-    own_route = jnp.take(flat_route, jnp.maximum(segment, 0))
-    first_route = jnp.take(flat_route, source_group * RESP)
-    block_start = jnp.where(own_route == first_route, 0, BUFFER - block)
-    gathered_idx = jnp.where(valid, source_group * block + within + source - block_start, 0)
+    flat_len, flat_route, group_of, dest_off, pair_off, src_start = tables
+    block_start = jnp.where(routes == routes[:, :1], 0, BUFFER - block).reshape(-1)
+    inside = (
+        (flat_route[None, :] == replica)
+        & (dest_off[None, :] <= all_pos[:, None])
+        & (all_pos[:, None] < (dest_off + flat_len)[None, :])
+    )
+    shift = jnp.sum(inside.astype(jnp.int32) * (src_start - block_start)[None, :], axis=1)
+    gathered_idx = jnp.where(valid, source_group * block + within + shift, 0)
     assembled = fill_rows(incoming, gathered_idx, valid)
 
     spread = jnp.broadcast_to(assembled[None], (x_count,) + assembled.shape)

time: 140 us -> 140 us (level)
  other arithmetic: 14.3 us -> 5.03 us
  waiting for transfers between devices: 41.2 us -> 50.3 us
    and x1, other arithmetic: 10 us -> 0.01 us  [fill_rows(): taken = jnp.take(table, indices.reshape(-1), axis=0)]
    all_to_all x1, waiting for transfers between devices: 0.01 us -> 9.16 us  [local(): lax.all_to_all(outgoing, 'rep', split_axis=0, concat_axis=0, tiled=True)]
  transfers between devices with their start and end apart: 5 -> 5, of which waited for: 4 -> 5; matrix products, arithmetic and copies ran while one was open for 12% -> 5% of each run, Pallas kernels for 0% -> 0%
where the time goes in v15:
time: 140 us
  waiting for transfers between devices  50.3 us (36%)
  blocking collectives  29.3 us (21%)
  starting transfers between devices  25.4 us (18%)
  between operations  13.8 us (10%)
  local copies, waits for them, and re-layouts  9.15 us (7%)
  matrix products  6.72 us (5%)
  other arithmetic  5.03 us (4%)
    all_to_all x1, blocking collectives, local(): lax.all_to_all(w_half, ('x', 'zh', 'zl'), split_axis=0, concat_axis=0, ti...  18.1 us
    ppermute x1, waiting for transfers between devices, local(): got = lax.ppermute(payload, 'seq', perm=[(0, 1), (1, 0)])  13.6 us
    all_to_all x1, waiting for transfers between devices, local(): lax.all_to_all(w_spread, 'rep', split_axis=0, concat_axis=0, tiled=True)  11.5 us
    all_to_all x1, blocking collectives, local(): lax.all_to_all(spread, 'x', split_axis=0, concat_axis=0, tiled=True)  11.2 us
    all_gather x1, waiting for transfers between devices, local(): gathered = lax.all_gather(gathered, ('zh', 'zl'), axis=0, tiled=False)  10.1 us
    all_to_all x1, waiting for transfers between devices, local(): lax.all_to_all(outgoing, 'rep', split_axis=0, concat_axis=0, tiled=True)  9.16 us
    all_to_all x1, starting transfers between devices, local(): lax.all_to_all(outgoing, 'rep', split_axis=0, concat_axis=0, tiled=True)  9.12 us
    all_to_all x1, starting transfers between devices, local(): lax.all_to_all(w_spread, 'rep', split_axis=0, concat_axis=0, tiled=True)  6.69 us
  transfers between devices with their start and end apart: 5, of which 5 were waited for; matrix products, arithmetic and copies ran while one was open for 5% of the time, Pallas kernels for 0%

profile of v15, /device:TPU:16, one launch (start us, length us, event | category | flops | bytes accessed | tf_op | source)
XLA Modules:
  0.0 139.7 jit_solution(488623048601007409)
XLA Ops:
  6.5 0.8 slice_bitcast_fusion
  7.4 0.9 fusion.53
  8.4 0.9 broadcast_select_fusion
  9.3 9.1 %all-to-all-start = ((bf16[8,256,128]{2,1,0:T(8,128)(2,1)}), bf16[8,256,128]{2,1,0:T(8,128)(2,1)S(1)}, u32[]{:S(2)}, u32[]{:S(2)}) async-start(bf16[8,256,128]{2,1,0:T(8,128)(2,1)} %broadcast_select_fusion), calls=%async_computation | async-start | bytes 1048576 | tf_op jit(solution)/shard_map/all_to_all | solution.py:114
  18.4 0.8 copy.86
  19.2 0.7 compare_select_fusion.2
  19.9 0.8 copy.87
  21.3 9.2 %all-to-all-done = bf16[8,256,128]{2,1,0:T(8,128)(2,1)S(1)} async-done(((bf16[8,256,128]{2,1,0:T(8,128)(2,1)}), bf16[8,256,128]{2,1,0:T(8,128)(2,1)S(1)}, u32[]{:S(2)}, u32[]{:S(2)}) %all-to-all-start) | async-done | bytes 524320 | tf_op jit(solution)/shard_map/all_to_all | solution.py:114
  30.5 1.4 %gather_fusion = bf16[384,128]{1,0:T(8,128)(2,1)S(1)} fusion(bf16[2048,128]{1,0:T(8,128)(2,1)S(1)} %bitcast.63, s32[1024]{0:T(1024)S(1)} %pad_clamp_fusion), kind=kCustom, calls=%fused_computation | custom fusion | bytes 198144 | tf_op jit(solution)/shard_map/jit(_take)/gather | solution.py:76
  32.2 11.2 %all_to_all.29 = bf16[4,384,128]{2,1,0:T(8,128)(2,1)} all-to-all(bf16[4,384,128]{2,1,0:T(8,128)(2,1)S(1)} %broadcast_in_dim.179), channel_id=1, replica_groups=mesh['rep'=8,'seq'=2,'x'=4,'zh'=2,'zl'=4] {'x'}, dimensions={0} | all-to-all | bytes 786432 | tf_op jit(solution)/shard_map/all_to_all | solution.py:132
  43.5 1.1 constant_dynamic-slice_fusion.2
  44.9 18.1 %all_to_all.30 = bf16[32,128,8]{1,2,0:T(8,128)(2,1)S(1)} all-to-all(bf16[32,128,8]{1,2,0:T(8,128)(2,1)S(1)} %bitcast.73), channel_id=1, replica_groups=mesh['rep'=8,'seq'=2,'x'=4,'zh'=2,'zl'=4] {'x','zh','zl'}, dimensions={0} | all-to-all | bytes 131072 | tf_op jit(solution)/shard_map/all_to_all | solution.py:110
  63.0 0.9 broadcast_in_dim.180
  63.9 6.7 %all-to-all-start.3 = ((bf16[8,32,128,8]{2,1,3,0:T(8,128)(2,1)}), bf16[8,32,128,8]{2,1,3,0:T(8,128)(2,1)S(1)}, u32[]{:S(2)}, u32[]{:S(2)}) async-start(bf16[8,32,128,8]{2,1,3,0:T(8,128)(2,1)} %broadcast_in_dim.180), calls=%async_computation.3 | async-start | bytes 1048576 | tf_op jit(solution)/shard_map/all_to_all | solution.py:112
  71.1 11.5 %all-to-all-done.3 = bf16[8,32,128,8]{2,1,3,0:T(8,128)(2,1)S(1)} async-done(((bf16[8,32,128,8]{2,1,3,0:T(8,128)(2,1)}), bf16[8,32,128,8]{2,1,3,0:T(8,128)(2,1)S(1)}, u32[]{:S(2)}, u32[]{:S(2)}) %all-to-all-start.3) | async-done | bytes 524320 | tf_op jit(solution)/shard_map/all_to_all | solution.py:112
  82.9 10.1 %all-gather.3.cloned.1.call-done = bf16[32,384,128]{2,1,0:T(8,128)(2,1)} async-done(((bf16[4,384,128]{2,1,0:T(8,128)(2,1)}), bf16[32,384,128]{2,1,0:T(8,128)(2,1)}) %all-gather.3.cloned.1.call-update) | async-done | bytes 3145744 | tf_op jit(solution)/shard_map/all_gather | solution.py:133
  93.1 3.0 %fusion.15 = f32[384,64]{0,1:T(8,128)S(1)} fusion(bf16[4,8,128,64]{2,3,1,0:T(8,128)(2,1)S(1)} %bitcast.70, f32[8,4,128]{2,1,0:T(4,128)S(1)} %copy.89, bf16[32,384,128]{2,1,0:T(8,128)(2,1)} %all-gather.3.cloned.1.call-done), kind=kOutput, calls=%fused_computation.18 | convolution fusion | flops 206045184 | bytes 3784704 | tf_op jit(solution)/shard_map/zxri,xzic->rc/dot_general | solution.py:142
  96.3 3.0 %fusion.9 = f32[384,256]{1,0:T(8,128)S(1)} fusion(bf16[4,8,128,256]{3,2,1,0:T(8,128)(2,1)S(1)} %bitcast.62, f32[8,4,128]{2,1,0:T(4,128)S(1)} %copy.89, bf16[32,384,128]{2,1,0:T(8,128)(2,1)} %all-gather.3.cloned.1.call-done), kind=kOutput, calls=%fused_computation.12 | convolution fusion | flops 810024960 | bytes 5652480 | tf_op jit(solution)/shard_map/zxri,xzic->rc/dot_general | solution.py:141
  99.5 0.7 fusion.1
  100.3 5.6 %collective-permute-start = (f32[65792]{0:T(1024)S(1)}, f32[65792]{0:T(1024)S(1)}, u32[]{:S(2)}, u32[]{:S(2)}) collective-permute-start(f32[65792]{0:T(1024)S(1)} %pad_maximum_fusion), channel_id=1, source_target_pairs={{0,32},{32,0},{1,33},{33,1},{2,34},{34,2},{3,35},{35,3},{4,36},{36... | collective-permute-start | bytes 789512 | tf_op jit(solution)/shard_map/ppermute | solution.py:155
  106.3 13.6 %collective-permute-done = f32[65792]{0:T(1024)S(1)} collective-permute-done((f32[65792]{0:T(1024)S(1)}, f32[65792]{0:T(1024)S(1)}, u32[]{:S(2)}, u32[]{:S(2)}) %collective-permute-start) | collective-permute-done | bytes 263200 | tf_op jit(solution)/shard_map/ppermute | solution.py:155
  121.2 4.0 %all-to-all-start.4 = ((bf16[4,256,2,32]{1,3,2,0:T(8,128)(2,1)}), bf16[4,256,2,32]{1,3,2,0:T(8,128)(2,1)S(1)}, u32[]{:S(2)}, u32[]{:S(2)}) async-start(bf16[4,256,2,32]{1,3,2,0:T(8,128)(2,1)} %broadcast_in_dim.181), calls=%async_computation.4 | async-start | bytes 262144 | tf_op jit(solution)/shard_map/all_to_all | solution.py:195
  125.5 5.8 %all-to-all-done.4 = bf16[4,256,2,32]{1,3,2,0:T(8,128)(2,1)S(1)} async-done(((bf16[4,256,2,32]{1,3,2,0:T(8,128)(2,1)}), bf16[4,256,2,32]{1,3,2,0:T(8,128)(2,1)S(1)}, u32[]{:S(2)}, u32[]{:S(2)}) %all-to-all-start.4) | async-done | bytes 131104 | tf_op jit(solution)/shard_map/all_to_all | solution.py:195
  132.1 0.7 bitcast_select_fusion
  (70 shorter events, 5.2 us)
Async XLA Ops:
  6.5 89.7 %copy-start = (bf16[4096,256]{1,0:T(8,128)(2,1)S(1)}, bf16[4096,256]{1,0:T(8,128)(2,1)}, u32[]{:S(2)}) copy-start(bf16[4096,256]{1,0:T(8,128)(2,1)} %param.8) | copy-start | bytes 6291460
  9.3 21.2 %all-to-all-start = ((bf16[8,256,128]{2,1,0:T(8,128)(2,1)}), bf16[8,256,128]{2,1,0:T(8,128)(2,1)S(1)}, u32[]{:S(2)}, u32[]{:S(2)}) async-start(bf16[8,256,128]{2,1,0:T(8,128)(2,1)} %broadcast_select_fusion), calls=%async_computation | async-start | bytes 1048576 | tf_op jit(solution)/shard_map/all_to_all | solution.py:114
  18.4 74.7 %all-gather.3.cloned.1.call-start = ((), (), s32[]{:S(2)}) async-start(), calls=%async_computation.5 | async-start | bytes 3538944 | tf_op jit(solution)/shard_map/all_gather | solution.py:133
  31.9 38.6 %copy-start.2 = (f32[8192]{0:T(1024)S(1)}, f32[8192]{0:T(1024)}, u32[]{:S(2)}) copy-start(f32[8192]{0:T(1024)} %param.7) | copy-start | bytes 98308
  63.9 18.8 %all-to-all-start.3 = ((bf16[8,32,128,8]{2,1,3,0:T(8,128)(2,1)}), bf16[8,32,128,8]{2,1,3,0:T(8,128)(2,1)S(1)}, u32[]{:S(2)}, u32[]{:S(2)}) async-start(bf16[8,32,128,8]{2,1,3,0:T(8,128)(2,1)} %broadcast_in_dim.180), calls=%async_computation.3 | async-start | bytes 1048576 | tf_op jit(solution)/shard_map/all_to_all | solution.py:112
  96.3 3.2 %copy-start.1 = (bf16[32,384,128]{2,1,0:T(8,128)(2,1)S(1)}, bf16[32,384,128]{2,1,0:T(8,128)(2,1)}, u32[]{:S(2)}) copy-start(bf16[32,384,128]{2,1,0:T(8,128)(2,1)} %all-gather.3.cloned.1.call-done) | copy-start | bytes 9437188
  100.3 19.7 %collective-permute-start = (f32[65792]{0:T(1024)S(1)}, f32[65792]{0:T(1024)S(1)}, u32[]{:S(2)}, u32[]{:S(2)}) collective-permute-start(f32[65792]{0:T(1024)S(1)} %pad_maximum_fusion), channel_id=1, source_target_pairs={{0,32},{32,0},{1,33},{33,1},{2,34},{34,2},{3,35},{35,3},{4,36},{36... | collective-permute-start | bytes 789512 | tf_op jit(solution)/shard_map/ppermute | solution.py:155
  121.2 10.1 %all-to-all-start.4 = ((bf16[4,256,2,32]{1,3,2,0:T(8,128)(2,1)}), bf16[4,256,2,32]{1,3,2,0:T(8,128)(2,1)S(1)}, u32[]{:S(2)}, u32[]{:S(2)}) async-start(bf16[4,256,2,32]{1,3,2,0:T(8,128)(2,1)} %broadcast_in_dim.181), calls=%async_computation.4 | async-start | bytes 262144 | tf_op jit(solution)/shard_map/all_to_all | solution.py:195
Sparse Core Ops, SparseCore 0:
  43.6 49.4 all-gather.2

commit v16 on v15

--- a/solution.py
+++ b/solution.py
@@ -147,23 +147,23 @@
     query_cols = query_part.shape[1]
     payload = jnp.concatenate(
         [
-            lax.dynamic_slice_in_dim(query_part, partner * local_rows, local_rows, 0).reshape(-1),
-            lax.dynamic_slice_in_dim(kv_part, partner * rest, window, 0).reshape(-1),
-            lax.dynamic_slice_in_dim(squares, partner * rest, window),
-        ]
+            lax.dynamic_slice_in_dim(query_part, partner * local_rows, local_rows, 0),
+            lax.dynamic_slice_in_dim(kv_part, partner * rest, window, 0).reshape(-1, query_cols),
+            lax.dynamic_slice_in_dim(squares, partner * rest, window).reshape(-1, query_cols),
+        ],
+        axis=0,
     )
     got = lax.ppermute(payload, "seq", perm=[(0, 1), (1, 0)])
-    q_size = local_rows * query_cols
-    kv_size = window * kv_cols
+    kv_rows = window * kv_cols // query_cols
     win_at = seq_index * rest
     query_at = seq_index * local_rows
-    query_raw = lax.dynamic_slice_in_dim(query_part, query_at, local_rows, 0) + got[
-        :q_size
-    ].reshape(local_rows, query_cols)
+    query_raw = lax.dynamic_slice_in_dim(query_part, query_at, local_rows, 0) + got[:local_rows]
     kv_raw = lax.dynamic_slice_in_dim(kv_part, win_at, window, 0) + got[
-        q_size : q_size + kv_size
+        local_rows : local_rows + kv_rows
     ].reshape(window, kv_cols)
-    win_squares = lax.dynamic_slice_in_dim(squares, win_at, window) + got[q_size + kv_size :]
+    win_squares = lax.dynamic_slice_in_dim(squares, win_at, window) + got[
+        local_rows + kv_rows :
+    ].reshape(-1)
     win_rms = lax.rsqrt(win_squares / D + NORM_EPS)
     query_rms = lax.dynamic_slice_in_dim(win_rms, query_at - win_at, local_rows)
 

time: 140 us -> 140 us (level)
  other arithmetic: 5.03 us -> 7.06 us
  matrix products: 6.72 us -> 4.71 us
    reduce_sum x1, other arithmetic: 0.7 us -> 2.74 us  [local(): squares = jnp.sum(gathered_f * gathered_f, axis=(0, 1, 3))]
    dot_general x1, matrix products: 3.02 us -> 1.01 us  [local(): jnp.einsum('zxri,xzic->rc', scaled, w_q, preferred_element_type=jnp.float32)]
where the time goes in v16:
time: 140 us
  waiting for transfers between devices  50.5 us (36%)
  blocking collectives  29.3 us (21%)
  starting transfers between devices  25.4 us (18%)
  between operations  13.7 us (10%)
  local copies, waits for them, and re-layouts  9.01 us (6%)
  other arithmetic  7.06 us (5%)
  matrix products  4.71 us (3%)
    all_to_all x1, blocking collectives, local(): lax.all_to_all(w_half, ('x', 'zh', 'zl'), split_axis=0, concat_axis=0, ti...  18.1 us
    ppermute x1, waiting for transfers between devices, local(): got = lax.ppermute(payload, 'seq', perm=[(0, 1), (1, 0)])  13.8 us
    all_to_all x1, waiting for transfers between devices, local(): lax.all_to_all(w_spread, 'rep', split_axis=0, concat_axis=0, tiled=True)  11.5 us
    all_to_all x1, blocking collectives, local(): lax.all_to_all(spread, 'x', split_axis=0, concat_axis=0, tiled=True)  11.2 us
    all_gather x1, waiting for transfers between devices, local(): gathered = lax.all_gather(gathered, ('zh', 'zl'), axis=0, tiled=False)  10.1 us
    all_to_all x1, waiting for transfers between devices, local(): lax.all_to_all(outgoing, 'rep', split_axis=0, concat_axis=0, tiled=True)  9.16 us
    all_to_all x1, starting transfers between devices, local(): lax.all_to_all(outgoing, 'rep', split_axis=0, concat_axis=0, tiled=True)  9.12 us
    all_to_all x1, starting transfers between devices, local(): lax.all_to_all(w_spread, 'rep', split_axis=0, concat_axis=0, tiled=True)  6.69 us
  transfers between devices with their start and end apart: 5, of which 5 were waited for; matrix products, arithmetic and copies ran while one was open for 5% of the time, Pallas kernels for 0%

profile of v16, /device:TPU:16, one launch (start us, length us, event | category | flops | bytes accessed | tf_op | source)
XLA Modules:
  0.0 139.7 jit_solution(12745078845535361979)
XLA Ops:
  6.5 0.8 slice_bitcast_fusion
  7.4 0.9 fusion.51
  8.4 0.9 broadcast_select_fusion
  9.3 9.1 %all-to-all-start = ((bf16[8,256,128]{2,1,0:T(8,128)(2,1)}), bf16[8,256,128]{2,1,0:T(8,128)(2,1)S(1)}, u32[]{:S(2)}, u32[]{:S(2)}) async-start(bf16[8,256,128]{2,1,0:T(8,128)(2,1)} %broadcast_select_fusion), calls=%async_computation | async-start | bytes 1048576 | tf_op jit(solution)/shard_map/all_to_all | solution.py:114
  18.4 0.8 copy.88
  19.2 0.7 compare_select_fusion.2
  19.9 0.8 copy.89
  21.3 9.2 %all-to-all-done = bf16[8,256,128]{2,1,0:T(8,128)(2,1)S(1)} async-done(((bf16[8,256,128]{2,1,0:T(8,128)(2,1)}), bf16[8,256,128]{2,1,0:T(8,128)(2,1)S(1)}, u32[]{:S(2)}, u32[]{:S(2)}) %all-to-all-start) | async-done | bytes 524320 | tf_op jit(solution)/shard_map/all_to_all | solution.py:114
  30.5 1.4 %gather_fusion = bf16[384,128]{1,0:T(8,128)(2,1)S(1)} fusion(bf16[2048,128]{1,0:T(8,128)(2,1)S(1)} %bitcast.62, s32[1024]{0:T(1024)S(1)} %pad_clamp_fusion), kind=kCustom, calls=%fused_computation | custom fusion | bytes 198144 | tf_op jit(solution)/shard_map/jit(_take)/gather | solution.py:76
  32.2 11.2 %all_to_all.29 = bf16[4,384,128]{2,1,0:T(8,128)(2,1)} all-to-all(bf16[4,384,128]{2,1,0:T(8,128)(2,1)S(1)} %broadcast_in_dim.179), channel_id=1, replica_groups=mesh['rep'=8,'seq'=2,'x'=4,'zh'=2,'zl'=4] {'x'}, dimensions={0} | all-to-all | bytes 786432 | tf_op jit(solution)/shard_map/all_to_all | solution.py:132
  43.5 1.1 constant_dynamic-slice_fusion.2
  44.9 18.1 %all_to_all.30 = bf16[32,128,8]{1,2,0:T(8,128)(2,1)S(1)} all-to-all(bf16[32,128,8]{1,2,0:T(8,128)(2,1)S(1)} %bitcast.71), channel_id=1, replica_groups=mesh['rep'=8,'seq'=2,'x'=4,'zh'=2,'zl'=4] {'x','zh','zl'}, dimensions={0} | all-to-all | bytes 131072 | tf_op jit(solution)/shard_map/all_to_all | solution.py:110
  63.0 0.9 broadcast_in_dim.180
  63.9 6.7 %all-to-all-start.3 = ((bf16[8,32,128,8]{2,1,3,0:T(8,128)(2,1)}), bf16[8,32,128,8]{2,1,3,0:T(8,128)(2,1)S(1)}, u32[]{:S(2)}, u32[]{:S(2)}) async-start(bf16[8,32,128,8]{2,1,3,0:T(8,128)(2,1)} %broadcast_in_dim.180), calls=%async_computation.3 | async-start | bytes 1048576 | tf_op jit(solution)/shard_map/all_to_all | solution.py:112
  71.1 11.5 %all-to-all-done.3 = bf16[8,32,128,8]{2,1,3,0:T(8,128)(2,1)S(1)} async-done(((bf16[8,32,128,8]{2,1,3,0:T(8,128)(2,1)}), bf16[8,32,128,8]{2,1,3,0:T(8,128)(2,1)S(1)}, u32[]{:S(2)}, u32[]{:S(2)}) %all-to-all-start.3) | async-done | bytes 524320 | tf_op jit(solution)/shard_map/all_to_all | solution.py:112
  82.9 10.1 %all-gather.3.cloned.1.call-done = bf16[32,384,128]{2,1,0:T(8,128)(2,1)} async-done(((bf16[4,384,128]{2,1,0:T(8,128)(2,1)}), bf16[32,384,128]{2,1,0:T(8,128)(2,1)}) %all-gather.3.cloned.1.call-update) | async-done | bytes 3145744 | tf_op jit(solution)/shard_map/all_gather | solution.py:133
  93.1 3.0 %fusion.15 = f32[384,64]{0,1:T(8,128)S(1)} fusion(bf16[4,8,128,64]{2,3,1,0:T(8,128)(2,1)S(1)} %bitcast.68, f32[8,4,128]{2,1,0:T(4,128)S(1)} %copy.91, bf16[32,384,128]{2,1,0:T(8,128)(2,1)} %all-gather.3.cloned.1.call-done), kind=kOutput, calls=%fused_computation.18 | convolution fusion | flops 206045184 | bytes 3784704 | tf_op jit(solution)/shard_map/zxri,xzic->rc/dot_general | solution.py:142
  96.3 2.7 %fusion.1 = f32[384]{0:T(512)S(1)} fusion(bf16[8,4,384,128]{3,2,1,0:T(8,128)(2,1)} %bitcast.63), kind=kLoop, calls=%fused_computation.4 | loop fusion | flops 4718208 | bytes 3147264 | tf_op jit(solution)/shard_map/reduce_sum | solution.py:139
  99.1 1.0 fusion.9
  100.2 5.6 %collective-permute-start = (f32[257,256]{1,0:T(8,128)S(1)}, f32[257,256]{1,0:T(8,128)S(1)}, u32[]{:S(2)}, u32[]{:S(2)}) collective-permute-start(f32[257,256]{1,0:T(8,128)S(1)} %pad_maximum_fusion), channel_id=1, source_target_pairs={{0,32},{32,0},{1,33},{33,1},{2,34},{34,2},{3,35},{35,3},{4,36},{36... | collective-permute-start | bytes 789512 | tf_op jit(solution)/shard_map/ppermute | solution.py:156
  106.2 13.8 %collective-permute-done = f32[257,256]{1,0:T(8,128)S(1)} collective-permute-done((f32[257,256]{1,0:T(8,128)S(1)}, f32[257,256]{1,0:T(8,128)S(1)}, u32[]{:S(2)}, u32[]{:S(2)}) %collective-permute-start) | collective-permute-done | bytes 263200 | tf_op jit(solution)/shard_map/ppermute | solution.py:156
  121.2 4.0 %all-to-all-start.4 = ((bf16[4,256,2,32]{1,3,2,0:T(8,128)(2,1)}), bf16[4,256,2,32]{1,3,2,0:T(8,128)(2,1)S(1)}, u32[]{:S(2)}, u32[]{:S(2)}) async-start(bf16[4,256,2,32]{1,3,2,0:T(8,128)(2,1)} %broadcast_in_dim.181), calls=%async_computation.4 | async-start | bytes 262144 | tf_op jit(solution)/shard_map/all_to_all | solution.py:195
  125.5 5.8 %all-to-all-done.4 = bf16[4,256,2,32]{1,3,2,0:T(8,128)(2,1)S(1)} async-done(((bf16[4,256,2,32]{1,3,2,0:T(8,128)(2,1)}), bf16[4,256,2,32]{1,3,2,0:T(8,128)(2,1)S(1)}, u32[]{:S(2)}, u32[]{:S(2)}) %all-to-all-start.4) | async-done | bytes 131104 | tf_op jit(solution)/shard_map/all_to_all | solution.py:195
  132.1 0.7 bitcast_select_fusion
  (68 shorter events, 5.1 us)
Async XLA Ops:
  6.5 92.6 %copy-start = (bf16[4096,256]{1,0:T(8,128)(2,1)S(1)}, bf16[4096,256]{1,0:T(8,128)(2,1)}, u32[]{:S(2)}) copy-start(bf16[4096,256]{1,0:T(8,128)(2,1)} %param.8) | copy-start | bytes 6291460
  9.3 21.2 %all-to-all-start = ((bf16[8,256,128]{2,1,0:T(8,128)(2,1)}), bf16[8,256,128]{2,1,0:T(8,128)(2,1)S(1)}, u32[]{:S(2)}, u32[]{:S(2)}) async-start(bf16[8,256,128]{2,1,0:T(8,128)(2,1)} %broadcast_select_fusion), calls=%async_computation | async-start | bytes 1048576 | tf_op jit(solution)/shard_map/all_to_all | solution.py:114
  18.4 74.7 %all-gather.3.cloned.1.call-start = ((), (), s32[]{:S(2)}) async-start(), calls=%async_computation.5 | async-start | bytes 3538944 | tf_op jit(solution)/shard_map/all_gather | solution.py:133
  31.9 38.6 %copy-start.2 = (f32[8192]{0:T(1024)S(1)}, f32[8192]{0:T(1024)}, u32[]{:S(2)}) copy-start(f32[8192]{0:T(1024)} %param.7) | copy-start | bytes 98308
  63.9 18.8 %all-to-all-start.3 = ((bf16[8,32,128,8]{2,1,3,0:T(8,128)(2,1)}), bf16[8,32,128,8]{2,1,3,0:T(8,128)(2,1)S(1)}, u32[]{:S(2)}, u32[]{:S(2)}) async-start(bf16[8,32,128,8]{2,1,3,0:T(8,128)(2,1)} %broadcast_in_dim.180), calls=%async_computation.3 | async-start | bytes 1048576 | tf_op jit(solution)/shard_map/all_to_all | solution.py:112
  96.3 2.8 %copy-start.1 = (bf16[32,384,128]{2,1,0:T(8,128)(2,1)S(1)}, bf16[32,384,128]{2,1,0:T(8,128)(2,1)}, u32[]{:S(2)}) copy-start(bf16[32,384,128]{2,1,0:T(8,128)(2,1)} %all-gather.3.cloned.1.call-done) | copy-start | bytes 9437188
  100.2 19.8 %collective-permute-start = (f32[257,256]{1,0:T(8,128)S(1)}, f32[257,256]{1,0:T(8,128)S(1)}, u32[]{:S(2)}, u32[]{:S(2)}) collective-permute-start(f32[257,256]{1,0:T(8,128)S(1)} %pad_maximum_fusion), channel_id=1, source_target_pairs={{0,32},{32,0},{1,33},{33,1},{2,34},{34,2},{3,35},{35,3},{4,36},{36... | collective-permute-start | bytes 789512 | tf_op jit(solution)/shard_map/ppermute | solution.py:156
  121.2 10.1 %all-to-all-start.4 = ((bf16[4,256,2,32]{1,3,2,0:T(8,128)(2,1)}), bf16[4,256,2,32]{1,3,2,0:T(8,128)(2,1)S(1)}, u32[]{:S(2)}, u32[]{:S(2)}) async-start(bf16[4,256,2,32]{1,3,2,0:T(8,128)(2,1)} %broadcast_in_dim.181), calls=%async_computation.4 | async-start | bytes 262144 | tf_op jit(solution)/shard_map/all_to_all | solution.py:195
Sparse Core Ops, SparseCore 0:
  43.6 49.4 all-gather.2
